TPU v7x, 1024 devices: a whole 4x8x16 slice. The times are simulated.
1024 devices in a mesh: ctx: 64 (over z_hi, y, core), chan: 16 (over x, z_lo).
Axes of the slice: x: 4, y: 8, z: 16 (z_hi: 4, z_lo: 4; z = z_hi * 4 + z_lo), core: 2. Of those that a mesh axis runs over, the one named last changes fastest.
Arguments:
- query: bfloat16 [16384, 8192], P('ctx', 'chan'), may hold values from -6 to 6
- key_proj: bfloat16 [16384, 8192], P('ctx', 'chan'), may hold values from -6 to 6
- value: bfloat16 [16384, 8192], P('ctx', 'chan'), may hold values from -6 to 6
- residues: float32 [16, 8192], P(None, 'chan'), may hold values from -1.5 to 1.5
- rates: float32 [16, 8192], P(None, 'chan'), as said below
- cotangent: bfloat16 [16384, 8192], P('ctx', 'chan'), may hold values from -6 to 6
Outputs:
- output: bfloat16 [16384, 8192], P('ctx', 'chan')
- grad_query: bfloat16 [16384, 8192], P('ctx', 'chan')
- grad_key: bfloat16 [16384, 8192], P('ctx', 'chan')
- grad_value: bfloat16 [16384, 8192], P('ctx', 'chan')
Inputs may be any that keep to these rules, and one draw needn't show every extreme that they name: `rates`: every rate is positive and at most 1/30.
All inputs are finite; a program needn't handle non-finite values.
Results may differ from a plain program's by a relative error of at most 0.0049.
Values sent between devices are 32-bit elements; how exact they have to be, the bound alone decides.
No kernel may reach another device: no remote copies, remote signals or barrier semaphores. Data moves between devices by JAX's collectives and lax.ppermute only.
A program may use at most 32 MiB of HBM per device.

v0:
```python
import jax
import jax.numpy as jnp
from jax import lax
from jax.sharding import PartitionSpec as P

BLOCK = 64


def entering(part, axis, combine, identity, reverse):
    count = lax.axis_size(axis)
    place = lax.axis_index(axis)
    ahead = count - 1 - place if reverse else place
    gathered = jax.tree.map(lambda a: lax.all_gather(a, axis), part)
    state = jax.tree.map(lambda a, e: jnp.zeros_like(a) + jnp.asarray(e, a.dtype), part, identity)

    def one(step, state):
        source = count - 1 - step if reverse else step
        return combine(
            state, jax.tree.map(lambda a: lax.dynamic_index_in_dim(a, source, 0, False), gathered)
        )

    return lax.fori_loop(0, ahead, one, state)


def local_pass(signal, scaled, rates):
    length, width = signal.shape
    count = length // BLOCK
    order = rates.shape[0]
    lags = jnp.arange(BLOCK).astype(jnp.float32)
    rising = jnp.exp(rates[None] * lags[:, None, None])
    falling = jnp.exp(-rates[None] * lags[:, None, None])
    lower = (lags[:, None] >= lags[None, :]).astype(jnp.float32)
    step_decay = jnp.exp(-rates)

    def advance(state, block):
        lifted = (rising * block[:, None, :]).reshape(BLOCK, order * width)
        summed = jnp.dot(lower, lifted, precision=lax.Precision.HIGHEST).reshape(
            BLOCK, order, width
        )
        states = falling * (summed + step_decay * state[None])
        return (states[-1], jnp.sum(scaled[None] * states, axis=1))

    final, pieces = lax.scan(
        advance, jnp.zeros((order, width), jnp.float32), signal.reshape(count, BLOCK, width)
    )
    return (final, pieces)


def apply_incoming(pieces, incoming, scaled, rates):
    count = pieces.shape[0]
    lags = jnp.arange(BLOCK).astype(jnp.float32)
    after = jnp.exp(-rates[None] * (lags + 1.0)[:, None, None])
    block_index = jnp.arange(count).astype(jnp.float32)
    block_start = jnp.exp(-rates[None] * (BLOCK * block_index)[:, None, None])
    weights = block_start * (scaled * incoming)[None]
    extra = jnp.einsum("ikc,bkc->bic", after, weights, precision=lax.Precision.HIGHEST)
    return (pieces + extra).reshape(count * BLOCK, pieces.shape[2])


def join_states(earlier, later):
    return (earlier[0] * later[0], earlier[1] * later[0] + later[1])


def incoming_states(local_state, rates, length, forward):
    local_decay = jnp.exp(-rates * length)
    empty = jnp.zeros_like(local_state)
    if forward:
        joined = entering(
            (local_decay, local_state),
            "ctx",
            join_states,
            (jnp.ones_like(local_decay), empty),
            False,
        )
    else:
        joined = entering(
            (local_decay, local_state),
            "ctx",
            join_states,
            (jnp.ones_like(local_decay), empty),
            True,
        )
    return joined[1]


def per_device(query, key_proj, value, residues, rates, cotangent):
    length = query.shape[0]
    query_f = query.astype(jnp.float32)
    key_f = key_proj.astype(jnp.float32)
    value_f = value.astype(jnp.float32)
    cot_f = cotangent.astype(jnp.float32)
    scaled = residues * jnp.sqrt(-jnp.expm1(-2.0 * rates))
    gated = lax.optimization_barrier((query_f * key_f).astype(jnp.bfloat16)).astype(jnp.float32)
    weighted = cot_f * value_f
    fwd_state, fwd_pieces = local_pass(gated, scaled, rates)
    bwd_state, bwd_pieces = local_pass(weighted[::-1], scaled, rates)
    fwd_in = incoming_states(fwd_state, rates, length, True)
    bwd_in = incoming_states(bwd_state, rates, length, False)
    mixed = apply_incoming(fwd_pieces, fwd_in, scaled, rates)
    back = apply_incoming(bwd_pieces, bwd_in, scaled, rates)[::-1]
    output = (value_f * mixed).astype(jnp.bfloat16)
    grad_value = (cot_f * mixed).astype(jnp.bfloat16)
    grad_query = (back * key_f).astype(jnp.bfloat16)
    grad_key = (back * query_f).astype(jnp.bfloat16)
    return (output, grad_query, grad_key, grad_value)


def solution(mesh):
    return jax.shard_map(
        per_device,
        mesh=mesh,
        in_specs=(
            P("ctx", "chan"),
            P("ctx", "chan"),
            P("ctx", "chan"),
            P(None, "chan"),
            P(None, "chan"),
            P("ctx", "chan"),
        ),
        out_specs=(P("ctx", "chan"), P("ctx", "chan"), P("ctx", "chan"), P("ctx", "chan")),
        check_vma=False,
    )
```

profile of v0, /device:TPU:6, one launch (start us, length us, event | category | flops | bytes accessed | tf_op | source)
XLA Modules:
  0.0 491.1 jit_solution(1659898457033158180)
XLA Ops:
  8.4 1.4 multiply_exponential_fusion.6
  9.9 22.7 %while.56 = (s32[]{:T(128)}, f32[16,512]{1,0:T(8,128)S(1)}, f32[4,64,512]{2,1,0:T(8,128)S(1)}, f32[4,64,512]{2,1,0:T(8,128)S(1)}, f32[16,512]{1,0:T(8,128)S(1)},...) while((s32[]{:T(128)}, f32[16,512]{1,0:T(8,128)S(1)}, ...), condition=%wide.region_2.3_spmd.clone.clone, body=%wide.region_0.2_spmd.clone.clone.sunk | while | flops 406306816 | bytes 19956588 | solution.py:43
  10.3 1.2 copy.41
  11.5 2.0 fusion.55
  13.5 1.2 copy.42
  15.9 1.2 copy.41
  17.2 2.0 fusion.55
  19.2 1.2 copy.42
  21.6 1.2 copy.41
  22.8 2.0 fusion.55
  24.8 1.2 copy.42
  27.3 1.2 copy.41
  28.5 2.0 fusion.55
  30.5 1.2 copy.42
  34.1 112.8 %all-gather.9.cloned.1.call-done = f32[1024,512]{1,0:T(8,128)} async-done(((f32[16,512]{1,0:T(8,128)}), f32[1024,512]{1,0:T(8,128)}) %all-gather.9.cloned.1.call-update) | async-done | bytes 2097168 | tf_op jit(solution)/shard_map/all_gather | solution.py:13
  147.0 102.4 %all-gather.7.cloned.1.call-done = f32[1024,512]{1,0:T(8,128)} async-done(((f32[16,512]{1,0:T(8,128)}), f32[1024,512]{1,0:T(8,128)}) %all-gather.7.cloned.1.call-update) | async-done | bytes 2097168 | tf_op jit(solution)/shard_map/all_gather | solution.py:13
  249.6 4.5 fusion.25
  256.4 22.7 %while.57 = (s32[]{:T(128)}, f32[16,512]{1,0:T(8,128)S(1)}, f32[4,64,512]{2,1,0:T(8,128)S(1)}, f32[4,64,512]{2,1,0:T(8,128)S(1)}, f32[16,512]{1,0:T(8,128)S(1)},...) while((s32[]{:T(128)}, f32[16,512]{1,0:T(8,128)S(1)}, ...), condition=%wide.region_7.8_spmd.clone.clone, body=%wide.region_5.7_spmd.clone.clone.sunk | while | flops 406306816 | bytes 19956588 | solution.py:43
  256.8 1.2 copy.43
  258.0 2.0 fusion.58
  260.0 1.2 copy.44
  262.5 1.2 copy.43
  263.7 2.0 fusion.58
  265.7 1.2 copy.44
  268.1 1.2 copy.43
  269.4 2.0 fusion.58
  271.4 1.2 copy.44
  273.8 1.2 copy.43
  275.0 2.0 fusion.58
  279.7 146.6 %all-gather.11.cloned.1.call-done = f32[1024,512]{1,0:T(8,128)} async-done(((f32[16,512]{1,0:T(8,128)}), f32[1024,512]{1,0:T(8,128)}) %all-gather.11.cloned.1.call-update) | async-done | bytes 2097168 | tf_op jit(solution)/shard_map/all_gather | solution.py:13
  426.3 51.7 %while.55 = (s32[]{:T(128)}, f32[16,512]{1,0:T(8,128)S(1)}, s32[]{:T(128)}, f32[64,16,512]{2,1,0:T(8,128)}, f32[64,16,512]{2,1,0:T(8,128)}, /*index=5*/s32[]{:T(128)}, s32[]{:T(128)}, s32[]{:T(128)}, s32[]{:T(128)}) while((s32[]{:T(128)}, f32[16,512]{1,0:T(8,128)S(1)}, s32[]{:T(128)}, f32[64,16,512]{2,1,0:T(8,128)}, ...), condition=%wide.region_9.10_spmd, body=%wide.region_8.9_spmd.sunk | while | flops 16390 | bytes 131215 | solution.py:22
  478.1 4.5 fusion.24
  (157 shorter events, 68.1 us)
Async XLA Ops:
  7.2 2.7 copy-start
  7.2 139.8 %all-gather.9.cloned.1.call-start = ((), (), s32[]{:S(2)}) async-start(), calls=%async_computation.1 | async-start | bytes 2129920 | tf_op jit(solution)/shard_map/all_gather | solution.py:13
  32.5 0.6 copy-start.1
  33.2 216.2 %all-gather.7.cloned.1.call-start = ((), (), s32[]{:S(2)}) async-start(), calls=%async_computation | async-start | bytes 2129920 | tf_op jit(solution)/shard_map/all_gather | solution.py:13
  33.9 392.3 %all-gather.11.cloned.1.call-start = ((), (), s32[]{:S(2)}) async-start(), calls=%async_computation.2 | async-start | bytes 2129920 | tf_op jit(solution)/shard_map/all_gather | solution.py:13
  254.1 1.0 copy-start.5
  254.1 1.0 copy-start.6
  279.1 0.6 copy-start.2
  482.6 1.0 copy-start.3
  482.6 1.0 copy-start.4
Sparse Core Ops, SparseCore 0:
  33.3 113.6 all-gather.8
  152.1 97.2 all-gather.6
  279.8 146.4 all-gather.10
where the time goes:
time: 496 us; the launch traced here: 491 us
  waiting for transfers between devices  363 us (73%)
  other arithmetic  63.4 us (13%)
  matrix products  25 us (5%)
  local copies, waits for them, and re-layouts  23.5 us (5%)
  between operations  14 us (3%)
    all_gather x3, waiting for transfers between devices, entering(): gathered = jax.tree.map(lambda a: lax.all_gather(a, axis), part)  362 us
    add x63, other arithmetic, join_states(): return (earlier[0] * later[0], earlier[1] * later[0] + later[1])  49.8 us
    while x16, local copies, waits for them, and re-layouts  19.4 us
    dot_general x8, matrix products, advance(): jnp.dot(lower, lifted, precision=lax.Precision.HIGHEST)  16 us
  transfers between devices with their start and end apart: 3, of which 3 were waited for; matrix products, arithmetic and copies ran while one was open for 0% of the time, Pallas kernels for 0%

commit v1 on v0

--- a/solution.py
+++ b/solution.py
@@ -4,22 +4,6 @@
 from jax.sharding import PartitionSpec as P
 
 BLOCK = 64
-
-
-def entering(part, axis, combine, identity, reverse):
-    count = lax.axis_size(axis)
-    place = lax.axis_index(axis)
-    ahead = count - 1 - place if reverse else place
-    gathered = jax.tree.map(lambda a: lax.all_gather(a, axis), part)
-    state = jax.tree.map(lambda a, e: jnp.zeros_like(a) + jnp.asarray(e, a.dtype), part, identity)
-
-    def one(step, state):
-        source = count - 1 - step if reverse else step
-        return combine(
-            state, jax.tree.map(lambda a: lax.dynamic_index_in_dim(a, source, 0, False), gathered)
-        )
-
-    return lax.fori_loop(0, ahead, one, state)
 
 
 def local_pass(signal, scaled, rates):
@@ -57,30 +41,22 @@
     return (pieces + extra).reshape(count * BLOCK, pieces.shape[2])
 
 
-def join_states(earlier, later):
-    return (earlier[0] * later[0], earlier[1] * later[0] + later[1])
+def incoming_states(local_state, rates, length, forward):
+    count = lax.axis_size("ctx")
 
+    def shift(carry, step):
+        if forward:
+            pairs = [(i, i + step) for i in range(count - step)]
+        else:
+            pairs = [(i + step, i) for i in range(count - step)]
+        return lax.ppermute(carry, "ctx", pairs)
 
-def incoming_states(local_state, rates, length, forward):
-    local_decay = jnp.exp(-rates * length)
-    empty = jnp.zeros_like(local_state)
-    if forward:
-        joined = entering(
-            (local_decay, local_state),
-            "ctx",
-            join_states,
-            (jnp.ones_like(local_decay), empty),
-            False,
-        )
-    else:
-        joined = entering(
-            (local_decay, local_state),
-            "ctx",
-            join_states,
-            (jnp.ones_like(local_decay), empty),
-            True,
-        )
-    return joined[1]
+    carry = shift(local_state, 1)
+    step = 1
+    while step < count:
+        carry = carry + jnp.exp(-rates * (length * step)) * shift(carry, step)
+        step *= 2
+    return carry
 
 
 def per_device(query, key_proj, value, residues, rates, cotangent):

time: 496 us -> 235 us (0.47)
  the two profiles are of different devices: /device:TPU:6 before, /device:TPU:191 now
where the time goes in v1:
time: 235 us; the launch traced here: 234 us
  waiting for transfers between devices  99.7 us (42%)
  starting transfers between devices  72.5 us (31%)
  matrix products  25.1 us (11%)
  local copies, waits for them, and re-layouts  22.3 us (9%)
  other arithmetic  13.1 us (6%)
    ppermute x14, waiting for transfers between devices, shift(): return lax.ppermute(carry, 'ctx', pairs)  99.7 us
    ppermute x14, starting transfers between devices, shift(): return lax.ppermute(carry, 'ctx', pairs)  72.5 us
    while x16, local copies, waits for them, and re-layouts  19.4 us
    dot_general x8, matrix products, advance(): jnp.dot(lower, lifted, precision=lax.Precision.HIGHEST)  16.1 us
    dot_general x2, matrix products, apply_incoming(): jnp.einsum('ikc,bkc->bic', after, weights, precision=lax.Precision.HIGHEST)  9.04 us
    reduce_sum x8, other arithmetic, advance(): return (states[-1], jnp.sum(scaled[None] * states, axis=1))  6.17 us
  transfers between devices with their start and end apart: 14, of which 14 were waited for; matrix products, arithmetic and copies ran while one was open for 0% of the time, Pallas kernels for 0%

profile of v1, /device:TPU:191, one launch (start us, length us, event | category | flops | bytes accessed | tf_op | source)
XLA Modules:
  0.0 234.4 jit_solution(14323003723435098403)
XLA Ops:
  2.7 22.7 %while.28 = (s32[]{:T(128)}, f32[16,512]{1,0:T(8,128)S(1)}, f32[4,64,512]{2,1,0:T(8,128)S(1)}, f32[4,64,512]{2,1,0:T(8,128)S(1)}, f32[16,512]{1,0:T(8,128)S(1)},...) while((s32[]{:T(128)}, f32[16,512]{1,0:T(8,128)S(1)}, ...), condition=%wide.region_2.3_spmd.clone.clone, body=%wide.region_0.2_spmd.clone.clone.sunk | while | flops 406306816 | bytes 19956588 | solution.py:27
  4.3 2.0 fusion.56
  10.0 2.0 fusion.56
  15.7 2.0 fusion.56
  21.4 2.0 fusion.56
  25.4 10.4 %collective-permute-start = (f32[16,512]{1,0:T(8,128)S(1)}, f32[16,512]{1,0:T(8,128)S(1)}, u32[]{:S(2)}, u32[]{:S(2)}) collective-permute-start(f32[16,512]{1,0:T(8,128)S(1)} %get-tuple-element.101), channel_id=1, source_target_pairs={{0,16},{16,32},{32,48},{48,64},{64,80},{80,96},{96,112},{112,128},... | collective-permute-start | bytes 98312 | tf_op jit(solution)/shard_map/ppermute | solution.py:52
  36.8 10.2 %collective-permute-start.1 = (f32[16,512]{1,0:T(8,128)S(1)}, f32[16,512]{1,0:T(8,128)S(1)}, u32[]{:S(2)}, u32[]{:S(2)}) collective-permute-start(f32[16,512]{1,0:T(8,128)S(1)} %collective-permute-done), channel_id=1, source_target_pairs={{0,16},{16,32},{32,48},{48,64},{64,80},{80,96},{96,112},{112,128},... | collective-permute-start | bytes 98312 | tf_op jit(solution)/shard_map/ppermute | solution.py:52
  48.1 1.9 collective-permute-start.2
  50.0 2.7 %collective-permute-done.2 = f32[16,512]{1,0:T(8,128)S(1)} collective-permute-done((f32[16,512]{1,0:T(8,128)S(1)}, f32[16,512]{1,0:T(8,128)S(1)}, u32[]{:S(2)}, u32[]{:S(2)}) %collective-permute-start.2) | collective-permute-done | bytes 32800 | tf_op jit(solution)/shard_map/ppermute | solution.py:52
  52.8 1.9 collective-permute-start.3
  54.7 3.6 %collective-permute-done.3 = f32[16,512]{1,0:T(8,128)S(1)} collective-permute-done((f32[16,512]{1,0:T(8,128)S(1)}, f32[16,512]{1,0:T(8,128)S(1)}, u32[]{:S(2)}, u32[]{:S(2)}) %collective-permute-start.3) | collective-permute-done | bytes 32800 | tf_op jit(solution)/shard_map/ppermute | solution.py:52
  58.3 2.7 %collective-permute-start.4 = (f32[16,512]{1,0:T(8,128)S(1)}, f32[16,512]{1,0:T(8,128)S(1)}, u32[]{:S(2)}, u32[]{:S(2)}) collective-permute-start(f32[16,512]{1,0:T(8,128)S(1)} %multiply_add_fusion.7), channel_id=1, source_target_pairs={{0,128},{16,144},{32,160},{48,176},{64,192},{80,208},{96,224},{112... | collective-permute-start | bytes 98312 | tf_op jit(solution)/shard_map/ppermute | solution.py:52
  61.0 5.9 %collective-permute-done.4 = f32[16,512]{1,0:T(8,128)S(1)} collective-permute-done((f32[16,512]{1,0:T(8,128)S(1)}, f32[16,512]{1,0:T(8,128)S(1)}, u32[]{:S(2)}, u32[]{:S(2)}) %collective-permute-start.4) | collective-permute-done | bytes 32800 | tf_op jit(solution)/shard_map/ppermute | solution.py:52
  66.9 9.6 %collective-permute-start.5 = (f32[16,512]{1,0:T(8,128)S(1)}, f32[16,512]{1,0:T(8,128)S(1)}, u32[]{:S(2)}, u32[]{:S(2)}) collective-permute-start(f32[16,512]{1,0:T(8,128)S(1)} %multiply_add_fusion.6), channel_id=1, source_target_pairs={{0,256},{16,272},{32,288},{48,304},{64,320},{80,336},{96,352},{112... | collective-permute-start | bytes 98312 | tf_op jit(solution)/shard_map/ppermute | solution.py:52
  77.6 11.4 %collective-permute-start.6 = (f32[16,512]{1,0:T(8,128)S(1)}, f32[16,512]{1,0:T(8,128)S(1)}, u32[]{:S(2)}, u32[]{:S(2)}) collective-permute-start(f32[16,512]{1,0:T(8,128)S(1)} %multiply_add_fusion.5), channel_id=1, source_target_pairs={{0,512},{16,528},{32,544},{48,560},{64,576},{80,592},{96,608},{112... | collective-permute-start | bytes 98312 | tf_op jit(solution)/shard_map/ppermute | solution.py:52
  90.0 4.5 %fusion.25 = f32[512,4,64]{2,1,0:T(4,128)S(1)} fusion(f32[64]{0:T(128)S(1)} %broadcast_add_fusion, f32[16,512]{0,1:T(8,128)S(1)} %copy.27, f32[16,512]{0,1:T(8,128)S(1)} %copy.28, f32[4]{0:T(128)S(1)} %convert_multiply_fusion.6), kind=kOutput, calls=%fused_computation.32 | convolution fusion | flops 25755648 | bytes 590096 | tf_op jit(solution)/shard_map/ikc,bkc->bic/dot_general | solution.py:40
  96.8 22.7 %while.29 = (s32[]{:T(128)}, f32[16,512]{1,0:T(8,128)S(1)}, f32[4,64,512]{2,1,0:T(8,128)S(1)}, f32[4,64,512]{2,1,0:T(8,128)S(1)}, f32[16,512]{1,0:T(8,128)S(1)},...) while((s32[]{:T(128)}, f32[16,512]{1,0:T(8,128)S(1)}, ...), condition=%wide.region_5.6_spmd.clone.clone, body=%wide.region_3.5_spmd.clone.clone.sunk | while | flops 406306816 | bytes 19956588 | solution.py:27
  98.4 2.0 fusion.59
  104.1 2.0 fusion.59
  109.8 2.0 fusion.59
  115.5 2.0 fusion.59
  119.5 13.8 %collective-permute-start.7 = (f32[16,512]{1,0:T(8,128)S(1)}, f32[16,512]{1,0:T(8,128)S(1)}, u32[]{:S(2)}, u32[]{:S(2)}) collective-permute-start(f32[16,512]{1,0:T(8,128)S(1)} %get-tuple-element.103), channel_id=1, source_target_pairs={{16,0},{32,16},{48,32},{64,48},{80,64},{96,80},{112,96},{128,112},... | collective-permute-start | bytes 98312 | tf_op jit(solution)/shard_map/ppermute | solution.py:52
  133.3 20.3 %collective-permute-done.7 = f32[16,512]{1,0:T(8,128)S(1)} collective-permute-done((f32[16,512]{1,0:T(8,128)S(1)}, f32[16,512]{1,0:T(8,128)S(1)}, u32[]{:S(2)}, u32[]{:S(2)}) %collective-permute-start.7) | collective-permute-done | bytes 32800 | tf_op jit(solution)/shard_map/ppermute | solution.py:52
  155.6 9.3 %collective-permute-done.8 = f32[16,512]{1,0:T(8,128)S(1)} collective-permute-done((f32[16,512]{1,0:T(8,128)S(1)}, f32[16,512]{1,0:T(8,128)S(1)}, u32[]{:S(2)}, u32[]{:S(2)}) %collective-permute-start.8) | collective-permute-done | bytes 32800 | tf_op jit(solution)/shard_map/ppermute | solution.py:52
  164.9 1.9 collective-permute-start.9
  166.8 8.8 %collective-permute-done.9 = f32[16,512]{1,0:T(8,128)S(1)} collective-permute-done((f32[16,512]{1,0:T(8,128)S(1)}, f32[16,512]{1,0:T(8,128)S(1)}, u32[]{:S(2)}, u32[]{:S(2)}) %collective-permute-start.9) | collective-permute-done | bytes 32800 | tf_op jit(solution)/shard_map/ppermute | solution.py:52
  175.6 1.9 collective-permute-start.10
  177.6 9.9 %collective-permute-done.10 = f32[16,512]{1,0:T(8,128)S(1)} collective-permute-done((f32[16,512]{1,0:T(8,128)S(1)}, f32[16,512]{1,0:T(8,128)S(1)}, u32[]{:S(2)}, u32[]{:S(2)}) %collective-permute-start.10) | collective-permute-done | bytes 32800 | tf_op jit(solution)/shard_map/ppermute | solution.py:52
  189.4 11.5 %collective-permute-done.11 = f32[16,512]{1,0:T(8,128)S(1)} collective-permute-done((f32[16,512]{1,0:T(8,128)S(1)}, f32[16,512]{1,0:T(8,128)S(1)}, u32[]{:S(2)}, u32[]{:S(2)}) %collective-permute-start.11) | collective-permute-done | bytes 32800 | tf_op jit(solution)/shard_map/ppermute | solution.py:52
  202.1 12.2 %collective-permute-done.12 = f32[16,512]{1,0:T(8,128)S(1)} collective-permute-done((f32[16,512]{1,0:T(8,128)S(1)}, f32[16,512]{1,0:T(8,128)S(1)}, u32[]{:S(2)}, u32[]{:S(2)}) %collective-permute-start.12) | collective-permute-done | bytes 32800 | tf_op jit(solution)/shard_map/ppermute | solution.py:52
  215.9 11.9 %collective-permute-done.13 = f32[16,512]{1,0:T(8,128)S(1)} collective-permute-done((f32[16,512]{1,0:T(8,128)S(1)}, f32[16,512]{1,0:T(8,128)S(1)}, u32[]{:S(2)}, u32[]{:S(2)}) %collective-permute-start.13) | collective-permute-done | bytes 32800 | tf_op jit(solution)/shard_map/ppermute | solution.py:52
  227.9 4.5 %fusion.24 = f32[512,4,64]{2,1,0:T(4,128)S(1)} fusion(f32[64]{0:T(128)S(1)} %broadcast_add_fusion, f32[16,512]{0,1:T(8,128)S(1)} %copy.27, f32[16,512]{0,1:T(8,128)S(1)} %copy.31, f32[4]{0:T(128)S(1)} %convert_multiply_fusion.6), kind=kOutput, calls=%fused_computation.31 | convolution fusion | flops 25755648 | bytes 590096 | tf_op jit(solution)/shard_map/ikc,bkc->bic/dot_general | solution.py:40
  (115 shorter events, 45.7 us)
Async XLA Ops:
  0.6 2.1 copy-start
  25.4 11.4 %collective-permute-start = (f32[16,512]{1,0:T(8,128)S(1)}, f32[16,512]{1,0:T(8,128)S(1)}, u32[]{:S(2)}, u32[]{:S(2)}) collective-permute-start(f32[16,512]{1,0:T(8,128)S(1)} %get-tuple-element.101), channel_id=1, source_target_pairs={{0,16},{16,32},{32,48},{48,64},{64,80},{80,96},{96,112},{112,128},... | collective-permute-start | bytes 98312 | tf_op jit(solution)/shard_map/ppermute | solution.py:52
  36.8 11.2 %collective-permute-start.1 = (f32[16,512]{1,0:T(8,128)S(1)}, f32[16,512]{1,0:T(8,128)S(1)}, u32[]{:S(2)}, u32[]{:S(2)}) collective-permute-start(f32[16,512]{1,0:T(8,128)S(1)} %collective-permute-done), channel_id=1, source_target_pairs={{0,16},{16,32},{32,48},{48,64},{64,80},{80,96},{96,112},{112,128},... | collective-permute-start | bytes 98312 | tf_op jit(solution)/shard_map/ppermute | solution.py:52
  48.1 4.7 %collective-permute-start.2 = (f32[16,512]{1,0:T(8,128)S(1)}, f32[16,512]{1,0:T(8,128)S(1)}, u32[]{:S(2)}, u32[]{:S(2)}) collective-permute-start(f32[16,512]{1,0:T(8,128)S(1)} %multiply_add_fusion.9), channel_id=1, source_target_pairs={{0,32},{16,48},{32,64},{48,80},{64,96},{80,112},{96,128},{112,144}... | collective-permute-start | bytes 98312 | tf_op jit(solution)/shard_map/ppermute | solution.py:52
  52.8 5.6 %collective-permute-start.3 = (f32[16,512]{1,0:T(8,128)S(1)}, f32[16,512]{1,0:T(8,128)S(1)}, u32[]{:S(2)}, u32[]{:S(2)}) collective-permute-start(f32[16,512]{1,0:T(8,128)S(1)} %multiply_add_fusion.8), channel_id=1, source_target_pairs={{0,64},{16,80},{32,96},{48,112},{64,128},{80,144},{96,160},{112,17... | collective-permute-start | bytes 98312 | tf_op jit(solution)/shard_map/ppermute | solution.py:52
  58.3 8.6 %collective-permute-start.4 = (f32[16,512]{1,0:T(8,128)S(1)}, f32[16,512]{1,0:T(8,128)S(1)}, u32[]{:S(2)}, u32[]{:S(2)}) collective-permute-start(f32[16,512]{1,0:T(8,128)S(1)} %multiply_add_fusion.7), channel_id=1, source_target_pairs={{0,128},{16,144},{32,160},{48,176},{64,192},{80,208},{96,224},{112... | collective-permute-start | bytes 98312 | tf_op jit(solution)/shard_map/ppermute | solution.py:52
  66.9 10.6 %collective-permute-start.5 = (f32[16,512]{1,0:T(8,128)S(1)}, f32[16,512]{1,0:T(8,128)S(1)}, u32[]{:S(2)}, u32[]{:S(2)}) collective-permute-start(f32[16,512]{1,0:T(8,128)S(1)} %multiply_add_fusion.6), channel_id=1, source_target_pairs={{0,256},{16,272},{32,288},{48,304},{64,320},{80,336},{96,352},{112... | collective-permute-start | bytes 98312 | tf_op jit(solution)/shard_map/ppermute | solution.py:52
  77.6 12.2 %collective-permute-start.6 = (f32[16,512]{1,0:T(8,128)S(1)}, f32[16,512]{1,0:T(8,128)S(1)}, u32[]{:S(2)}, u32[]{:S(2)}) collective-permute-start(f32[16,512]{1,0:T(8,128)S(1)} %multiply_add_fusion.5), channel_id=1, source_target_pairs={{0,512},{16,528},{32,544},{48,560},{64,576},{80,592},{96,608},{112... | collective-permute-start | bytes 98312 | tf_op jit(solution)/shard_map/ppermute | solution.py:52
  94.5 1.0 copy-start.3
  94.5 1.0 copy-start.4
  119.5 34.1 %collective-permute-start.7 = (f32[16,512]{1,0:T(8,128)S(1)}, f32[16,512]{1,0:T(8,128)S(1)}, u32[]{:S(2)}, u32[]{:S(2)}) collective-permute-start(f32[16,512]{1,0:T(8,128)S(1)} %get-tuple-element.103), channel_id=1, source_target_pairs={{16,0},{32,16},{48,32},{64,48},{80,64},{96,80},{112,96},{128,112},... | collective-permute-start | bytes 98312 | tf_op jit(solution)/shard_map/ppermute | solution.py:52
  153.7 11.2 %collective-permute-start.8 = (f32[16,512]{1,0:T(8,128)S(1)}, f32[16,512]{1,0:T(8,128)S(1)}, u32[]{:S(2)}, u32[]{:S(2)}) collective-permute-start(f32[16,512]{1,0:T(8,128)S(1)} %collective-permute-done.7), channel_id=1, source_target_pairs={{16,0},{32,16},{48,32},{64,48},{80,64},{96,80},{112,96},{128,112},... | collective-permute-start | bytes 98312 | tf_op jit(solution)/shard_map/ppermute | solution.py:52
  164.9 10.7 %collective-permute-start.9 = (f32[16,512]{1,0:T(8,128)S(1)}, f32[16,512]{1,0:T(8,128)S(1)}, u32[]{:S(2)}, u32[]{:S(2)}) collective-permute-start(f32[16,512]{1,0:T(8,128)S(1)} %multiply_add_fusion.4), channel_id=1, source_target_pairs={{32,0},{48,16},{64,32},{80,48},{96,64},{112,80},{128,96},{144,112}... | collective-permute-start | bytes 98312 | tf_op jit(solution)/shard_map/ppermute | solution.py:52
  175.6 11.8 %collective-permute-start.10 = (f32[16,512]{1,0:T(8,128)S(1)}, f32[16,512]{1,0:T(8,128)S(1)}, u32[]{:S(2)}, u32[]{:S(2)}) collective-permute-start(f32[16,512]{1,0:T(8,128)S(1)} %multiply_add_fusion.3), channel_id=1, source_target_pairs={{64,0},{80,16},{96,32},{112,48},{128,64},{144,80},{160,96},{176,11... | collective-permute-start | bytes 98312 | tf_op jit(solution)/shard_map/ppermute | solution.py:52
  187.4 13.4 %collective-permute-start.11 = (f32[16,512]{1,0:T(8,128)S(1)}, f32[16,512]{1,0:T(8,128)S(1)}, u32[]{:S(2)}, u32[]{:S(2)}) collective-permute-start(f32[16,512]{1,0:T(8,128)S(1)} %multiply_add_fusion.2), channel_id=1, source_target_pairs={{128,0},{144,16},{160,32},{176,48},{192,64},{208,80},{224,96},{240... | collective-permute-start | bytes 98312 | tf_op jit(solution)/shard_map/ppermute | solution.py:52
  200.8 13.5 %collective-permute-start.12 = (f32[16,512]{1,0:T(8,128)S(1)}, f32[16,512]{1,0:T(8,128)S(1)}, u32[]{:S(2)}, u32[]{:S(2)}) collective-permute-start(f32[16,512]{1,0:T(8,128)S(1)} %multiply_add_fusion.1), channel_id=1, source_target_pairs={{256,0},{272,16},{288,32},{304,48},{320,64},{336,80},{352,96},{368... | collective-permute-start | bytes 98312 | tf_op jit(solution)/shard_map/ppermute | solution.py:52
  214.4 13.4 %collective-permute-start.13 = (f32[16,512]{1,0:T(8,128)S(1)}, f32[16,512]{1,0:T(8,128)S(1)}, u32[]{:S(2)}, u32[]{:S(2)}) collective-permute-start(f32[16,512]{1,0:T(8,128)S(1)} %multiply_add_fusion), channel_id=1, source_target_pairs={{512,0},{528,16},{544,32},{560,48},{576,64},{592,80},{608,96},{624... | collective-permute-start | bytes 98312 | tf_op jit(solution)/shard_map/ppermute | solution.py:52
  232.4 1.0 copy-start.1
  232.4 1.0 copy-start.2

commit v2 on v1

--- a/solution.py
+++ b/solution.py
@@ -41,22 +41,46 @@
     return (pieces + extra).reshape(count * BLOCK, pieces.shape[2])
 
 
-def incoming_states(local_state, rates, length, forward):
+def end_state(signal, rates):
+    length, width = signal.shape
+    part = 16
+    lags = jnp.arange(part).astype(jnp.float32)
+    inner = jnp.exp(-rates[None] * (part - 1.0 - lags)[:, None, None])
+    outer = jnp.exp(-rates[None] * (part * (length // part - 1.0 - jnp.arange(length // part)))[:, None, None])
+    rows = signal.reshape(length // part, part, 1, width)
+    return jnp.sum(outer * jnp.sum(inner[None] * rows, axis=1), axis=0)
+
+
+def incoming_states(fwd_state, bwd_state, rates, length, cover):
     count = lax.axis_size("ctx")
-
-    def shift(carry, step):
-        if forward:
-            pairs = [(i, i + step) for i in range(count - step)]
-        else:
-            pairs = [(i + step, i) for i in range(count - step)]
-        return lax.ppermute(carry, "ctx", pairs)
-
-    carry = shift(local_state, 1)
-    step = 1
-    while step < count:
-        carry = carry + jnp.exp(-rates * (length * step)) * shift(carry, step)
-        step *= 2
-    return carry
+    radix = 4
+    fwd_sum, bwd_sum = fwd_state, bwd_state
+    fwd_in = jnp.zeros_like(fwd_state)
+    bwd_in = jnp.zeros_like(bwd_state)
+    span = 1
+    while span < count:
+        last = span * radix >= count
+        fwd_next, bwd_next = fwd_sum, bwd_sum
+        for k in range(1, radix):
+            step = k * span
+            if step >= count:
+                break
+            ahead = [(i, i + step) for i in range(count - step)]
+            behind = [(i + step, i) for i in range(count - step)]
+            fwd_got = lax.ppermute(fwd_sum, "ctx", ahead)
+            bwd_got = lax.ppermute(bwd_sum, "ctx", behind)
+            if last:
+                fwd_got, bwd_got, cover = lax.optimization_barrier((fwd_got, bwd_got, cover))
+            into = jnp.exp(-rates * (length * (step - 1.0)))
+            fwd_in = fwd_in + into * fwd_got
+            bwd_in = bwd_in + into * bwd_got
+            if not last:
+                past = jnp.exp(-rates * (length * step))
+                fwd_next = fwd_next + past * fwd_got
+                bwd_next = bwd_next + past * bwd_got
+        fwd_sum, bwd_sum = fwd_next, bwd_next
+        span *= radix
+    return fwd_in, bwd_in, cover
 
 
 def per_device(query, key_proj, value, residues, rates, cotangent):
@@ -68,10 +92,16 @@
     scaled = residues * jnp.sqrt(-jnp.expm1(-2.0 * rates))
     gated = lax.optimization_barrier((query_f * key_f).astype(jnp.bfloat16)).astype(jnp.float32)
     weighted = cot_f * value_f
-    fwd_state, fwd_pieces = local_pass(gated, scaled, rates)
-    bwd_state, bwd_pieces = local_pass(weighted[::-1], scaled, rates)
-    fwd_in = incoming_states(fwd_state, rates, length, True)
-    bwd_in = incoming_states(bwd_state, rates, length, False)
+    reversed_weighted = weighted[::-1]
+    _, fwd_pieces = local_pass(gated, scaled, rates)
+    _, bwd_pieces = local_pass(reversed_weighted, scaled, rates)
+    fwd_in, bwd_in, (fwd_pieces, bwd_pieces) = incoming_states(
+        end_state(gated, rates),
+        end_state(reversed_weighted, rates),
+        rates,
+        length,
+        (fwd_pieces, bwd_pieces),
+    )
     mixed = apply_incoming(fwd_pieces, fwd_in, scaled, rates)
     back = apply_incoming(bwd_pieces, bwd_in, scaled, rates)[::-1]
     output = (value_f * mixed).astype(jnp.bfloat16)

time: 235 us -> 177 us (0.75)
  the two profiles are of different devices: /device:TPU:191 before, /device:TPU:10 now
where the time goes in v2:
time: 177 us; the launch traced here: 176 us
  starting transfers between devices  102 us (58%)
  matrix products  26.1 us (15%)
  local copies, waits for them, and re-layouts  23.5 us (13%)
  other arithmetic  16.5 us (9%)
  waiting for transfers between devices  5.36 us (3%)
    ppermute x9, starting transfers between devices, incoming_states(): fwd_got = lax.ppermute(fwd_sum, 'ctx', ahead)  89.6 us
    while x16, local copies, waits for them, and re-layouts  19.4 us
    dot_general x8, matrix products, advance(): jnp.dot(lower, lifted, precision=lax.Precision.HIGHEST)  16.1 us
    ppermute x9, starting transfers between devices, incoming_states(): bwd_got = lax.ppermute(bwd_sum, 'ctx', behind)  12.9 us
    dot_general x2, matrix products, apply_incoming(): jnp.einsum('ikc,bkc->bic', after, weights, precision=lax.Precision.HIGHEST)  9.99 us
    reduce_sum x8, other arithmetic, advance(): return (states[-1], jnp.sum(scaled[None] * states, axis=1))  6.17 us
    ppermute x9, waiting for transfers between devices, incoming_states(): bwd_got = lax.ppermute(bwd_sum, 'ctx', behind)  4 us
  transfers between devices with their start and end apart: 18, of which 3 were waited for; matrix products, arithmetic and copies ran while one was open for 26% of the time, Pallas kernels for 0%

profile of v2, /device:TPU:10, one launch (start us, length us, event | category | flops | bytes accessed | tf_op | source)
XLA Modules:
  0.0 176.3 jit_solution(3845639632001200044)
XLA Ops:
  3.2 2.0 %multiply_reduce_fusion.2 = (f32[16,16,512]{2,1,0:T(8,128)S(1)}, f32[16,16,512]{2,1,0:T(8,128)S(1)}) fusion(f32[16,16,512]{2,1,0:T(8,128)S(1)} %bitcast.80, f32[16,16,512]{2,1,0:T(8,128)S(1)} %multiply_exponential_fusion.6, f32[16,16,512]{2,1,0:T(8,128)S(1)} %bitcast.78), kind=kLoop, calls=%fused_computation.30 | loop fusion | flops 8126464 | bytes 2621440 | tf_op jit(solution)/shard_map/reduce_sum | solution.py:51
  5.4 1.9 %collective-permute-start = (f32[16,512]{1,0:T(8,128)S(1)}, f32[16,512]{1,0:T(8,128)S(1)}, u32[]{:S(2)}, u32[]{:S(2)}) collective-permute-start(f32[16,512]{1,0:T(8,128)S(1)} %get-tuple-element.235), channel_id=1, source_target_pairs={{0,16},{16,32},{32,48},{48,64},{64,80},{80,96},{96,112},{112,128},... | collective-permute-start | bytes 98312 | tf_op jit(solution)/shard_map/ppermute | solution.py:70
  7.3 3.5 %collective-permute-start.1 = (f32[16,512]{1,0:T(8,128)S(1)}, f32[16,512]{1,0:T(8,128)S(1)}, u32[]{:S(2)}, u32[]{:S(2)}) collective-permute-start(f32[16,512]{1,0:T(8,128)S(1)} %get-tuple-element.235), channel_id=1, source_target_pairs={{0,32},{16,48},{32,64},{48,80},{64,96},{80,112},{96,128},{112,144}... | collective-permute-start | bytes 98312 | tf_op jit(solution)/shard_map/ppermute | solution.py:70
  10.8 5.7 %collective-permute-start.2 = (f32[16,512]{1,0:T(8,128)S(1)}, f32[16,512]{1,0:T(8,128)S(1)}, u32[]{:S(2)}, u32[]{:S(2)}) collective-permute-start(f32[16,512]{1,0:T(8,128)S(1)} %get-tuple-element.235), channel_id=1, source_target_pairs={{0,48},{16,64},{32,80},{48,96},{64,112},{80,128},{96,144},{112,160... | collective-permute-start | bytes 98312 | tf_op jit(solution)/shard_map/ppermute | solution.py:70
  16.5 1.9 %collective-permute-start.7 = (f32[16,512]{1,0:T(8,128)S(1)}, f32[16,512]{1,0:T(8,128)S(1)}, u32[]{:S(2)}, u32[]{:S(2)}) collective-permute-start(f32[16,512]{1,0:T(8,128)S(1)} %get-tuple-element.234), channel_id=1, source_target_pairs={{16,0},{32,16},{48,32},{64,48},{80,64},{96,80},{112,96},{128,112},... | collective-permute-start | bytes 98312 | tf_op jit(solution)/shard_map/ppermute | solution.py:71
  18.4 1.9 %collective-permute-start.8 = (f32[16,512]{1,0:T(8,128)S(1)}, f32[16,512]{1,0:T(8,128)S(1)}, u32[]{:S(2)}, u32[]{:S(2)}) collective-permute-start(f32[16,512]{1,0:T(8,128)S(1)} %get-tuple-element.234), channel_id=1, source_target_pairs={{32,0},{48,16},{64,32},{80,48},{96,64},{112,80},{128,96},{144,112}... | collective-permute-start | bytes 98312 | tf_op jit(solution)/shard_map/ppermute | solution.py:71
  20.4 1.3 collective-permute-start.9
  21.7 2.5 %collective-permute-done.8 = f32[16,512]{1,0:T(8,128)S(1)} collective-permute-done((f32[16,512]{1,0:T(8,128)S(1)}, f32[16,512]{1,0:T(8,128)S(1)}, u32[]{:S(2)}, u32[]{:S(2)}) %collective-permute-start.8) | collective-permute-done | bytes 32800 | tf_op jit(solution)/shard_map/ppermute | solution.py:71
  24.2 1.5 collective-permute-done.9
  27.1 1.3 collective-permute-start.11
  28.4 1.3 collective-permute-start.12
  29.7 7.1 %collective-permute-start.3 = (f32[16,512]{1,0:T(8,128)S(1)}, f32[16,512]{1,0:T(8,128)S(1)}, u32[]{:S(2)}, u32[]{:S(2)}) collective-permute-start(f32[16,512]{1,0:T(8,128)S(1)} %get-tuple-element.281), channel_id=1, source_target_pairs={{0,64},{16,80},{32,96},{48,112},{64,128},{80,144},{96,160},{112,17... | collective-permute-start | bytes 98312 | tf_op jit(solution)/shard_map/ppermute | solution.py:70
  36.8 17.1 %collective-permute-start.4 = (f32[16,512]{1,0:T(8,128)S(1)}, f32[16,512]{1,0:T(8,128)S(1)}, u32[]{:S(2)}, u32[]{:S(2)}) collective-permute-start(f32[16,512]{1,0:T(8,128)S(1)} %get-tuple-element.281), channel_id=1, source_target_pairs={{0,128},{16,144},{32,160},{48,176},{64,192},{80,208},{96,224},{112... | collective-permute-start | bytes 98312 | tf_op jit(solution)/shard_map/ppermute | solution.py:70
  53.8 14.4 %collective-permute-start.5 = (f32[16,512]{1,0:T(8,128)S(1)}, f32[16,512]{1,0:T(8,128)S(1)}, u32[]{:S(2)}, u32[]{:S(2)}) collective-permute-start(f32[16,512]{1,0:T(8,128)S(1)} %get-tuple-element.281), channel_id=1, source_target_pairs={{0,192},{16,208},{32,224},{48,240},{64,256},{80,272},{96,288},{112... | collective-permute-start | bytes 98312 | tf_op jit(solution)/shard_map/ppermute | solution.py:70
  68.5 1.3 collective-permute-done.5
  69.9 11.8 %collective-permute-start.16 = (f32[16,512]{1,0:T(8,128)S(1)}, f32[16,512]{1,0:T(8,128)S(1)}, u32[]{:S(2)}, u32[]{:S(2)}) collective-permute-start(f32[16,512]{1,0:T(8,128)S(1)} %get-tuple-element.285), channel_id=1, source_target_pairs={{0,256},{16,272},{32,288},{48,304},{64,320},{80,336},{96,352},{112... | collective-permute-start | bytes 98312 | tf_op jit(solution)/shard_map/ppermute | solution.py:70
  81.8 22.7 %while.29 = (s32[]{:T(128)}, f32[16,512]{1,0:T(8,128)S(1)}, f32[4,64,512]{2,1,0:T(8,128)S(1)}, f32[4,64,512]{2,1,0:T(8,128)S(1)}, f32[16,512]{1,0:T(8,128)S(1)},...) while((s32[]{:T(128)}, f32[16,512]{1,0:T(8,128)S(1)}, ...), condition=%wide.region_9.10_spmd.clone.clone, body=%wide.region_7.9_spmd.clone.clone.sunk | while | flops 406306816 | bytes 19956588 | solution.py:27
  83.4 2.0 %fusion.58 = f32[8192,64]{0,1:T(8,128)S(1)} fusion(f32[64,8192]{1,0:T(8,128)S(1)} %bitcast.73, f32[64]{0:T(128)S(1)} %get-tuple-element.462), kind=kOutput, calls=%fused_computation.25.clone.1 | convolution fusion | flops 402661376 | bytes 4194560 | tf_op jit(solution)/shard_map/while/body/eval_jaxpr/dot_general | solution.py:21
  89.1 2.0 %fusion.58 = f32[8192,64]{0,1:T(8,128)S(1)} fusion(f32[64,8192]{1,0:T(8,128)S(1)} %bitcast.73, f32[64]{0:T(128)S(1)} %get-tuple-element.462), kind=kOutput, calls=%fused_computation.25.clone.1 | convolution fusion | flops 402661376 | bytes 4194560 | tf_op jit(solution)/shard_map/while/body/eval_jaxpr/dot_general | solution.py:21
  94.8 2.0 %fusion.58 = f32[8192,64]{0,1:T(8,128)S(1)} fusion(f32[64,8192]{1,0:T(8,128)S(1)} %bitcast.73, f32[64]{0:T(128)S(1)} %get-tuple-element.462), kind=kOutput, calls=%fused_computation.25.clone.1 | convolution fusion | flops 402661376 | bytes 4194560 | tf_op jit(solution)/shard_map/while/body/eval_jaxpr/dot_general | solution.py:21
  100.5 2.0 %fusion.58 = f32[8192,64]{0,1:T(8,128)S(1)} fusion(f32[64,8192]{1,0:T(8,128)S(1)} %bitcast.73, f32[64]{0:T(128)S(1)} %get-tuple-element.462), kind=kOutput, calls=%fused_computation.25.clone.1 | convolution fusion | flops 402661376 | bytes 4194560 | tf_op jit(solution)/shard_map/while/body/eval_jaxpr/dot_general | solution.py:21
  104.5 13.5 %collective-permute-start.14 = (f32[16,512]{1,0:T(8,128)S(1)}, f32[16,512]{1,0:T(8,128)S(1)}, u32[]{:S(2)}, u32[]{:S(2)}) collective-permute-start(f32[16,512]{1,0:T(8,128)S(1)} %get-tuple-element.285), channel_id=1, source_target_pairs={{0,512},{16,528},{32,544},{48,560},{64,576},{80,592},{96,608},{112... | collective-permute-start | bytes 98312 | tf_op jit(solution)/shard_map/ppermute | solution.py:70
  121.9 14.6 %collective-permute-start.6 = (f32[16,512]{1,0:T(8,128)S(1)}, f32[16,512]{1,0:T(8,128)S(1)}, u32[]{:S(2)}, u32[]{:S(2)}) collective-permute-start(f32[16,512]{1,0:T(8,128)S(1)} %get-tuple-element.285), channel_id=1, source_target_pairs={{0,768},{16,784},{32,800},{48,816},{64,832},{80,848},{96,864},{112... | collective-permute-start | bytes 98312 | tf_op jit(solution)/shard_map/ppermute | solution.py:70
  136.6 22.9 %while.28 = (s32[]{:T(128)}, f32[16,512]{1,0:T(8,128)S(1)}, f32[4,64,512]{2,1,0:T(8,128)S(1)}, f32[4,64,512]{2,1,0:T(8,128)S(1)}, f32[16,512]{1,0:T(8,128)S(1)},...) while((s32[]{:T(128)}, f32[16,512]{1,0:T(8,128)S(1)}, ...), condition=%wide.region_6.7_spmd.clone.clone, body=%wide.region_4.0_spmd.clone.clone.sunk | while | flops 406306816 | bytes 19956588 | solution.py:27
  138.2 2.0 %fusion.55 = f32[8192,64]{0,1:T(8,128)S(1)} fusion(f32[64,8192]{1,0:T(8,128)S(1)} %bitcast.76, f32[64]{0:T(128)S(1)} %get-tuple-element.432), kind=kOutput, calls=%fused_computation.13.clone.1 | convolution fusion | flops 402661376 | bytes 4194560 | tf_op jit(solution)/shard_map/while/body/eval_jaxpr/dot_general | solution.py:21
  143.9 2.0 %fusion.55 = f32[8192,64]{0,1:T(8,128)S(1)} fusion(f32[64,8192]{1,0:T(8,128)S(1)} %bitcast.76, f32[64]{0:T(128)S(1)} %get-tuple-element.432), kind=kOutput, calls=%fused_computation.13.clone.1 | convolution fusion | flops 402661376 | bytes 4194560 | tf_op jit(solution)/shard_map/while/body/eval_jaxpr/dot_general | solution.py:21
  149.6 2.0 %fusion.55 = f32[8192,64]{0,1:T(8,128)S(1)} fusion(f32[64,8192]{1,0:T(8,128)S(1)} %bitcast.76, f32[64]{0:T(128)S(1)} %get-tuple-element.432), kind=kOutput, calls=%fused_computation.13.clone.1 | convolution fusion | flops 402661376 | bytes 4194560 | tf_op jit(solution)/shard_map/while/body/eval_jaxpr/dot_general | solution.py:21
  155.3 2.0 %fusion.55 = f32[8192,64]{0,1:T(8,128)S(1)} fusion(f32[64,8192]{1,0:T(8,128)S(1)} %bitcast.76, f32[64]{0:T(128)S(1)} %get-tuple-element.432), kind=kOutput, calls=%fused_computation.13.clone.1 | convolution fusion | flops 402661376 | bytes 4194560 | tf_op jit(solution)/shard_map/while/body/eval_jaxpr/dot_general | solution.py:21
  160.5 4.5 %fusion.25 = f32[512,4,64]{2,1,0:T(4,128)S(1)} fusion(f32[64]{0:T(128)S(1)} %broadcast_add_fusion, f32[16,512]{0,1:T(8,128)S(1)} %copy.35, f32[16,512]{0,1:T(8,128)S(1)} %copy.36, f32[4]{0:T(128)S(1)} %convert_multiply_fusion.6), kind=kOutput, calls=%fused_computation.34 | convolution fusion | flops 25755648 | bytes 590096 | tf_op jit(solution)/shard_map/ikc,bkc->bic/dot_general | solution.py:40
  165.9 5.5 %fusion.24 = f32[512,4,64]{2,1,0:T(4,128)} fusion(f32[64]{0:T(128)S(1)} %broadcast_add_fusion, f32[16,512]{0,1:T(8,128)S(1)} %copy-done.6, f32[16,512]{0,1:T(8,128)S(1)} %copy.39, f32[4]{0:T(128)S(1)} %convert_multiply_fusion.6), kind=kOutput, calls=%fused_computation.33 | convolution fusion | flops 25755648 | bytes 590096 | tf_op jit(solution)/shard_map/ikc,bkc->bic/dot_general | solution.py:40
  171.4 1.5 copy.40
  173.5 1.9 %fusion.33 = (bf16[256,512]{1,0:T(8,128)(2,1)}, bf16[256,512]{1,0:T(8,128)(2,1)}) fusion(f32[256,512]{1,0:T(8,128)S(1)} %rev.7, bf16[256,512]{1,0:T(8,128)(2,1)} %param.10, bf16[256,512]{1,0:T(8,128)(2,1)S(1)} %copy-done.1), kind=kLoop, calls=%fused_computation.49 | loop fusion | flops 786432 | bytes 1572864 | tf_op jit(solution)/shard_map/convert_element_type | solution.py:110
  (162 shorter events, 39.9 us)
Async XLA Ops:
  3.0 22.7 %copy-start = (f32[16,512]{1,0:T(8,128)S(1)}, f32[16,512]{1,0:T(8,128)}, u32[]{:S(2)}) copy-start(f32[16,512]{1,0:T(8,128)} %param.14) | copy-start | bytes 98308
  3.0 22.7 %copy-start.19 = (f32[16,512]{1,0:T(8,128)S(1)}, f32[16,512]{1,0:T(8,128)}, u32[]{:S(2)}) copy-start(f32[16,512]{1,0:T(8,128)} %param.13) | copy-start | bytes 98308
  5.4 15.0 %collective-permute-start = (f32[16,512]{1,0:T(8,128)S(1)}, f32[16,512]{1,0:T(8,128)S(1)}, u32[]{:S(2)}, u32[]{:S(2)}) collective-permute-start(f32[16,512]{1,0:T(8,128)S(1)} %get-tuple-element.235), channel_id=1, source_target_pairs={{0,16},{16,32},{32,48},{48,64},{64,80},{80,96},{96,112},{112,128},... | collective-permute-start | bytes 98312 | tf_op jit(solution)/shard_map/ppermute | solution.py:70
  7.3 14.4 %collective-permute-start.1 = (f32[16,512]{1,0:T(8,128)S(1)}, f32[16,512]{1,0:T(8,128)S(1)}, u32[]{:S(2)}, u32[]{:S(2)}) collective-permute-start(f32[16,512]{1,0:T(8,128)S(1)} %get-tuple-element.235), channel_id=1, source_target_pairs={{0,32},{16,48},{32,64},{48,80},{64,96},{80,112},{96,128},{112,144}... | collective-permute-start | bytes 98312 | tf_op jit(solution)/shard_map/ppermute | solution.py:70
  10.8 10.9 %collective-permute-start.2 = (f32[16,512]{1,0:T(8,128)S(1)}, f32[16,512]{1,0:T(8,128)S(1)}, u32[]{:S(2)}, u32[]{:S(2)}) collective-permute-start(f32[16,512]{1,0:T(8,128)S(1)} %get-tuple-element.235), channel_id=1, source_target_pairs={{0,48},{16,64},{32,80},{48,96},{64,112},{80,128},{96,144},{112,160... | collective-permute-start | bytes 98312 | tf_op jit(solution)/shard_map/ppermute | solution.py:70
  16.5 5.2 %collective-permute-start.7 = (f32[16,512]{1,0:T(8,128)S(1)}, f32[16,512]{1,0:T(8,128)S(1)}, u32[]{:S(2)}, u32[]{:S(2)}) collective-permute-start(f32[16,512]{1,0:T(8,128)S(1)} %get-tuple-element.234), channel_id=1, source_target_pairs={{16,0},{32,16},{48,32},{64,48},{80,64},{96,80},{112,96},{128,112},... | collective-permute-start | bytes 98312 | tf_op jit(solution)/shard_map/ppermute | solution.py:71
  18.4 5.8 %collective-permute-start.8 = (f32[16,512]{1,0:T(8,128)S(1)}, f32[16,512]{1,0:T(8,128)S(1)}, u32[]{:S(2)}, u32[]{:S(2)}) collective-permute-start(f32[16,512]{1,0:T(8,128)S(1)} %get-tuple-element.234), channel_id=1, source_target_pairs={{32,0},{48,16},{64,32},{80,48},{96,64},{112,80},{128,96},{144,112}... | collective-permute-start | bytes 98312 | tf_op jit(solution)/shard_map/ppermute | solution.py:71
  20.4 5.3 %collective-permute-start.9 = (f32[16,512]{1,0:T(8,128)S(1)}, f32[16,512]{1,0:T(8,128)S(1)}, u32[]{:S(2)}, u32[]{:S(2)}) collective-permute-start(f32[16,512]{1,0:T(8,128)S(1)} %get-tuple-element.234), channel_id=1, source_target_pairs={{48,0},{64,16},{80,32},{96,48},{112,64},{128,80},{144,96},{160,112... | collective-permute-start | bytes 98312 | tf_op jit(solution)/shard_map/ppermute | solution.py:71
  21.7 60.0 %copy-start.7 = (f32[16,512]{1,0:T(8,128)}, f32[16,512]{1,0:T(8,128)S(1)}, u32[]{:S(2)}) copy-start(f32[16,512]{1,0:T(8,128)S(1)} %collective-permute-done.7) | copy-start | bytes 98308
  24.2 44.0 %copy-start.9 = (f32[16,512]{1,0:T(8,128)}, f32[16,512]{1,0:T(8,128)S(1)}, u32[]{:S(2)}) copy-start(f32[16,512]{1,0:T(8,128)S(1)} %collective-permute-done.8) | copy-start | bytes 98308
  25.7 42.6 %copy-start.11 = (f32[16,512]{1,0:T(8,128)}, f32[16,512]{1,0:T(8,128)S(1)}, u32[]{:S(2)}) copy-start(f32[16,512]{1,0:T(8,128)S(1)} %collective-permute-done.9) | copy-start | bytes 98308
  25.8 28.1 %collective-permute-start.10 = (f32[16,512]{1,0:T(8,128)S(1)}, f32[16,512]{1,0:T(8,128)S(1)}, u32[]{:S(2)}, u32[]{:S(2)}) collective-permute-start(f32[16,512]{1,0:T(8,128)S(1)} %get-tuple-element.282), channel_id=1, source_target_pairs={{64,0},{80,16},{96,32},{112,48},{128,64},{144,80},{160,96},{176,11... | collective-permute-start | bytes 98312 | tf_op jit(solution)/shard_map/ppermute | solution.py:71
  27.1 41.3 %collective-permute-start.11 = (f32[16,512]{1,0:T(8,128)S(1)}, f32[16,512]{1,0:T(8,128)S(1)}, u32[]{:S(2)}, u32[]{:S(2)}) collective-permute-start(f32[16,512]{1,0:T(8,128)S(1)} %get-tuple-element.282), channel_id=1, source_target_pairs={{128,0},{144,16},{160,32},{176,48},{192,64},{208,80},{224,96},{240... | collective-permute-start | bytes 98312 | tf_op jit(solution)/shard_map/ppermute | solution.py:71
  28.4 40.1 %collective-permute-start.12 = (f32[16,512]{1,0:T(8,128)S(1)}, f32[16,512]{1,0:T(8,128)S(1)}, u32[]{:S(2)}, u32[]{:S(2)}) collective-permute-start(f32[16,512]{1,0:T(8,128)S(1)} %get-tuple-element.282), channel_id=1, source_target_pairs={{192,0},{208,16},{224,32},{240,48},{256,64},{272,80},{288,96},{304... | collective-permute-start | bytes 98312 | tf_op jit(solution)/shard_map/ppermute | solution.py:71
  29.7 38.8 %collective-permute-start.3 = (f32[16,512]{1,0:T(8,128)S(1)}, f32[16,512]{1,0:T(8,128)S(1)}, u32[]{:S(2)}, u32[]{:S(2)}) collective-permute-start(f32[16,512]{1,0:T(8,128)S(1)} %get-tuple-element.281), channel_id=1, source_target_pairs={{0,64},{16,80},{32,96},{48,112},{64,128},{80,144},{96,160},{112,17... | collective-permute-start | bytes 98312 | tf_op jit(solution)/shard_map/ppermute | solution.py:70
  36.8 31.7 %collective-permute-start.4 = (f32[16,512]{1,0:T(8,128)S(1)}, f32[16,512]{1,0:T(8,128)S(1)}, u32[]{:S(2)}, u32[]{:S(2)}) collective-permute-start(f32[16,512]{1,0:T(8,128)S(1)} %get-tuple-element.281), channel_id=1, source_target_pairs={{0,128},{16,144},{32,160},{48,176},{64,192},{80,208},{96,224},{112... | collective-permute-start | bytes 98312 | tf_op jit(solution)/shard_map/ppermute | solution.py:70
  53.8 27.9 %copy-start.13 = (f32[16,512]{1,0:T(8,128)}, f32[16,512]{1,0:T(8,128)S(1)}, u32[]{:S(2)}) copy-start(f32[16,512]{1,0:T(8,128)S(1)} %collective-permute-done.10) | copy-start | bytes 98308
  53.8 16.0 %collective-permute-start.5 = (f32[16,512]{1,0:T(8,128)S(1)}, f32[16,512]{1,0:T(8,128)S(1)}, u32[]{:S(2)}, u32[]{:S(2)}) collective-permute-start(f32[16,512]{1,0:T(8,128)S(1)} %get-tuple-element.281), channel_id=1, source_target_pairs={{0,192},{16,208},{32,224},{48,240},{64,256},{80,272},{96,288},{112... | collective-permute-start | bytes 98312 | tf_op jit(solution)/shard_map/ppermute | solution.py:70
  68.4 92.0 %copy-start.5 = (f32[16,512]{0,1:T(8,128)}, f32[16,512]{0,1:T(8,128)S(1)}, u32[]{:S(2)}) copy-start(f32[16,512]{0,1:T(8,128)S(1)} %copy.35) | copy-start | bytes 98308
  68.4 13.3 %copy-start.15 = (f32[16,512]{1,0:T(8,128)}, f32[16,512]{1,0:T(8,128)S(1)}, u32[]{:S(2)}) copy-start(f32[16,512]{1,0:T(8,128)S(1)} %collective-permute-done.11) | copy-start | bytes 98308
  68.4 13.3 %copy-start.17 = (f32[16,512]{1,0:T(8,128)}, f32[16,512]{1,0:T(8,128)S(1)}, u32[]{:S(2)}) copy-start(f32[16,512]{1,0:T(8,128)S(1)} %collective-permute-done.12) | copy-start | bytes 98308
  69.9 52.1 %collective-permute-start.16 = (f32[16,512]{1,0:T(8,128)S(1)}, f32[16,512]{1,0:T(8,128)S(1)}, u32[]{:S(2)}, u32[]{:S(2)}) collective-permute-start(f32[16,512]{1,0:T(8,128)S(1)} %get-tuple-element.285), channel_id=1, source_target_pairs={{0,256},{16,272},{32,288},{48,304},{64,320},{80,336},{96,352},{112... | collective-permute-start | bytes 98312 | tf_op jit(solution)/shard_map/ppermute | solution.py:70
  104.5 55.0 %collective-permute-start.14 = (f32[16,512]{1,0:T(8,128)S(1)}, f32[16,512]{1,0:T(8,128)S(1)}, u32[]{:S(2)}, u32[]{:S(2)}) collective-permute-start(f32[16,512]{1,0:T(8,128)S(1)} %get-tuple-element.285), channel_id=1, source_target_pairs={{0,512},{16,528},{32,544},{48,560},{64,576},{80,592},{96,608},{112... | collective-permute-start | bytes 98312 | tf_op jit(solution)/shard_map/ppermute | solution.py:70
  118.0 41.5 %collective-permute-start.17 = (f32[16,512]{1,0:T(8,128)S(1)}, f32[16,512]{1,0:T(8,128)S(1)}, u32[]{:S(2)}, u32[]{:S(2)}) collective-permute-start(f32[16,512]{1,0:T(8,128)S(1)} %get-tuple-element.284), channel_id=1, source_target_pairs={{256,0},{272,16},{288,32},{304,48},{320,64},{336,80},{352,96},{368... | collective-permute-start | bytes 98312 | tf_op jit(solution)/shard_map/ppermute | solution.py:71
  119.3 40.3 %collective-permute-start.15 = (f32[16,512]{1,0:T(8,128)S(1)}, f32[16,512]{1,0:T(8,128)S(1)}, u32[]{:S(2)}, u32[]{:S(2)}) collective-permute-start(f32[16,512]{1,0:T(8,128)S(1)} %get-tuple-element.284), channel_id=1, source_target_pairs={{512,0},{528,16},{544,32},{560,48},{576,64},{592,80},{608,96},{624... | collective-permute-start | bytes 98312 | tf_op jit(solution)/shard_map/ppermute | solution.py:71
  120.6 39.0 %collective-permute-start.13 = (f32[16,512]{1,0:T(8,128)S(1)}, f32[16,512]{1,0:T(8,128)S(1)}, u32[]{:S(2)}, u32[]{:S(2)}) collective-permute-start(f32[16,512]{1,0:T(8,128)S(1)} %get-tuple-element.284), channel_id=1, source_target_pairs={{768,0},{784,16},{800,32},{816,48},{832,64},{848,80},{864,96},{880... | collective-permute-start | bytes 98312 | tf_op jit(solution)/shard_map/ppermute | solution.py:71
  121.9 37.7 %collective-permute-start.6 = (f32[16,512]{1,0:T(8,128)S(1)}, f32[16,512]{1,0:T(8,128)S(1)}, u32[]{:S(2)}, u32[]{:S(2)}) collective-permute-start(f32[16,512]{1,0:T(8,128)S(1)} %get-tuple-element.285), channel_id=1, source_target_pairs={{0,768},{16,784},{32,800},{48,816},{64,832},{80,848},{96,864},{112... | collective-permute-start | bytes 98312 | tf_op jit(solution)/shard_map/ppermute | solution.py:70
  160.4 5.0 %copy-start.8 = (f32[16,512]{1,0:T(8,128)S(1)}, f32[16,512]{1,0:T(8,128)}, u32[]{:S(2)}) copy-start(f32[16,512]{1,0:T(8,128)} %copy-done.7) | copy-start | bytes 98308
  160.4 5.0 %copy-start.10 = (f32[16,512]{1,0:T(8,128)S(1)}, f32[16,512]{1,0:T(8,128)}, u32[]{:S(2)}) copy-start(f32[16,512]{1,0:T(8,128)} %copy-done.9) | copy-start | bytes 98308
  160.4 5.0 %copy-start.12 = (f32[16,512]{1,0:T(8,128)S(1)}, f32[16,512]{1,0:T(8,128)}, u32[]{:S(2)}) copy-start(f32[16,512]{1,0:T(8,128)} %copy-done.11) | copy-start | bytes 98308
  160.4 5.0 %copy-start.14 = (f32[16,512]{1,0:T(8,128)S(1)}, f32[16,512]{1,0:T(8,128)}, u32[]{:S(2)}) copy-start(f32[16,512]{1,0:T(8,128)} %copy-done.13) | copy-start | bytes 98308
  160.4 5.0 %copy-start.16 = (f32[16,512]{1,0:T(8,128)S(1)}, f32[16,512]{1,0:T(8,128)}, u32[]{:S(2)}) copy-start(f32[16,512]{1,0:T(8,128)} %copy-done.15) | copy-start | bytes 98308
  (12 other events, 31.6 us)

commit v3 on v2

--- a/solution.py
+++ b/solution.py
@@ -53,34 +53,35 @@
 
 def incoming_states(fwd_state, bwd_state, rates, length, cover):
     count = lax.axis_size("ctx")
-    radix = 4
-    fwd_sum, bwd_sum = fwd_state, bwd_state
+    place = lax.axis_index("ctx")
+    rounds = []
+    span = 1
+    while span < count:
+        rounds.append(span)
+        span *= 2
+    slots = {rounds[min(2, len(rounds) - 1)]: 0, rounds[min(4, len(rounds) - 1)]: 1}
+    cover = list(cover)
+    fwd_total, bwd_total = fwd_state, bwd_state
     fwd_in = jnp.zeros_like(fwd_state)
     bwd_in = jnp.zeros_like(bwd_state)
-    span = 1
-    while span < count:
-        last = span * radix >= count
-        fwd_next, bwd_next = fwd_sum, bwd_sum
-        for k in range(1, radix):
-            step = k * span
-            if step >= count:
-                break
-            ahead = [(i, i + step) for i in range(count - step)]
-            behind = [(i + step, i) for i in range(count - step)]
-            fwd_got = lax.ppermute(fwd_sum, "ctx", ahead)
-            bwd_got = lax.ppermute(bwd_sum, "ctx", behind)
-            if last:
-                fwd_got, bwd_got, cover = lax.optimization_barrier((fwd_got, bwd_got, cover))
-            into = jnp.exp(-rates * (length * (step - 1.0)))
-            fwd_in = fwd_in + into * fwd_got
-            bwd_in = bwd_in + into * bwd_got
-            if not last:
-                past = jnp.exp(-rates * (length * step))
-                fwd_next = fwd_next + past * fwd_got
-                bwd_next = bwd_next + past * bwd_got
-        fwd_sum, bwd_sum = fwd_next, bwd_next
-        span *= radix
-    return fwd_in, bwd_in, cover
+    for span in rounds:
+        got = lax.ppermute(
+            jnp.stack([fwd_total, bwd_total]), "ctx", [(i, i ^ span) for i in range(count)]
+        )
+        if span in slots:
+            got, cover[slots[span]] = lax.optimization_barrier((got, cover[slots[span]]))
+        fwd_got, bwd_got = got[0], got[1]
+        upper = (place // span) % 2 == 1
+        offset = (place % span).astype(jnp.float32)
+        fwd_in = fwd_in + jnp.where(upper, jnp.exp(-rates * (length * offset)), 0.0) * fwd_got
+        bwd_in = bwd_in + jnp.where(
+            upper, 0.0, jnp.exp(-rates * (length * (span - 1.0 - offset)))
+        ) * bwd_got
+        if 2 * span < count:
+            whole = jnp.exp(-rates * (length * span))
+            fwd_total = jnp.where(upper, whole * fwd_got + fwd_total, whole * fwd_total + fwd_got)
+            bwd_total = jnp.where(upper, bwd_got + whole * bwd_total, bwd_total + whole * bwd_got)
+    return fwd_in, bwd_in, tuple(cover)
 
 
 def per_device(query, key_proj, value, residues, rates, cotangent):

time: 177 us -> 122 us (0.69)
  the two profiles are of different devices: /device:TPU:10 before, /device:TPU:6 now
where the time goes in v3:
time: 122 us; the launch traced here: 121 us
  starting transfers between devices  41.7 us (34%)
  matrix products  28 us (23%)
  local copies, waits for them, and re-layouts  24.5 us (20%)
  other arithmetic  15.8 us (13%)
  waiting for transfers between devices  9.22 us (8%)
    ppermute x6, starting transfers between devices, incoming_states(): lax.ppermute(jnp.stack([fwd_total, bwd_total]), 'ctx', [(i, i ^ span) for...  41.7 us
    while x16, local copies, waits for them, and re-layouts  19.4 us
    dot_general x8, matrix products, advance(): jnp.dot(lower, lifted, precision=lax.Precision.HIGHEST)  16.1 us
    dot_general x2, matrix products, apply_incoming(): jnp.einsum('ikc,bkc->bic', after, weights, precision=lax.Precision.HIGHEST)  11.9 us
    ppermute x6, waiting for transfers between devices, incoming_states(): lax.ppermute(jnp.stack([fwd_total, bwd_total]), 'ctx', [(i, i ^ span) for...  9.22 us
    reduce_sum x8, other arithmetic, advance(): return (states[-1], jnp.sum(scaled[None] * states, axis=1))  6.17 us
    mul x8, other arithmetic, advance(): lifted = (rising * block[:, None, :]).reshape(BLOCK, order * width)  2.75 us
  transfers between devices with their start and end apart: 6, of which 4 were waited for; matrix products, arithmetic and copies ran while one was open for 38% of the time, Pallas kernels for 0%

profile of v3, /device:TPU:6, one launch (start us, length us, event | category | flops | bytes accessed | tf_op | source)
XLA Modules:
  0.0 121.0 jit_solution(17251985965613145010)
XLA Ops:
  3.2 2.0 %multiply_reduce_fusion.3 = (f32[16,16,512]{2,1,0:T(8,128)S(1)}, f32[16,16,512]{2,1,0:T(8,128)S(1)}) fusion(f32[16,16,512]{2,1,0:T(8,128)S(1)} %bitcast.230, f32[16,16,512]{2,1,0:T(8,128)S(1)} %multiply_exponential_fusion.6, f32[16,16,512]{2,1,0:T(8,128)S(1)} %bitcast.228), kind=kLoop, calls=%fused_computation.31 | loop fusion | flops 8126464 | bytes 2621440 | tf_op jit(solution)/shard_map/reduce_sum | solution.py:51
  5.4 1.9 %collective-permute-start = (f32[2,16,512]{2,1,0:T(8,128)S(1)}, f32[2,16,512]{2,1,0:T(8,128)S(1)}, u32[]{:S(2)}, u32[]{:S(2)}) collective-permute-start(f32[2,16,512]{2,1,0:T(8,128)S(1)} %pad_maximum_fusion), channel_id=1, source_target_pairs={{0,16},{16,0},{32,48},{48,32},{64,80},{80,64},{96,112},{112,96},{1... | collective-permute-start | bytes 196616 | tf_op jit(solution)/shard_map/ppermute | solution.py:68
  8.6 3.5 %collective-permute-start.1 = (f32[2,16,512]{2,1,0:T(8,128)S(1)}, f32[2,16,512]{2,1,0:T(8,128)S(1)}, u32[]{:S(2)}, u32[]{:S(2)}) collective-permute-start(f32[2,16,512]{2,1,0:T(8,128)S(1)} %pad_maximum_fusion.1), channel_id=1, source_target_pairs={{0,32},{16,48},{32,0},{48,16},{64,96},{80,112},{96,64},{112,80},{1... | collective-permute-start | bytes 196616 | tf_op jit(solution)/shard_map/ppermute | solution.py:68
  12.1 2.7 %collective-permute-done.1 = f32[2,16,512]{2,1,0:T(8,128)S(1)} collective-permute-done((f32[2,16,512]{2,1,0:T(8,128)S(1)}, f32[2,16,512]{2,1,0:T(8,128)S(1)}, u32[]{:S(2)}, u32[]{:S(2)}) %collective-permute-start.1) | collective-permute-done | bytes 65568 | tf_op jit(solution)/shard_map/ppermute | solution.py:68
  14.8 4.5 %collective-permute-start.2 = (f32[2,16,512]{2,1,0:T(8,128)S(1)}, f32[2,16,512]{2,1,0:T(8,128)S(1)}, u32[]{:S(2)}, u32[]{:S(2)}) collective-permute-start(f32[2,16,512]{2,1,0:T(8,128)S(1)} %pad_maximum_fusion.2), channel_id=1, source_target_pairs={{0,64},{16,80},{32,96},{48,112},{64,0},{80,16},{96,32},{112,48},{1... | collective-permute-start | bytes 196616 | tf_op jit(solution)/shard_map/ppermute | solution.py:68
  19.4 22.7 %while.28 = (s32[]{:T(128)}, f32[16,512]{1,0:T(8,128)S(1)}, f32[4,64,512]{2,1,0:T(8,128)S(1)}, f32[4,64,512]{2,1,0:T(8,128)S(1)}, f32[16,512]{1,0:T(8,128)S(1)},...) while((s32[]{:T(128)}, f32[16,512]{1,0:T(8,128)S(1)}, ...), condition=%wide.region_6.7_spmd.clone.clone, body=%wide.region_4.0_spmd.clone.clone.sunk | while | flops 406306816 | bytes 19956588 | solution.py:27
  19.8 1.2 %copy.49 = f32[8,8,16,512]{3,1,2,0:T(8,128)S(1)} copy(f32[8,8,16,512]{3,2,1,0:T(8,128)S(1)} %bitcast.222) | data formatting | bytes 4194304 | tf_op jit(solution)/shard_map/while
  21.0 2.0 %fusion.81 = f32[8192,64]{0,1:T(8,128)S(1)} fusion(f32[64,8192]{1,0:T(8,128)S(1)} %bitcast.223, f32[64]{0:T(128)S(1)} %get-tuple-element.424), kind=kOutput, calls=%fused_computation.13.clone.1 | convolution fusion | flops 402661376 | bytes 4194560 | tf_op jit(solution)/shard_map/while/body/eval_jaxpr/dot_general | solution.py:21
  25.5 1.2 %copy.49 = f32[8,8,16,512]{3,1,2,0:T(8,128)S(1)} copy(f32[8,8,16,512]{3,2,1,0:T(8,128)S(1)} %bitcast.222) | data formatting | bytes 4194304 | tf_op jit(solution)/shard_map/while
  26.7 2.0 %fusion.81 = f32[8192,64]{0,1:T(8,128)S(1)} fusion(f32[64,8192]{1,0:T(8,128)S(1)} %bitcast.223, f32[64]{0:T(128)S(1)} %get-tuple-element.424), kind=kOutput, calls=%fused_computation.13.clone.1 | convolution fusion | flops 402661376 | bytes 4194560 | tf_op jit(solution)/shard_map/while/body/eval_jaxpr/dot_general | solution.py:21
  28.7 1.2 copy.50
  31.1 1.2 %copy.49 = f32[8,8,16,512]{3,1,2,0:T(8,128)S(1)} copy(f32[8,8,16,512]{3,2,1,0:T(8,128)S(1)} %bitcast.222) | data formatting | bytes 4194304 | tf_op jit(solution)/shard_map/while
  32.4 2.0 %fusion.81 = f32[8192,64]{0,1:T(8,128)S(1)} fusion(f32[64,8192]{1,0:T(8,128)S(1)} %bitcast.223, f32[64]{0:T(128)S(1)} %get-tuple-element.424), kind=kOutput, calls=%fused_computation.13.clone.1 | convolution fusion | flops 402661376 | bytes 4194560 | tf_op jit(solution)/shard_map/while/body/eval_jaxpr/dot_general | solution.py:21
  36.8 1.2 %copy.49 = f32[8,8,16,512]{3,1,2,0:T(8,128)S(1)} copy(f32[8,8,16,512]{3,2,1,0:T(8,128)S(1)} %bitcast.222) | data formatting | bytes 4194304 | tf_op jit(solution)/shard_map/while
  38.0 2.0 %fusion.81 = f32[8192,64]{0,1:T(8,128)S(1)} fusion(f32[64,8192]{1,0:T(8,128)S(1)} %bitcast.223, f32[64]{0:T(128)S(1)} %get-tuple-element.424), kind=kOutput, calls=%fused_computation.13.clone.1 | convolution fusion | flops 402661376 | bytes 4194560 | tf_op jit(solution)/shard_map/while/body/eval_jaxpr/dot_general | solution.py:21
  42.2 5.9 %collective-permute-start.3 = (f32[2,16,512]{2,1,0:T(8,128)S(1)}, f32[2,16,512]{2,1,0:T(8,128)S(1)}, u32[]{:S(2)}, u32[]{:S(2)}) collective-permute-start(f32[2,16,512]{2,1,0:T(8,128)S(1)} %pad_maximum_fusion.3), channel_id=1, source_target_pairs={{0,128},{16,144},{32,160},{48,176},{64,192},{80,208},{96,224},{112... | collective-permute-start | bytes 196616 | tf_op jit(solution)/shard_map/ppermute | solution.py:68
  48.1 4.1 %collective-permute-done.3 = f32[2,16,512]{2,1,0:T(8,128)S(1)} collective-permute-done((f32[2,16,512]{2,1,0:T(8,128)S(1)}, f32[2,16,512]{2,1,0:T(8,128)S(1)}, u32[]{:S(2)}, u32[]{:S(2)}) %collective-permute-start.3) | collective-permute-done | bytes 65568 | tf_op jit(solution)/shard_map/ppermute | solution.py:68
  52.3 11.1 %collective-permute-start.4 = (f32[2,16,512]{2,1,0:T(8,128)S(1)}, f32[2,16,512]{2,1,0:T(8,128)S(1)}, u32[]{:S(2)}, u32[]{:S(2)}) collective-permute-start(f32[2,16,512]{2,1,0:T(8,128)S(1)} %pad_maximum_fusion.4), channel_id=1, source_target_pairs={{0,256},{16,272},{32,288},{48,304},{64,320},{80,336},{96,352},{112... | collective-permute-start | bytes 196616 | tf_op jit(solution)/shard_map/ppermute | solution.py:68
  63.4 22.7 %while.29 = (s32[]{:T(128)}, f32[16,512]{1,0:T(8,128)S(1)}, f32[4,64,512]{2,1,0:T(8,128)S(1)}, f32[4,64,512]{2,1,0:T(8,128)S(1)}, f32[16,512]{1,0:T(8,128)S(1)},...) while((s32[]{:T(128)}, f32[16,512]{1,0:T(8,128)S(1)}, ...), condition=%wide.region_9.10_spmd.clone.clone, body=%wide.region_7.9_spmd.clone.clone.sunk | while | flops 406306816 | bytes 19956588 | solution.py:27
  63.8 1.2 %copy.51 = f32[8,8,16,512]{3,1,2,0:T(8,128)S(1)} copy(f32[8,8,16,512]{3,2,1,0:T(8,128)S(1)} %bitcast.225) | data formatting | bytes 4194304 | tf_op jit(solution)/shard_map/while
  65.1 2.0 %fusion.84 = f32[8192,64]{0,1:T(8,128)S(1)} fusion(f32[64,8192]{1,0:T(8,128)S(1)} %bitcast.226, f32[64]{0:T(128)S(1)} %get-tuple-element.454), kind=kOutput, calls=%fused_computation.25.clone.1 | convolution fusion | flops 402661376 | bytes 4194560 | tf_op jit(solution)/shard_map/while/body/eval_jaxpr/dot_general | solution.py:21
  69.5 1.2 %copy.51 = f32[8,8,16,512]{3,1,2,0:T(8,128)S(1)} copy(f32[8,8,16,512]{3,2,1,0:T(8,128)S(1)} %bitcast.225) | data formatting | bytes 4194304 | tf_op jit(solution)/shard_map/while
  70.7 2.0 %fusion.84 = f32[8192,64]{0,1:T(8,128)S(1)} fusion(f32[64,8192]{1,0:T(8,128)S(1)} %bitcast.226, f32[64]{0:T(128)S(1)} %get-tuple-element.454), kind=kOutput, calls=%fused_computation.25.clone.1 | convolution fusion | flops 402661376 | bytes 4194560 | tf_op jit(solution)/shard_map/while/body/eval_jaxpr/dot_general | solution.py:21
  75.2 1.2 %copy.51 = f32[8,8,16,512]{3,1,2,0:T(8,128)S(1)} copy(f32[8,8,16,512]{3,2,1,0:T(8,128)S(1)} %bitcast.225) | data formatting | bytes 4194304 | tf_op jit(solution)/shard_map/while
  76.4 2.0 %fusion.84 = f32[8192,64]{0,1:T(8,128)S(1)} fusion(f32[64,8192]{1,0:T(8,128)S(1)} %bitcast.226, f32[64]{0:T(128)S(1)} %get-tuple-element.454), kind=kOutput, calls=%fused_computation.25.clone.1 | convolution fusion | flops 402661376 | bytes 4194560 | tf_op jit(solution)/shard_map/while/body/eval_jaxpr/dot_general | solution.py:21
  80.9 1.2 %copy.51 = f32[8,8,16,512]{3,1,2,0:T(8,128)S(1)} copy(f32[8,8,16,512]{3,2,1,0:T(8,128)S(1)} %bitcast.225) | data formatting | bytes 4194304 | tf_op jit(solution)/shard_map/while
  82.1 2.0 %fusion.84 = f32[8192,64]{0,1:T(8,128)S(1)} fusion(f32[64,8192]{1,0:T(8,128)S(1)} %bitcast.226, f32[64]{0:T(128)S(1)} %get-tuple-element.454), kind=kOutput, calls=%fused_computation.25.clone.1 | convolution fusion | flops 402661376 | bytes 4194560 | tf_op jit(solution)/shard_map/while/body/eval_jaxpr/dot_general | solution.py:21
  86.2 14.8 %collective-permute-start.5 = (f32[2,16,512]{2,1,0:T(8,128)S(1)}, f32[2,16,512]{2,1,0:T(8,128)S(1)}, u32[]{:S(2)}, u32[]{:S(2)}) collective-permute-start(f32[2,16,512]{2,1,0:T(8,128)S(1)} %pad_maximum_fusion.5), channel_id=1, source_target_pairs={{0,512},{16,528},{32,544},{48,560},{64,576},{80,592},{96,608},{112... | collective-permute-start | bytes 196616 | tf_op jit(solution)/shard_map/ppermute | solution.py:68
  101.0 2.2 %collective-permute-done.5 = f32[2,16,512]{2,1,0:T(8,128)S(1)} collective-permute-done((f32[2,16,512]{2,1,0:T(8,128)S(1)}, f32[2,16,512]{2,1,0:T(8,128)S(1)}, u32[]{:S(2)}, u32[]{:S(2)}) %collective-permute-start.5) | collective-permute-done | bytes 65568 | tf_op jit(solution)/shard_map/ppermute | solution.py:68
  104.0 5.5 %fusion.25 = f32[512,4,64]{2,1,0:T(4,128)S(1)} fusion(f32[64]{0:T(128)S(1)} %broadcast_add_fusion, f32[16,512]{0,1:T(8,128)} %copy.35, f32[16,512]{0,1:T(8,128)S(1)} %copy.36, f32[4]{0:T(128)S(1)} %convert_multiply_fusion.6), kind=kOutput, calls=%fused_computation.34 | convolution fusion | flops 25755648 | bytes 590096 | tf_op jit(solution)/shard_map/ikc,bkc->bic/dot_general | solution.py:40
  110.8 6.4 %fusion.24 = f32[512,4,64]{2,1,0:T(4,128)} fusion(f32[64]{0:T(128)S(1)} %broadcast_add_fusion, f32[16,512]{0,1:T(8,128)} %copy.35, f32[16,512]{0,1:T(8,128)S(1)} %copy.39, f32[4]{0:T(128)S(1)} %convert_multiply_fusion.6), kind=kOutput, calls=%fused_computation.33 | convolution fusion | flops 25755648 | bytes 590096 | tf_op jit(solution)/shard_map/ikc,bkc->bic/dot_general | solution.py:40
  117.2 1.5 %copy.40 = f32[512,4,64]{0,2,1:T(8,128)S(1)} copy(f32[512,4,64]{2,1,0:T(4,128)} %fusion.24) | data formatting | bytes 1048576 | tf_op jit(solution)/shard_map/ikc,bkc->bic/dot_general | solution.py:40
  (111 shorter events, 26.0 us)
Async XLA Ops:
  0.6 2.3 %copy-start.2 = (bf16[256,512]{1,0:T(8,128)(2,1)S(1)}, bf16[256,512]{1,0:T(8,128)(2,1)}, u32[]{:S(2)}) copy-start(bf16[256,512]{1,0:T(8,128)(2,1)} %param.10) | copy-start | bytes 786436
  0.6 2.3 %copy-start.1 = (bf16[256,512]{1,0:T(8,128)(2,1)S(1)}, bf16[256,512]{1,0:T(8,128)(2,1)}, u32[]{:S(2)}) copy-start(bf16[256,512]{1,0:T(8,128)(2,1)} %param.11) | copy-start | bytes 786436
  3.2 5.3 %copy-start = (f32[16,512]{1,0:T(8,128)S(1)}, f32[16,512]{1,0:T(8,128)}, u32[]{:S(2)}) copy-start(f32[16,512]{1,0:T(8,128)} %param.14) | copy-start | bytes 98308
  3.2 11.5 %copy-start.7 = (f32[16,512]{1,0:T(8,128)S(1)}, f32[16,512]{1,0:T(8,128)}, u32[]{:S(2)}) copy-start(f32[16,512]{1,0:T(8,128)} %param.13) | copy-start | bytes 98308
  5.4 3.1 %collective-permute-start = (f32[2,16,512]{2,1,0:T(8,128)S(1)}, f32[2,16,512]{2,1,0:T(8,128)S(1)}, u32[]{:S(2)}, u32[]{:S(2)}) collective-permute-start(f32[2,16,512]{2,1,0:T(8,128)S(1)} %pad_maximum_fusion), channel_id=1, source_target_pairs={{0,16},{16,0},{32,48},{48,32},{64,80},{80,64},{96,112},{112,96},{1... | collective-permute-start | bytes 196616 | tf_op jit(solution)/shard_map/ppermute | solution.py:68
  8.6 6.2 %collective-permute-start.1 = (f32[2,16,512]{2,1,0:T(8,128)S(1)}, f32[2,16,512]{2,1,0:T(8,128)S(1)}, u32[]{:S(2)}, u32[]{:S(2)}) collective-permute-start(f32[2,16,512]{2,1,0:T(8,128)S(1)} %pad_maximum_fusion.1), channel_id=1, source_target_pairs={{0,32},{16,48},{32,0},{48,16},{64,96},{80,112},{96,64},{112,80},{1... | collective-permute-start | bytes 196616 | tf_op jit(solution)/shard_map/ppermute | solution.py:68
  14.8 27.3 %collective-permute-start.2 = (f32[2,16,512]{2,1,0:T(8,128)S(1)}, f32[2,16,512]{2,1,0:T(8,128)S(1)}, u32[]{:S(2)}, u32[]{:S(2)}) collective-permute-start(f32[2,16,512]{2,1,0:T(8,128)S(1)} %pad_maximum_fusion.2), channel_id=1, source_target_pairs={{0,64},{16,80},{32,96},{48,112},{64,0},{80,16},{96,32},{112,48},{1... | collective-permute-start | bytes 196616 | tf_op jit(solution)/shard_map/ppermute | solution.py:68
  42.2 10.1 %collective-permute-start.3 = (f32[2,16,512]{2,1,0:T(8,128)S(1)}, f32[2,16,512]{2,1,0:T(8,128)S(1)}, u32[]{:S(2)}, u32[]{:S(2)}) collective-permute-start(f32[2,16,512]{2,1,0:T(8,128)S(1)} %pad_maximum_fusion.3), channel_id=1, source_target_pairs={{0,128},{16,144},{32,160},{48,176},{64,192},{80,208},{96,224},{112... | collective-permute-start | bytes 196616 | tf_op jit(solution)/shard_map/ppermute | solution.py:68
  52.3 33.9 %collective-permute-start.4 = (f32[2,16,512]{2,1,0:T(8,128)S(1)}, f32[2,16,512]{2,1,0:T(8,128)S(1)}, u32[]{:S(2)}, u32[]{:S(2)}) collective-permute-start(f32[2,16,512]{2,1,0:T(8,128)S(1)} %pad_maximum_fusion.4), channel_id=1, source_target_pairs={{0,256},{16,272},{32,288},{48,304},{64,320},{80,336},{96,352},{112... | collective-permute-start | bytes 196616 | tf_op jit(solution)/shard_map/ppermute | solution.py:68
  86.2 17.1 %copy-start.5 = (f32[2,16,512]{2,1,0:T(8,128)}, f32[2,16,512]{2,1,0:T(8,128)S(1)}, u32[]{:S(2)}) copy-start(f32[2,16,512]{2,1,0:T(8,128)S(1)} %collective-permute-done.4) | copy-start | bytes 196612
  86.2 17.0 %collective-permute-start.5 = (f32[2,16,512]{2,1,0:T(8,128)S(1)}, f32[2,16,512]{2,1,0:T(8,128)S(1)}, u32[]{:S(2)}, u32[]{:S(2)}) collective-permute-start(f32[2,16,512]{2,1,0:T(8,128)S(1)} %pad_maximum_fusion.5), channel_id=1, source_target_pairs={{0,512},{16,528},{32,544},{48,560},{64,576},{80,592},{96,608},{112... | collective-permute-start | bytes 196616 | tf_op jit(solution)/shard_map/ppermute | solution.py:68
  103.2 0.6 copy-start.6
  118.8 1.0 copy-start.3
  118.9 1.0 copy-start.4

commit v4 on v3

--- a/solution.py
+++ b/solution.py
@@ -1,33 +1,51 @@
 import jax
 import jax.numpy as jnp
 from jax import lax
+from jax.experimental import pallas as pl
 from jax.sharding import PartitionSpec as P
 
 BLOCK = 64
 
 
+def local_kernel(signal_ref, scaled_ref, rates_ref, out_ref):
+    length, width = signal_ref.shape
+    order = rates_ref.shape[0]
+    lags = lax.broadcasted_iota(jnp.int32, (BLOCK, width), 0).astype(jnp.float32)
+    lower = (
+        lax.broadcasted_iota(jnp.int32, (BLOCK, BLOCK), 0)
+        >= lax.broadcasted_iota(jnp.int32, (BLOCK, BLOCK), 1)
+    ).astype(jnp.float32)
+    out_ref[...] = jnp.zeros(out_ref.shape, jnp.float32)
+
+    def mode(m, carry):
+        rate = rates_ref[pl.ds(m, 1), :]
+        weight = scaled_ref[pl.ds(m, 1), :]
+        rising = jnp.exp(rate * lags)
+        falling = jnp.exp(-rate * lags)
+        step_decay = jnp.exp(-rate)
+        state = jnp.zeros((1, width), jnp.float32)
+        for b in range(length // BLOCK):
+            rows = pl.ds(b * BLOCK, BLOCK)
+            summed = jnp.dot(
+                lower,
+                rising * signal_ref[rows, :],
+                precision=lax.Precision.HIGHEST,
+                preferred_element_type=jnp.float32,
+            )
+            states = falling * (summed + step_decay * state)
+            out_ref[rows, :] += weight * states
+            state = states[BLOCK - 1 : BLOCK, :]
+        return carry
+
+    lax.fori_loop(0, order, mode, 0)
+
+
 def local_pass(signal, scaled, rates):
     length, width = signal.shape
-    count = length // BLOCK
-    order = rates.shape[0]
-    lags = jnp.arange(BLOCK).astype(jnp.float32)
-    rising = jnp.exp(rates[None] * lags[:, None, None])
-    falling = jnp.exp(-rates[None] * lags[:, None, None])
-    lower = (lags[:, None] >= lags[None, :]).astype(jnp.float32)
-    step_decay = jnp.exp(-rates)
-
-    def advance(state, block):
-        lifted = (rising * block[:, None, :]).reshape(BLOCK, order * width)
-        summed = jnp.dot(lower, lifted, precision=lax.Precision.HIGHEST).reshape(
-            BLOCK, order, width
-        )
-        states = falling * (summed + step_decay * state[None])
-        return (states[-1], jnp.sum(scaled[None] * states, axis=1))
-
-    final, pieces = lax.scan(
-        advance, jnp.zeros((order, width), jnp.float32), signal.reshape(count, BLOCK, width)
-    )
-    return (final, pieces)
+    pieces = pl.pallas_call(
+        local_kernel, out_shape=jax.ShapeDtypeStruct((length, width), jnp.float32)
+    )(signal, scaled, rates)
+    return pieces.reshape(length // BLOCK, BLOCK, width)
 
 
 def apply_incoming(pieces, incoming, scaled, rates):
@@ -94,8 +112,8 @@
     gated = lax.optimization_barrier((query_f * key_f).astype(jnp.bfloat16)).astype(jnp.float32)
     weighted = cot_f * value_f
     reversed_weighted = weighted[::-1]
-    _, fwd_pieces = local_pass(gated, scaled, rates)
-    _, bwd_pieces = local_pass(reversed_weighted, scaled, rates)
+    fwd_pieces = local_pass(gated, scaled, rates)
+    bwd_pieces = local_pass(reversed_weighted, scaled, rates)
     fwd_in, bwd_in, (fwd_pieces, bwd_pieces) = incoming_states(
         end_state(gated, rates),
         end_state(reversed_weighted, rates),

time: 122 us -> 98 us (0.80)
  Pallas kernels: 0 us -> 23 us
  matrix products: 28 us -> 9.01 us
  local copies, waits for them, and re-layouts: 24.5 us -> 5.78 us
  other arithmetic: 15.8 us -> 6.56 us
    pallas_call x0 -> x2, Pallas kernels: none -> 23 us  [local_pass(): pl.pallas_call(local_kernel, out_shape=jax.ShapeDtypeStruct((length, widt...]
    while x16 -> x0, local copies, waits for them, and re-layouts: 19.4 us -> none
    dot_general x8 -> x0, matrix products: 16.1 us -> none  [advance(): jnp.dot(lower, lifted, precision=lax.Precision.HIGHEST)]
    reduce_sum x8 -> x0, other arithmetic: 6.17 us -> none  [advance(): return (states[-1], jnp.sum(scaled[None] * states, axis=1))]
    dot_general x2, matrix products: 11.9 us -> 9.01 us  [apply_incoming(): jnp.einsum('ikc,bkc->bic', after, weights, precision=lax.Precision.HIGHEST)]
    mul x17 -> x0, other arithmetic: 2.88 us -> none  [the longest x8 2.75 us: advance(): lifted = (rising * block[:, None, :]).reshape(BLOCK, order * width)]
    unnamed x16 -> x34, local copies, waits for them, and re-layouts: 1.18 us -> 3.44 us
  transfers between devices with their start and end apart: 6 -> 6, of which waited for: 4 -> 4; matrix products, arithmetic and copies ran while one was open for 38% -> 0% of each run, Pallas kernels for 0% -> 24%
where the time goes in v4:
time: 98 us; the launch traced here: 97 us
  starting transfers between devices  41.5 us (42%)
  Pallas kernels  23 us (23%)
  waiting for transfers between devices  9.88 us (10%)
  matrix products  9.01 us (9%)
  other arithmetic  6.56 us (7%)
  local copies, waits for them, and re-layouts  5.78 us (6%)
  between operations  1.3 us (1%)
    ppermute x6, starting transfers between devices, incoming_states(): lax.ppermute(jnp.stack([fwd_total, bwd_total]), 'ctx', [(i, i ^ span) for...  41.5 us
    pallas_call x2, Pallas kernels, local_pass(): pl.pallas_call(local_kernel, out_shape=jax.ShapeDtypeStruct((length, widt...  23 us
    ppermute x6, waiting for transfers between devices, incoming_states(): lax.ppermute(jnp.stack([fwd_total, bwd_total]), 'ctx', [(i, i ^ span) for...  9.88 us
    dot_general x2, matrix products, apply_incoming(): jnp.einsum('ikc,bkc->bic', after, weights, precision=lax.Precision.HIGHEST)  9.01 us
    unnamed x34, local copies, waits for them, and re-layouts  3.44 us
    reduce_sum x2, other arithmetic, end_state(): return jnp.sum(outer * jnp.sum(inner[None] * rows, axis=1), axis=0)  2.14 us
  transfers between devices with their start and end apart: 6, of which 4 were waited for; matrix products, arithmetic and copies ran while one was open for 0% of the time, Pallas kernels for 24%

profile of v4, /device:TPU:6, one launch (start us, length us, event | category | flops | bytes accessed | tf_op | source)
XLA Modules:
  0.0 97.0 jit_solution(10353414445995193011)
XLA Ops:
  0.7 0.8 neg.5
  1.5 1.1 %fusion.10 = bf16[256,512]{1,0:T(8,128)(2,1)S(1)} fusion(bf16[256,512]{1,0:T(8,128)(2,1)} %param.7, bf16[256,512]{1,0:T(8,128)(2,1)} %param.6), kind=kLoop, calls=%fused_computation.20 | loop fusion | flops 524288 | bytes 786432 | tf_op jit(solution)/shard_map/convert_element_type | solution.py:112
  2.8 0.3 rev.6.signal_ref
  3.1 0.1 multiply_exponential_fusion.6
  3.2 0.3 copy-done.1
  3.5 1.9 %multiply_reduce_fusion.1 = (f32[16,16,512]{2,1,0:T(8,128)S(1)}, f32[16,16,512]{2,1,0:T(8,128)S(1)}) fusion(f32[16,16,512]{2,1,0:T(8,128)S(1)} %bitcast.163, f32[16,16,512]{2,1,0:T(8,128)S(1)} %multiply_exponential_fusion.6, f32[16,16,512]{2,1,0:T(8,128)S(1)} %bitcast.162), kind=kLoop, calls=%fused_computation.1 | loop fusion | flops 8126464 | bytes 2621440 | tf_op jit(solution)/shard_map/reduce_sum | solution.py:69
  5.5 0.2 multiply_reduce_fusion.3
  5.7 1.9 %collective-permute-start = (f32[2,16,512]{2,1,0:T(8,128)S(1)}, f32[2,16,512]{2,1,0:T(8,128)S(1)}, u32[]{:S(2)}, u32[]{:S(2)}) collective-permute-start(f32[2,16,512]{2,1,0:T(8,128)S(1)} %pad_maximum_fusion), channel_id=1, source_target_pairs={{0,16},{16,0},{32,48},{48,32},{64,80},{80,64},{96,112},{112,96},{1... | collective-permute-start | bytes 196616 | tf_op jit(solution)/shard_map/ppermute | solution.py:86
  7.6 1.2 %collective-permute-done = f32[2,16,512]{2,1,0:T(8,128)S(1)} collective-permute-done((f32[2,16,512]{2,1,0:T(8,128)S(1)}, f32[2,16,512]{2,1,0:T(8,128)S(1)}, u32[]{:S(2)}, u32[]{:S(2)}) %collective-permute-start) | collective-permute-done | bytes 65568 | tf_op jit(solution)/shard_map/ppermute | solution.py:86
  8.9 3.5 %collective-permute-start.1 = (f32[2,16,512]{2,1,0:T(8,128)S(1)}, f32[2,16,512]{2,1,0:T(8,128)S(1)}, u32[]{:S(2)}, u32[]{:S(2)}) collective-permute-start(f32[2,16,512]{2,1,0:T(8,128)S(1)} %pad_maximum_fusion.1), channel_id=1, source_target_pairs={{0,32},{16,48},{32,0},{48,16},{64,96},{80,112},{96,64},{112,80},{1... | collective-permute-start | bytes 196616 | tf_op jit(solution)/shard_map/ppermute | solution.py:86
  12.4 2.6 %collective-permute-done.1 = f32[2,16,512]{2,1,0:T(8,128)S(1)} collective-permute-done((f32[2,16,512]{2,1,0:T(8,128)S(1)}, f32[2,16,512]{2,1,0:T(8,128)S(1)}, u32[]{:S(2)}, u32[]{:S(2)}) %collective-permute-start.1) | collective-permute-done | bytes 65568 | tf_op jit(solution)/shard_map/ppermute | solution.py:86
  15.0 0.7 add_select_fusion.3
  15.7 4.5 %collective-permute-start.2 = (f32[2,16,512]{2,1,0:T(8,128)S(1)}, f32[2,16,512]{2,1,0:T(8,128)S(1)}, u32[]{:S(2)}, u32[]{:S(2)}) collective-permute-start(f32[2,16,512]{2,1,0:T(8,128)S(1)} %pad_maximum_fusion.2), channel_id=1, source_target_pairs={{0,64},{16,80},{32,96},{48,112},{64,0},{80,16},{96,32},{112,48},{1... | collective-permute-start | bytes 196616 | tf_op jit(solution)/shard_map/ppermute | solution.py:86
  20.3 11.5 %shard_map.93 = f32[256,512]{1,0:T(8,128)} custom-call(f32[256,512]{1,0:T(8,128)} %copy-done.1, f32[16,512]{1,0:T(8,128)} %get-tuple-element.30.scaled_ref, f32[16,512]{1,0:T(8,128)} %rates_ref.3), custom_call_target="tpu_custom_call" | custom-call | tf_op jit(solution)/shard_map/pallas_call | solution.py:45
  31.8 5.9 %collective-permute-start.3 = (f32[2,16,512]{2,1,0:T(8,128)S(1)}, f32[2,16,512]{2,1,0:T(8,128)S(1)}, u32[]{:S(2)}, u32[]{:S(2)}) collective-permute-start(f32[2,16,512]{2,1,0:T(8,128)S(1)} %pad_maximum_fusion.3), channel_id=1, source_target_pairs={{0,128},{16,144},{32,160},{48,176},{64,192},{80,208},{96,224},{112... | collective-permute-start | bytes 196616 | tf_op jit(solution)/shard_map/ppermute | solution.py:86
  37.8 0.1 copy.26
  38.1 3.8 %collective-permute-done.3 = f32[2,16,512]{2,1,0:T(8,128)S(1)} collective-permute-done((f32[2,16,512]{2,1,0:T(8,128)S(1)}, f32[2,16,512]{2,1,0:T(8,128)S(1)}, u32[]{:S(2)}, u32[]{:S(2)}) %collective-permute-start.3) | collective-permute-done | bytes 65568 | tf_op jit(solution)/shard_map/ppermute | solution.py:86
  41.9 10.9 %collective-permute-start.4 = (f32[2,16,512]{2,1,0:T(8,128)S(1)}, f32[2,16,512]{2,1,0:T(8,128)S(1)}, u32[]{:S(2)}, u32[]{:S(2)}) collective-permute-start(f32[2,16,512]{2,1,0:T(8,128)S(1)} %pad_maximum_fusion.4), channel_id=1, source_target_pairs={{0,256},{16,272},{32,288},{48,304},{64,320},{80,336},{96,352},{112... | collective-permute-start | bytes 196616 | tf_op jit(solution)/shard_map/ppermute | solution.py:86
  52.8 11.5 %shard_map.94 = f32[256,512]{1,0:T(8,128)} custom-call(f32[256,512]{1,0:T(8,128)} %copy-done, f32[16,512]{1,0:T(8,128)} %get-tuple-element.30.scaled_ref, f32[16,512]{1,0:T(8,128)} %rates_ref.3), custom_call_target="tpu_custom_call" | custom-call | tf_op jit(solution)/shard_map/pallas_call | solution.py:45
  64.4 14.7 %collective-permute-start.5 = (f32[2,16,512]{2,1,0:T(8,128)S(1)}, f32[2,16,512]{2,1,0:T(8,128)S(1)}, u32[]{:S(2)}, u32[]{:S(2)}) collective-permute-start(f32[2,16,512]{2,1,0:T(8,128)S(1)} %pad_maximum_fusion.5), channel_id=1, source_target_pairs={{0,512},{16,528},{32,544},{48,560},{64,576},{80,592},{96,608},{112... | collective-permute-start | bytes 196616 | tf_op jit(solution)/shard_map/ppermute | solution.py:86
  79.1 2.3 %collective-permute-done.5 = f32[2,16,512]{2,1,0:T(8,128)S(1)} collective-permute-done((f32[2,16,512]{2,1,0:T(8,128)S(1)}, f32[2,16,512]{2,1,0:T(8,128)S(1)}, u32[]{:S(2)}, u32[]{:S(2)}) %collective-permute-start.5) | collective-permute-done | bytes 65568 | tf_op jit(solution)/shard_map/ppermute | solution.py:86
  81.4 0.8 copy.27
  82.5 4.5 %fusion = f32[512,4,64]{2,1,0:T(4,128)S(1)} fusion(f32[64]{0:T(128)S(1)} %convert_add_fusion, f32[16,512]{0,1:T(8,128)S(1)} %copy.26, f32[16,512]{0,1:T(8,128)S(1)} %copy.30, f32[4]{0:T(128)S(1)} %convert_multiply_fusion.6), kind=kOutput, calls=%fused_computation.3 | convolution fusion | flops 25755648 | bytes 590096 | tf_op jit(solution)/shard_map/ikc,bkc->bic/dot_general | solution.py:58
  87.0 0.3 copy.31
  87.3 0.7 copy-done.6
  88.1 0.3 rev.7
  88.4 0.6 copy-done.14
  89.1 4.5 %fusion.1 = f32[512,4,64]{2,1,0:T(4,128)S(1)} fusion(f32[64]{0:T(128)S(1)} %convert_add_fusion, f32[16,512]{0,1:T(8,128)S(1)} %copy-done.14, f32[16,512]{0,1:T(8,128)S(1)} %copy-done.15, f32[4]{0:T(128)S(1)} %convert_multiply_fusion.6), kind=kOutput, calls=%fused_computation.4 | convolution fusion | flops 25755648 | bytes 590096 | tf_op jit(solution)/shard_map/ikc,bkc->bic/dot_general | solution.py:58
  93.7 0.3 copy.29
  94.0 0.7 copy-done.5
  94.8 0.9 copy-done.7
  95.8 1.2 %fusion.9 = (bf16[256,512]{1,0:T(8,128)(2,1)}, bf16[256,512]{1,0:T(8,128)(2,1)}, bf16[256,512]{1,0:T(8,128)(2,1)}, bf16[256,512]{1,0:T(8,128)(2,1)}) fusion(f32[256,512]{1,0:T(8,128)S(1)} %rev.7, bf16[256,512]{1,0:T(8,128)(2,1)S(1)} %copy-done.8, bf16[256,512]{1,0:T(8,128)(2,1)S(1)} %copy-done.7, f32[4,64,512]{2,1,0:T(8,128)S(1)} %bitcast_add_fusion.1, ...), kind=kLoop, calls=%fused_computation.19 | loop fusion | flops 1572864 | bytes 3145728 | tf_op jit(solution)/shard_map/convert_element_type | solution.py:129
  (52 shorter events, 1.0 us)
Async XLA Ops:
  0.6 2.0 %copy-start.9 = (bf16[256,512]{1,0:T(8,128)(2,1)S(1)}, bf16[256,512]{1,0:T(8,128)(2,1)}, u32[]{:S(2)}) copy-start(bf16[256,512]{1,0:T(8,128)(2,1)} %param.11) | copy-start | bytes 786436
  0.6 2.0 %copy-start.10 = (bf16[256,512]{1,0:T(8,128)(2,1)S(1)}, bf16[256,512]{1,0:T(8,128)(2,1)}, u32[]{:S(2)}) copy-start(bf16[256,512]{1,0:T(8,128)(2,1)} %param.8) | copy-start | bytes 786436
  2.7 0.8 copy-start.1
  3.0 2.4 %copy-start = (f32[256,512]{1,0:T(8,128)}, f32[256,512]{1,0:T(8,128)S(1)}, u32[]{:S(2)}) copy-start(f32[256,512]{1,0:T(8,128)S(1)} %rev.6.signal_ref) | copy-start | bytes 1572868
  5.4 3.4 %copy-start.2 = (f32[16,512]{1,0:T(8,128)S(1)}, f32[16,512]{1,0:T(8,128)}, u32[]{:S(2)}) copy-start(f32[16,512]{1,0:T(8,128)} %rates_ref.3) | copy-start | bytes 98308
  5.5 9.6 %copy-start.16 = (f32[16,512]{1,0:T(8,128)S(1)}, f32[16,512]{1,0:T(8,128)}, u32[]{:S(2)}) copy-start(f32[16,512]{1,0:T(8,128)} %param.9) | copy-start | bytes 98308
  5.7 26.0 %copy-start.3 = (f32[16,512]{1,0:T(8,128)S(1)}, f32[16,512]{1,0:T(8,128)}, u32[]{:S(2)}) copy-start(f32[16,512]{1,0:T(8,128)} %rates_ref.3) | copy-start | bytes 98308
  5.7 3.1 %collective-permute-start = (f32[2,16,512]{2,1,0:T(8,128)S(1)}, f32[2,16,512]{2,1,0:T(8,128)S(1)}, u32[]{:S(2)}, u32[]{:S(2)}) collective-permute-start(f32[2,16,512]{2,1,0:T(8,128)S(1)} %pad_maximum_fusion), channel_id=1, source_target_pairs={{0,16},{16,0},{32,48},{48,32},{64,80},{80,64},{96,112},{112,96},{1... | collective-permute-start | bytes 196616 | tf_op jit(solution)/shard_map/ppermute | solution.py:86
  8.9 6.2 %collective-permute-start.1 = (f32[2,16,512]{2,1,0:T(8,128)S(1)}, f32[2,16,512]{2,1,0:T(8,128)S(1)}, u32[]{:S(2)}, u32[]{:S(2)}) collective-permute-start(f32[2,16,512]{2,1,0:T(8,128)S(1)} %pad_maximum_fusion.1), channel_id=1, source_target_pairs={{0,32},{16,48},{32,0},{48,16},{64,96},{80,112},{96,64},{112,80},{1... | collective-permute-start | bytes 196616 | tf_op jit(solution)/shard_map/ppermute | solution.py:86
  15.7 16.0 %collective-permute-start.2 = (f32[2,16,512]{2,1,0:T(8,128)S(1)}, f32[2,16,512]{2,1,0:T(8,128)S(1)}, u32[]{:S(2)}, u32[]{:S(2)}) collective-permute-start(f32[2,16,512]{2,1,0:T(8,128)S(1)} %pad_maximum_fusion.2), channel_id=1, source_target_pairs={{0,64},{16,80},{32,96},{48,112},{64,0},{80,16},{96,32},{112,48},{1... | collective-permute-start | bytes 196616 | tf_op jit(solution)/shard_map/ppermute | solution.py:86
  31.8 32.6 %copy-start.4 = (f32[16,512]{1,0:T(8,128)S(1)}, f32[16,512]{1,0:T(8,128)}, u32[]{:S(2)}) copy-start(f32[16,512]{1,0:T(8,128)} %rates_ref.3) | copy-start | bytes 98308
  31.8 10.1 %collective-permute-start.3 = (f32[2,16,512]{2,1,0:T(8,128)S(1)}, f32[2,16,512]{2,1,0:T(8,128)S(1)}, u32[]{:S(2)}, u32[]{:S(2)}) collective-permute-start(f32[2,16,512]{2,1,0:T(8,128)S(1)} %pad_maximum_fusion.3), channel_id=1, source_target_pairs={{0,128},{16,144},{32,160},{48,176},{64,192},{80,208},{96,224},{112... | collective-permute-start | bytes 196616 | tf_op jit(solution)/shard_map/ppermute | solution.py:86
  38.0 44.5 %copy-start.13 = (f32[16,512]{0,1:T(8,128)}, f32[16,512]{0,1:T(8,128)S(1)}, u32[]{:S(2)}) copy-start(f32[16,512]{0,1:T(8,128)S(1)} %copy.26) | copy-start | bytes 98308
  38.0 43.4 %copy-start.12 = (f32[16,512]{1,0:T(8,128)S(1)}, f32[16,512]{1,0:T(8,128)}, u32[]{:S(2)}) copy-start(f32[16,512]{1,0:T(8,128)} %get-tuple-element.30.scaled_ref) | copy-start | bytes 98308
  41.9 22.4 %collective-permute-start.4 = (f32[2,16,512]{2,1,0:T(8,128)S(1)}, f32[2,16,512]{2,1,0:T(8,128)S(1)}, u32[]{:S(2)}, u32[]{:S(2)}) collective-permute-start(f32[2,16,512]{2,1,0:T(8,128)S(1)} %pad_maximum_fusion.4), channel_id=1, source_target_pairs={{0,256},{16,272},{32,288},{48,304},{64,320},{80,336},{96,352},{112... | collective-permute-start | bytes 196616 | tf_op jit(solution)/shard_map/ppermute | solution.py:86
  64.4 17.0 %collective-permute-start.5 = (f32[2,16,512]{2,1,0:T(8,128)S(1)}, f32[2,16,512]{2,1,0:T(8,128)S(1)}, u32[]{:S(2)}, u32[]{:S(2)}) collective-permute-start(f32[2,16,512]{2,1,0:T(8,128)S(1)} %pad_maximum_fusion.5), channel_id=1, source_target_pairs={{0,512},{16,528},{32,544},{48,560},{64,576},{80,592},{96,608},{112... | collective-permute-start | bytes 196616 | tf_op jit(solution)/shard_map/ppermute | solution.py:86
  87.0 1.0 %copy-start.6 = (f32[256,512]{1,0:T(8,128)S(1)}, f32[256,512]{1,0:T(8,128)}, u32[]{:S(2)}) copy-start(f32[256,512]{1,0:T(8,128)} %shard_map.94) | copy-start | bytes 1572868
  88.1 1.0 copy-start.14
  88.1 1.0 %copy-start.15 = (f32[16,512]{0,1:T(8,128)S(1)}, f32[16,512]{0,1:T(8,128)}, u32[]{:S(2)}) copy-start(f32[16,512]{0,1:T(8,128)} %copy.27) | copy-start | bytes 98308
  93.6 1.0 %copy-start.5 = (f32[256,512]{1,0:T(8,128)S(1)}, f32[256,512]{1,0:T(8,128)}, u32[]{:S(2)}) copy-start(f32[256,512]{1,0:T(8,128)} %shard_map.93) | copy-start | bytes 1572868
  94.7 0.9 copy-start.7
  94.7 1.0 %copy-start.8 = (bf16[256,512]{1,0:T(8,128)(2,1)S(1)}, bf16[256,512]{1,0:T(8,128)(2,1)}, u32[]{:S(2)}) copy-start(bf16[256,512]{1,0:T(8,128)(2,1)} %param.6) | copy-start | bytes 786436
  94.7 1.1 %copy-start.11 = (bf16[256,512]{1,0:T(8,128)(2,1)S(1)}, bf16[256,512]{1,0:T(8,128)(2,1)}, u32[]{:S(2)}) copy-start(bf16[256,512]{1,0:T(8,128)(2,1)} %param.8) | copy-start | bytes 786436

commit v5 on v4

--- a/solution.py
+++ b/solution.py
@@ -48,15 +48,30 @@
     return pieces.reshape(length // BLOCK, BLOCK, width)
 
 
+def carried_kernel(weights_ref, rates_ref, out_ref):
+    length, width = out_ref.shape
+    order = rates_ref.shape[0]
+    lags = lax.broadcasted_iota(jnp.int32, (BLOCK, width), 0).astype(jnp.float32) + 1.0
+    out_ref[...] = jnp.zeros(out_ref.shape, jnp.float32)
+
+    def mode(m, carry):
+        rate = rates_ref[pl.ds(m, 1), :]
+        weight = weights_ref[pl.ds(m, 1), :]
+        after = jnp.exp(-rate * lags)
+        for b in range(length // BLOCK):
+            rows = pl.ds(b * BLOCK, BLOCK)
+            out_ref[rows, :] += after * (weight * jnp.exp(-rate * float(b * BLOCK)))
+        return carry
+
+    lax.fori_loop(0, order, mode, 0)
+
+
 def apply_incoming(pieces, incoming, scaled, rates):
-    count = pieces.shape[0]
-    lags = jnp.arange(BLOCK).astype(jnp.float32)
-    after = jnp.exp(-rates[None] * (lags + 1.0)[:, None, None])
-    block_index = jnp.arange(count).astype(jnp.float32)
-    block_start = jnp.exp(-rates[None] * (BLOCK * block_index)[:, None, None])
-    weights = block_start * (scaled * incoming)[None]
-    extra = jnp.einsum("ikc,bkc->bic", after, weights, precision=lax.Precision.HIGHEST)
-    return (pieces + extra).reshape(count * BLOCK, pieces.shape[2])
+    count, _, width = pieces.shape
+    extra = pl.pallas_call(
+        carried_kernel, out_shape=jax.ShapeDtypeStruct((count * BLOCK, width), jnp.float32)
+    )(scaled * incoming, rates)
+    return pieces.reshape(count * BLOCK, width) + extra
 
 
 def end_state(signal, rates):

time: 98 us -> 93.3 us (0.952)
  matrix products: 9.01 us -> 0 us
  Pallas kernels: 23 us -> 28.3 us
  local copies, waits for them, and re-layouts: 5.78 us -> 2.03 us
  other arithmetic: 6.56 us -> 9.01 us
    dot_general x2 -> x0, matrix products: 9.01 us -> none  [apply_incoming(): jnp.einsum('ikc,bkc->bic', after, weights, precision=lax.Precision.HIGHEST)]
    pallas_call x0 -> x2, Pallas kernels: none -> 5.34 us  [apply_incoming(): pl.pallas_call(carried_kernel, out_shape=jax.ShapeDtypeStruct((count * BL...]
    unnamed x34 -> x28, local copies, waits for them, and re-layouts: 3.44 us -> 1.46 us
    mul x3 -> x2, other arithmetic: 0.1 us -> 1.33 us  [apply_incoming(): scaled * incoming]
    convert_element_type x1, other arithmetic: 1.16 us -> 2.24 us  [per_device(): grad_key = (back * query_f).astype(jnp.bfloat16)]
  transfers between devices with their start and end apart: 6 -> 6, of which waited for: 4 -> 4; matrix products, arithmetic and copies ran while one was open for 0% -> 0% of each run, Pallas kernels for 24% -> 25%
where the time goes in v5:
time: 93.3 us; the launch traced here: 92.2 us
  starting transfers between devices  41.4 us (44%)
  Pallas kernels  28.3 us (30%)
  waiting for transfers between devices  10.3 us (11%)
  other arithmetic  9.01 us (10%)
  local copies, waits for them, and re-layouts  2.03 us (2%)
  between operations  1.16 us (1%)
    ppermute x6, starting transfers between devices, incoming_states(): lax.ppermute(jnp.stack([fwd_total, bwd_total]), 'ctx', [(i, i ^ span) for...  41.4 us
    pallas_call x2, Pallas kernels, local_pass(): pl.pallas_call(local_kernel, out_shape=jax.ShapeDtypeStruct((length, widt...  23 us
    ppermute x6, waiting for transfers between devices, incoming_states(): lax.ppermute(jnp.stack([fwd_total, bwd_total]), 'ctx', [(i, i ^ span) for...  10.3 us
    pallas_call x2, Pallas kernels, apply_incoming(): pl.pallas_call(carried_kernel, out_shape=jax.ShapeDtypeStruct((count * BL...  5.34 us
    convert_element_type x1, other arithmetic, per_device(): grad_key = (back * query_f).astype(jnp.bfloat16)  2.24 us
    reduce_sum x2, other arithmetic, end_state(): return jnp.sum(outer * jnp.sum(inner[None] * rows, axis=1), axis=0)  2.14 us
  transfers between devices with their start and end apart: 6, of which 4 were waited for; matrix products, arithmetic and copies ran while one was open for 0% of the time, Pallas kernels for 25%

profile of v5, /device:TPU:6, one launch (start us, length us, event | category | flops | bytes accessed | tf_op | source)
XLA Modules:
  0.0 92.2 jit_solution(1325924096255576671)
XLA Ops:
  0.7 1.1 %fusion.2 = bf16[256,512]{1,0:T(8,128)(2,1)S(1)} fusion(bf16[256,512]{1,0:T(8,128)(2,1)} %param.7, bf16[256,512]{1,0:T(8,128)(2,1)} %param.6), kind=kLoop, calls=%fused_computation.10 | loop fusion | flops 524288 | bytes 786432 | tf_op jit(solution)/shard_map/convert_element_type | solution.py:127
  1.8 0.1 convert_element_type.66.signal_ref
  1.8 0.7 copy-done
  2.5 0.2 copy-done.10
  2.7 0.1 copy-done.11
  2.8 0.1 convert_multiply_fusion.1
  2.9 0.3 rev.6.signal_ref
  3.2 0.1 multiply_exponential_fusion
  3.3 0.0 copy-done.5
  3.3 2.0 %multiply_reduce_fusion.1 = (f32[16,16,512]{2,1,0:T(8,128)S(1)}, f32[16,16,512]{2,1,0:T(8,128)S(1)}) fusion(f32[16,16,512]{2,1,0:T(8,128)S(1)} %bitcast.163, f32[16,16,512]{2,1,0:T(8,128)S(1)} %multiply_exponential_fusion, f32[16,16,512]{2,1,0:T(8,128)S(1)} %bitcast.162), kind=kLoop, calls=%fused_computation.1 | loop fusion | flops 8126464 | bytes 2621440 | tf_op jit(solution)/shard_map/reduce_sum | solution.py:84
  5.3 0.2 multiply_reduce_fusion.3
  5.5 1.9 %collective-permute-start = (f32[2,16,512]{2,1,0:T(8,128)S(1)}, f32[2,16,512]{2,1,0:T(8,128)S(1)}, u32[]{:S(2)}, u32[]{:S(2)}) collective-permute-start(f32[2,16,512]{2,1,0:T(8,128)S(1)} %pad_maximum_fusion), channel_id=1, source_target_pairs={{0,16},{16,0},{32,48},{48,32},{64,80},{80,64},{96,112},{112,96},{1... | collective-permute-start | bytes 196616 | tf_op jit(solution)/shard_map/ppermute | solution.py:101
  7.5 1.2 %collective-permute-done = f32[2,16,512]{2,1,0:T(8,128)S(1)} collective-permute-done((f32[2,16,512]{2,1,0:T(8,128)S(1)}, f32[2,16,512]{2,1,0:T(8,128)S(1)}, u32[]{:S(2)}, u32[]{:S(2)}) %collective-permute-start) | collective-permute-done | bytes 65568 | tf_op jit(solution)/shard_map/ppermute | solution.py:101
  8.7 3.5 %collective-permute-start.1 = (f32[2,16,512]{2,1,0:T(8,128)S(1)}, f32[2,16,512]{2,1,0:T(8,128)S(1)}, u32[]{:S(2)}, u32[]{:S(2)}) collective-permute-start(f32[2,16,512]{2,1,0:T(8,128)S(1)} %pad_maximum_fusion.1), channel_id=1, source_target_pairs={{0,32},{16,48},{32,0},{48,16},{64,96},{80,112},{96,64},{112,80},{1... | collective-permute-start | bytes 196616 | tf_op jit(solution)/shard_map/ppermute | solution.py:101
  12.3 2.6 %collective-permute-done.1 = f32[2,16,512]{2,1,0:T(8,128)S(1)} collective-permute-done((f32[2,16,512]{2,1,0:T(8,128)S(1)}, f32[2,16,512]{2,1,0:T(8,128)S(1)}, u32[]{:S(2)}, u32[]{:S(2)}) %collective-permute-start.1) | collective-permute-done | bytes 65568 | tf_op jit(solution)/shard_map/ppermute | solution.py:101
  14.9 0.7 add_select_fusion.3
  15.6 4.5 %collective-permute-start.2 = (f32[2,16,512]{2,1,0:T(8,128)S(1)}, f32[2,16,512]{2,1,0:T(8,128)S(1)}, u32[]{:S(2)}, u32[]{:S(2)}) collective-permute-start(f32[2,16,512]{2,1,0:T(8,128)S(1)} %pad_maximum_fusion.2), channel_id=1, source_target_pairs={{0,64},{16,80},{32,96},{48,112},{64,0},{80,16},{96,32},{112,48},{1... | collective-permute-start | bytes 196616 | tf_op jit(solution)/shard_map/ppermute | solution.py:101
  20.1 11.5 %shard_map.93 = f32[256,512]{1,0:T(8,128)} custom-call(f32[256,512]{1,0:T(8,128)} %copy-done.5, f32[16,512]{1,0:T(8,128)} %get-tuple-element.30.scaled_ref, f32[16,512]{1,0:T(8,128)} %rates_ref.7), custom_call_target="tpu_custom_call" | custom-call | tf_op jit(solution)/shard_map/pallas_call | solution.py:45
  31.6 5.9 %collective-permute-start.3 = (f32[2,16,512]{2,1,0:T(8,128)S(1)}, f32[2,16,512]{2,1,0:T(8,128)S(1)}, u32[]{:S(2)}, u32[]{:S(2)}) collective-permute-start(f32[2,16,512]{2,1,0:T(8,128)S(1)} %pad_maximum_fusion.3), channel_id=1, source_target_pairs={{0,128},{16,144},{32,160},{48,176},{64,192},{80,208},{96,224},{112... | collective-permute-start | bytes 196616 | tf_op jit(solution)/shard_map/ppermute | solution.py:101
  37.6 4.1 %collective-permute-done.3 = f32[2,16,512]{2,1,0:T(8,128)S(1)} collective-permute-done((f32[2,16,512]{2,1,0:T(8,128)S(1)}, f32[2,16,512]{2,1,0:T(8,128)S(1)}, u32[]{:S(2)}, u32[]{:S(2)}) %collective-permute-start.3) | collective-permute-done | bytes 65568 | tf_op jit(solution)/shard_map/ppermute | solution.py:101
  41.7 10.9 %collective-permute-start.4 = (f32[2,16,512]{2,1,0:T(8,128)S(1)}, f32[2,16,512]{2,1,0:T(8,128)S(1)}, u32[]{:S(2)}, u32[]{:S(2)}) collective-permute-start(f32[2,16,512]{2,1,0:T(8,128)S(1)} %pad_maximum_fusion.4), channel_id=1, source_target_pairs={{0,256},{16,272},{32,288},{48,304},{64,320},{80,336},{96,352},{112... | collective-permute-start | bytes 196616 | tf_op jit(solution)/shard_map/ppermute | solution.py:101
  52.7 11.5 %shard_map.94 = f32[256,512]{1,0:T(8,128)} custom-call(f32[256,512]{1,0:T(8,128)} %copy-done.4, f32[16,512]{1,0:T(8,128)} %get-tuple-element.30.scaled_ref, f32[16,512]{1,0:T(8,128)} %rates_ref.7), custom_call_target="tpu_custom_call" | custom-call | tf_op jit(solution)/shard_map/pallas_call | solution.py:45
  64.3 14.7 %collective-permute-start.5 = (f32[2,16,512]{2,1,0:T(8,128)S(1)}, f32[2,16,512]{2,1,0:T(8,128)S(1)}, u32[]{:S(2)}, u32[]{:S(2)}) collective-permute-start(f32[2,16,512]{2,1,0:T(8,128)S(1)} %pad_maximum_fusion.5), channel_id=1, source_target_pairs={{0,512},{16,528},{32,544},{48,560},{64,576},{80,592},{96,608},{112... | collective-permute-start | bytes 196616 | tf_op jit(solution)/shard_map/ppermute | solution.py:101
  79.1 2.4 %collective-permute-done.5 = f32[2,16,512]{2,1,0:T(8,128)S(1)} collective-permute-done((f32[2,16,512]{2,1,0:T(8,128)S(1)}, f32[2,16,512]{2,1,0:T(8,128)S(1)}, u32[]{:S(2)}, u32[]{:S(2)}) %collective-permute-start.5) | collective-permute-done | bytes 65568 | tf_op jit(solution)/shard_map/ppermute | solution.py:101
  81.4 0.7 fusion.7.weights_ref
  82.1 2.7 %shard_map.96 = f32[256,512]{1,0:T(8,128)} custom-call(f32[16,512]{1,0:T(8,128)} %fusion.7.weights_ref, f32[16,512]{1,0:T(8,128)} %rates_ref.7), custom_call_target="tpu_custom_call" | custom-call | tf_op jit(solution)/shard_map/pallas_call | solution.py:71
  84.8 1.1 %bitcast_add_fusion = f32[256,512]{1,0:T(8,128)S(1)} fusion(f32[256,512]{1,0:T(8,128)} %shard_map.96, f32[4,64,512]{2,1,0:T(8,128)S(1)} %bitcast.165), kind=kLoop, calls=%fused_computation.13 | loop fusion | flops 131072 | bytes 1572864 | tf_op jit(solution)/shard_map/add | solution.py:74
  85.9 0.3 rev.7
  86.2 0.4 copy-done.3
  86.6 0.7 fusion.10.weights_ref
  87.3 2.7 %shard_map.95 = f32[256,512]{1,0:T(8,128)} custom-call(f32[16,512]{1,0:T(8,128)} %fusion.10.weights_ref, f32[16,512]{1,0:T(8,128)} %rates_ref.7), custom_call_target="tpu_custom_call" | custom-call | tf_op jit(solution)/shard_map/pallas_call | solution.py:71
  90.0 2.2 %fusion.1 = (bf16[256,512]{1,0:T(8,128)(2,1)}, bf16[256,512]{1,0:T(8,128)(2,1)}, bf16[256,512]{1,0:T(8,128)(2,1)}, bf16[256,512]{1,0:T(8,128)(2,1)}) fusion(f32[256,512]{1,0:T(8,128)S(1)} %rev.7, bf16[256,512]{1,0:T(8,128)(2,1)S(1)} %copy-done.9, bf16[256,512]{1,0:T(8,128)(2,1)S(1)} %copy-done.8, f32[256,512]{1,0:T(8,128)} %shard_map.95, ...), kind=kLoop, calls=%fused_computation.9 | loop fusion | flops 1703936 | bytes 3670016 | tf_op jit(solution)/shard_map/convert_element_type | solution.py:144
  (38 shorter events, 0.2 us)
Async XLA Ops:
  1.8 0.8 copy-start
  1.8 1.0 %copy-start.10 = (bf16[256,512]{1,0:T(8,128)(2,1)S(1)}, bf16[256,512]{1,0:T(8,128)(2,1)}, u32[]{:S(2)}) copy-start(bf16[256,512]{1,0:T(8,128)(2,1)} %param.11) | copy-start | bytes 786436
  1.8 1.0 %copy-start.11 = (bf16[256,512]{1,0:T(8,128)(2,1)S(1)}, bf16[256,512]{1,0:T(8,128)(2,1)}, u32[]{:S(2)}) copy-start(bf16[256,512]{1,0:T(8,128)(2,1)} %param.8) | copy-start | bytes 786436
  2.5 0.8 copy-start.5
  3.2 2.1 %copy-start.4 = (f32[256,512]{1,0:T(8,128)}, f32[256,512]{1,0:T(8,128)S(1)}, u32[]{:S(2)}) copy-start(f32[256,512]{1,0:T(8,128)S(1)} %rev.6.signal_ref) | copy-start | bytes 1572868
  5.5 9.4 %copy-start.13 = (f32[16,512]{1,0:T(8,128)S(1)}, f32[16,512]{1,0:T(8,128)}, u32[]{:S(2)}) copy-start(f32[16,512]{1,0:T(8,128)} %param.9) | copy-start | bytes 98308
  5.5 3.1 %collective-permute-start = (f32[2,16,512]{2,1,0:T(8,128)S(1)}, f32[2,16,512]{2,1,0:T(8,128)S(1)}, u32[]{:S(2)}, u32[]{:S(2)}) collective-permute-start(f32[2,16,512]{2,1,0:T(8,128)S(1)} %pad_maximum_fusion), channel_id=1, source_target_pairs={{0,16},{16,0},{32,48},{48,32},{64,80},{80,64},{96,112},{112,96},{1... | collective-permute-start | bytes 196616 | tf_op jit(solution)/shard_map/ppermute | solution.py:101
  8.7 6.2 %collective-permute-start.1 = (f32[2,16,512]{2,1,0:T(8,128)S(1)}, f32[2,16,512]{2,1,0:T(8,128)S(1)}, u32[]{:S(2)}, u32[]{:S(2)}) collective-permute-start(f32[2,16,512]{2,1,0:T(8,128)S(1)} %pad_maximum_fusion.1), channel_id=1, source_target_pairs={{0,32},{16,48},{32,0},{48,16},{64,96},{80,112},{96,64},{112,80},{1... | collective-permute-start | bytes 196616 | tf_op jit(solution)/shard_map/ppermute | solution.py:101
  15.6 16.0 %collective-permute-start.2 = (f32[2,16,512]{2,1,0:T(8,128)S(1)}, f32[2,16,512]{2,1,0:T(8,128)S(1)}, u32[]{:S(2)}, u32[]{:S(2)}) collective-permute-start(f32[2,16,512]{2,1,0:T(8,128)S(1)} %pad_maximum_fusion.2), channel_id=1, source_target_pairs={{0,64},{16,80},{32,96},{48,112},{64,0},{80,16},{96,32},{112,48},{1... | collective-permute-start | bytes 196616 | tf_op jit(solution)/shard_map/ppermute | solution.py:101
  20.1 11.5 %copy-start.1 = (f32[16,512]{1,0:T(8,128)S(1)}, f32[16,512]{1,0:T(8,128)}, u32[]{:S(2)}) copy-start(f32[16,512]{1,0:T(8,128)} %rates_ref.7) | copy-start | bytes 98308
  31.6 10.1 %collective-permute-start.3 = (f32[2,16,512]{2,1,0:T(8,128)S(1)}, f32[2,16,512]{2,1,0:T(8,128)S(1)}, u32[]{:S(2)}, u32[]{:S(2)}) collective-permute-start(f32[2,16,512]{2,1,0:T(8,128)S(1)} %pad_maximum_fusion.3), channel_id=1, source_target_pairs={{0,128},{16,144},{32,160},{48,176},{64,192},{80,208},{96,224},{112... | collective-permute-start | bytes 196616 | tf_op jit(solution)/shard_map/ppermute | solution.py:101
  41.7 22.5 %collective-permute-start.4 = (f32[2,16,512]{2,1,0:T(8,128)S(1)}, f32[2,16,512]{2,1,0:T(8,128)S(1)}, u32[]{:S(2)}, u32[]{:S(2)}) collective-permute-start(f32[2,16,512]{2,1,0:T(8,128)S(1)} %pad_maximum_fusion.4), channel_id=1, source_target_pairs={{0,256},{16,272},{32,288},{48,304},{64,320},{80,336},{96,352},{112... | collective-permute-start | bytes 196616 | tf_op jit(solution)/shard_map/ppermute | solution.py:101
  52.7 11.5 %copy-start.2 = (f32[16,512]{1,0:T(8,128)S(1)}, f32[16,512]{1,0:T(8,128)}, u32[]{:S(2)}) copy-start(f32[16,512]{1,0:T(8,128)} %rates_ref.7) | copy-start | bytes 98308
  64.2 17.2 %copy-start.12 = (f32[16,512]{1,0:T(8,128)S(1)}, f32[16,512]{1,0:T(8,128)}, u32[]{:S(2)}) copy-start(f32[16,512]{1,0:T(8,128)} %get-tuple-element.30.scaled_ref) | copy-start | bytes 98308
  64.3 20.5 %copy-start.7 = (f32[256,512]{1,0:T(8,128)S(1)}, f32[256,512]{1,0:T(8,128)}, u32[]{:S(2)}) copy-start(f32[256,512]{1,0:T(8,128)} %shard_map.94) | copy-start | bytes 1572868
  64.3 17.1 %collective-permute-start.5 = (f32[2,16,512]{2,1,0:T(8,128)S(1)}, f32[2,16,512]{2,1,0:T(8,128)S(1)}, u32[]{:S(2)}, u32[]{:S(2)}) collective-permute-start(f32[2,16,512]{2,1,0:T(8,128)S(1)} %pad_maximum_fusion.5), channel_id=1, source_target_pairs={{0,512},{16,528},{32,544},{48,560},{64,576},{80,592},{96,608},{112... | collective-permute-start | bytes 196616 | tf_op jit(solution)/shard_map/ppermute | solution.py:101
  85.9 0.8 copy-start.3
  85.9 4.1 %copy-start.9 = (bf16[256,512]{1,0:T(8,128)(2,1)S(1)}, bf16[256,512]{1,0:T(8,128)(2,1)}, u32[]{:S(2)}) copy-start(bf16[256,512]{1,0:T(8,128)(2,1)} %param.6) | copy-start | bytes 786436
  86.6 3.3 %copy-start.6 = (f32[256,512]{1,0:T(8,128)S(1)}, f32[256,512]{1,0:T(8,128)}, u32[]{:S(2)}) copy-start(f32[256,512]{1,0:T(8,128)} %shard_map.93) | copy-start | bytes 1572868
  86.6 3.3 %copy-start.8 = (bf16[256,512]{1,0:T(8,128)(2,1)S(1)}, bf16[256,512]{1,0:T(8,128)(2,1)}, u32[]{:S(2)}) copy-start(bf16[256,512]{1,0:T(8,128)(2,1)} %param.7) | copy-start | bytes 786436

commit v6 on v5

--- a/solution.py
+++ b/solution.py
@@ -84,6 +84,26 @@
     return jnp.sum(outer * jnp.sum(inner[None] * rows, axis=1), axis=0)
 
 
+RINGS = (4, 8, 2)
+
+
+def partner(place, span, count):
+    sizes = RINGS if count == 4 * 8 * 2 else (count,)
+    inner = count
+    for size in sizes:
+        inner //= size
+        coord = (place // inner) % size
+        if span < inner or span >= inner * size:
+            continue
+        bit = span // inner
+        if size >= 4 and bit == size // 2:
+            quarter = size // 4
+            moved = coord + quarter if (coord // quarter) % 2 == 1 else coord - quarter
+            return place + ((moved % size) - coord) * inner
+        return place ^ span
+    return place ^ span
+
+
 def incoming_states(fwd_state, bwd_state, rates, length, cover):
     count = lax.axis_size("ctx")
     place = lax.axis_index("ctx")
@@ -99,7 +119,9 @@
     bwd_in = jnp.zeros_like(bwd_state)
     for span in rounds:
         got = lax.ppermute(
-            jnp.stack([fwd_total, bwd_total]), "ctx", [(i, i ^ span) for i in range(count)]
+            jnp.stack([fwd_total, bwd_total]),
+            "ctx",
+            [(i, partner(i, span, count)) for i in range(count)],
         )
         if span in slots:
             got, cover[slots[span]] = lax.optimization_barrier((got, cover[slots[span]]))

time: 93.3 us -> 88 us (0.943)
  starting transfers between devices: 41.4 us -> 37.6 us
  waiting for transfers between devices: 10.3 us -> 8.71 us
    ppermute x6, starting transfers between devices: 41.4 us -> 37.6 us  [incoming_states(): lax.ppermute(jnp.stack([fwd_total, bwd_total]), 'ctx', [(i, partner(i, sp...]
    ppermute x6, waiting for transfers between devices: 10.3 us -> 8.71 us  [incoming_states(): lax.ppermute(jnp.stack([fwd_total, bwd_total]), 'ctx', [(i, partner(i, sp...]
  transfers between devices with their start and end apart: 6 -> 6, of which waited for: 4 -> 4; matrix products, arithmetic and copies ran while one was open for 0% -> 0% of each run, Pallas kernels for 25% -> 26%
where the time goes in v6:
time: 88 us; the launch traced here: 86.8 us
  starting transfers between devices  37.6 us (43%)
  Pallas kernels  28.3 us (32%)
  other arithmetic  9.01 us (10%)
  waiting for transfers between devices  8.71 us (10%)
  local copies, waits for them, and re-layouts  2.03 us (2%)
  between operations  1.16 us (1%)
    ppermute x6, starting transfers between devices, incoming_states(): lax.ppermute(jnp.stack([fwd_total, bwd_total]), 'ctx', [(i, partner(i, sp...  37.6 us
    pallas_call x2, Pallas kernels, local_pass(): pl.pallas_call(local_kernel, out_shape=jax.ShapeDtypeStruct((length, widt...  23 us
    ppermute x6, waiting for transfers between devices, incoming_states(): lax.ppermute(jnp.stack([fwd_total, bwd_total]), 'ctx', [(i, partner(i, sp...  8.71 us
    pallas_call x2, Pallas kernels, apply_incoming(): pl.pallas_call(carried_kernel, out_shape=jax.ShapeDtypeStruct((count * BL...  5.34 us
    convert_element_type x1, other arithmetic, per_device(): grad_key = (back * query_f).astype(jnp.bfloat16)  2.24 us
    reduce_sum x2, other arithmetic, end_state(): return jnp.sum(outer * jnp.sum(inner[None] * rows, axis=1), axis=0)  2.14 us
  transfers between devices with their start and end apart: 6, of which 4 were waited for; matrix products, arithmetic and copies ran while one was open for 0% of the time, Pallas kernels for 26%

profile of v6, /device:TPU:6, one launch (start us, length us, event | category | flops | bytes accessed | tf_op | source)
XLA Modules:
  0.0 86.8 jit_solution(10279040876266905897)
XLA Ops:
  0.7 1.1 %fusion.2 = bf16[256,512]{1,0:T(8,128)(2,1)S(1)} fusion(bf16[256,512]{1,0:T(8,128)(2,1)} %param.7, bf16[256,512]{1,0:T(8,128)(2,1)} %param.6), kind=kLoop, calls=%fused_computation.10 | loop fusion | flops 524288 | bytes 786432 | tf_op jit(solution)/shard_map/convert_element_type | solution.py:149
  1.8 0.1 convert_element_type.66.signal_ref
  1.8 0.7 copy-done
  2.5 0.2 copy-done.10
  2.7 0.1 copy-done.11
  2.8 0.1 convert_multiply_fusion.1
  2.9 0.3 rev.6.signal_ref
  3.2 0.1 multiply_exponential_fusion
  3.3 0.0 copy-done.5
  3.3 2.0 %multiply_reduce_fusion.1 = (f32[16,16,512]{2,1,0:T(8,128)S(1)}, f32[16,16,512]{2,1,0:T(8,128)S(1)}) fusion(f32[16,16,512]{2,1,0:T(8,128)S(1)} %bitcast.163, f32[16,16,512]{2,1,0:T(8,128)S(1)} %multiply_exponential_fusion, f32[16,16,512]{2,1,0:T(8,128)S(1)} %bitcast.162), kind=kLoop, calls=%fused_computation.1 | loop fusion | flops 8126464 | bytes 2621440 | tf_op jit(solution)/shard_map/reduce_sum | solution.py:84
  5.3 0.2 multiply_reduce_fusion.3
  5.5 1.9 %collective-permute-start = (f32[2,16,512]{2,1,0:T(8,128)S(1)}, f32[2,16,512]{2,1,0:T(8,128)S(1)}, u32[]{:S(2)}, u32[]{:S(2)}) collective-permute-start(f32[2,16,512]{2,1,0:T(8,128)S(1)} %pad_maximum_fusion), channel_id=1, source_target_pairs={{0,16},{16,0},{32,48},{48,32},{64,80},{80,64},{96,112},{112,96},{1... | collective-permute-start | bytes 196616 | tf_op jit(solution)/shard_map/ppermute | solution.py:121
  7.5 1.2 %collective-permute-done = f32[2,16,512]{2,1,0:T(8,128)S(1)} collective-permute-done((f32[2,16,512]{2,1,0:T(8,128)S(1)}, f32[2,16,512]{2,1,0:T(8,128)S(1)}, u32[]{:S(2)}, u32[]{:S(2)}) %collective-permute-start) | collective-permute-done | bytes 65568 | tf_op jit(solution)/shard_map/ppermute | solution.py:121
  8.7 3.5 %collective-permute-start.1 = (f32[2,16,512]{2,1,0:T(8,128)S(1)}, f32[2,16,512]{2,1,0:T(8,128)S(1)}, u32[]{:S(2)}, u32[]{:S(2)}) collective-permute-start(f32[2,16,512]{2,1,0:T(8,128)S(1)} %pad_maximum_fusion.1), channel_id=1, source_target_pairs={{0,32},{16,48},{32,0},{48,16},{64,96},{80,112},{96,64},{112,80},{1... | collective-permute-start | bytes 196616 | tf_op jit(solution)/shard_map/ppermute | solution.py:121
  12.3 2.6 %collective-permute-done.1 = f32[2,16,512]{2,1,0:T(8,128)S(1)} collective-permute-done((f32[2,16,512]{2,1,0:T(8,128)S(1)}, f32[2,16,512]{2,1,0:T(8,128)S(1)}, u32[]{:S(2)}, u32[]{:S(2)}) %collective-permute-start.1) | collective-permute-done | bytes 65568 | tf_op jit(solution)/shard_map/ppermute | solution.py:121
  14.9 0.7 add_select_fusion.3
  15.6 4.5 %collective-permute-start.2 = (f32[2,16,512]{2,1,0:T(8,128)S(1)}, f32[2,16,512]{2,1,0:T(8,128)S(1)}, u32[]{:S(2)}, u32[]{:S(2)}) collective-permute-start(f32[2,16,512]{2,1,0:T(8,128)S(1)} %pad_maximum_fusion.2), channel_id=1, source_target_pairs={{0,64},{16,80},{32,96},{48,112},{64,0},{80,16},{96,32},{112,48},{1... | collective-permute-start | bytes 196616 | tf_op jit(solution)/shard_map/ppermute | solution.py:121
  20.1 11.5 %shard_map.93 = f32[256,512]{1,0:T(8,128)} custom-call(f32[256,512]{1,0:T(8,128)} %copy-done.5, f32[16,512]{1,0:T(8,128)} %get-tuple-element.30.scaled_ref, f32[16,512]{1,0:T(8,128)} %rates_ref.7), custom_call_target="tpu_custom_call" | custom-call | tf_op jit(solution)/shard_map/pallas_call | solution.py:45
  31.6 5.7 %collective-permute-start.3 = (f32[2,16,512]{2,1,0:T(8,128)S(1)}, f32[2,16,512]{2,1,0:T(8,128)S(1)}, u32[]{:S(2)}, u32[]{:S(2)}) collective-permute-start(f32[2,16,512]{2,1,0:T(8,128)S(1)} %pad_maximum_fusion.3), channel_id=1, source_target_pairs={{0,192},{16,208},{32,224},{48,240},{64,128},{80,144},{96,160},{112... | collective-permute-start | bytes 196616 | tf_op jit(solution)/shard_map/ppermute | solution.py:121
  37.4 2.6 %collective-permute-done.3 = f32[2,16,512]{2,1,0:T(8,128)S(1)} collective-permute-done((f32[2,16,512]{2,1,0:T(8,128)S(1)}, f32[2,16,512]{2,1,0:T(8,128)S(1)}, u32[]{:S(2)}, u32[]{:S(2)}) %collective-permute-start.3) | collective-permute-done | bytes 65568 | tf_op jit(solution)/shard_map/ppermute | solution.py:121
  40.0 10.9 %collective-permute-start.4 = (f32[2,16,512]{2,1,0:T(8,128)S(1)}, f32[2,16,512]{2,1,0:T(8,128)S(1)}, u32[]{:S(2)}, u32[]{:S(2)}) collective-permute-start(f32[2,16,512]{2,1,0:T(8,128)S(1)} %pad_maximum_fusion.4), channel_id=1, source_target_pairs={{0,256},{16,272},{32,288},{48,304},{64,320},{80,336},{96,352},{112... | collective-permute-start | bytes 196616 | tf_op jit(solution)/shard_map/ppermute | solution.py:121
  51.0 11.5 %shard_map.94 = f32[256,512]{1,0:T(8,128)} custom-call(f32[256,512]{1,0:T(8,128)} %copy-done.4, f32[16,512]{1,0:T(8,128)} %get-tuple-element.30.scaled_ref, f32[16,512]{1,0:T(8,128)} %rates_ref.7), custom_call_target="tpu_custom_call" | custom-call | tf_op jit(solution)/shard_map/pallas_call | solution.py:45
  62.5 11.0 %collective-permute-start.5 = (f32[2,16,512]{2,1,0:T(8,128)S(1)}, f32[2,16,512]{2,1,0:T(8,128)S(1)}, u32[]{:S(2)}, u32[]{:S(2)}) collective-permute-start(f32[2,16,512]{2,1,0:T(8,128)S(1)} %pad_maximum_fusion.5), channel_id=1, source_target_pairs={{0,768},{16,784},{32,800},{48,816},{64,832},{80,848},{96,864},{112... | collective-permute-start | bytes 196616 | tf_op jit(solution)/shard_map/ppermute | solution.py:121
  73.7 2.3 %collective-permute-done.5 = f32[2,16,512]{2,1,0:T(8,128)S(1)} collective-permute-done((f32[2,16,512]{2,1,0:T(8,128)S(1)}, f32[2,16,512]{2,1,0:T(8,128)S(1)}, u32[]{:S(2)}, u32[]{:S(2)}) %collective-permute-start.5) | collective-permute-done | bytes 65568 | tf_op jit(solution)/shard_map/ppermute | solution.py:121
  76.0 0.7 fusion.7.weights_ref
  76.6 2.7 %shard_map.96 = f32[256,512]{1,0:T(8,128)} custom-call(f32[16,512]{1,0:T(8,128)} %fusion.7.weights_ref, f32[16,512]{1,0:T(8,128)} %rates_ref.7), custom_call_target="tpu_custom_call" | custom-call | tf_op jit(solution)/shard_map/pallas_call | solution.py:71
  79.3 1.1 %bitcast_add_fusion = f32[256,512]{1,0:T(8,128)S(1)} fusion(f32[256,512]{1,0:T(8,128)} %shard_map.96, f32[4,64,512]{2,1,0:T(8,128)S(1)} %bitcast.165), kind=kLoop, calls=%fused_computation.13 | loop fusion | flops 131072 | bytes 1572864 | tf_op jit(solution)/shard_map/add | solution.py:74
  80.4 0.3 rev.7
  80.7 0.4 copy-done.3
  81.2 0.7 fusion.10.weights_ref
  81.8 2.7 %shard_map.95 = f32[256,512]{1,0:T(8,128)} custom-call(f32[16,512]{1,0:T(8,128)} %fusion.10.weights_ref, f32[16,512]{1,0:T(8,128)} %rates_ref.7), custom_call_target="tpu_custom_call" | custom-call | tf_op jit(solution)/shard_map/pallas_call | solution.py:71
  84.5 2.2 %fusion.1 = (bf16[256,512]{1,0:T(8,128)(2,1)}, bf16[256,512]{1,0:T(8,128)(2,1)}, bf16[256,512]{1,0:T(8,128)(2,1)}, bf16[256,512]{1,0:T(8,128)(2,1)}) fusion(f32[256,512]{1,0:T(8,128)S(1)} %rev.7, bf16[256,512]{1,0:T(8,128)(2,1)S(1)} %copy-done.9, bf16[256,512]{1,0:T(8,128)(2,1)S(1)} %copy-done.8, f32[256,512]{1,0:T(8,128)} %shard_map.95, ...), kind=kLoop, calls=%fused_computation.9 | loop fusion | flops 1703936 | bytes 3670016 | tf_op jit(solution)/shard_map/convert_element_type | solution.py:166
  (38 shorter events, 0.2 us)
Async XLA Ops:
  1.8 0.8 copy-start
  1.8 1.0 %copy-start.10 = (bf16[256,512]{1,0:T(8,128)(2,1)S(1)}, bf16[256,512]{1,0:T(8,128)(2,1)}, u32[]{:S(2)}) copy-start(bf16[256,512]{1,0:T(8,128)(2,1)} %param.11) | copy-start | bytes 786436
  1.8 1.0 %copy-start.11 = (bf16[256,512]{1,0:T(8,128)(2,1)S(1)}, bf16[256,512]{1,0:T(8,128)(2,1)}, u32[]{:S(2)}) copy-start(bf16[256,512]{1,0:T(8,128)(2,1)} %param.8) | copy-start | bytes 786436
  2.5 0.8 copy-start.5
  3.2 2.1 %copy-start.4 = (f32[256,512]{1,0:T(8,128)}, f32[256,512]{1,0:T(8,128)S(1)}, u32[]{:S(2)}) copy-start(f32[256,512]{1,0:T(8,128)S(1)} %rev.6.signal_ref) | copy-start | bytes 1572868
  5.5 9.4 %copy-start.13 = (f32[16,512]{1,0:T(8,128)S(1)}, f32[16,512]{1,0:T(8,128)}, u32[]{:S(2)}) copy-start(f32[16,512]{1,0:T(8,128)} %param.9) | copy-start | bytes 98308
  5.5 3.1 %collective-permute-start = (f32[2,16,512]{2,1,0:T(8,128)S(1)}, f32[2,16,512]{2,1,0:T(8,128)S(1)}, u32[]{:S(2)}, u32[]{:S(2)}) collective-permute-start(f32[2,16,512]{2,1,0:T(8,128)S(1)} %pad_maximum_fusion), channel_id=1, source_target_pairs={{0,16},{16,0},{32,48},{48,32},{64,80},{80,64},{96,112},{112,96},{1... | collective-permute-start | bytes 196616 | tf_op jit(solution)/shard_map/ppermute | solution.py:121
  8.7 6.2 %collective-permute-start.1 = (f32[2,16,512]{2,1,0:T(8,128)S(1)}, f32[2,16,512]{2,1,0:T(8,128)S(1)}, u32[]{:S(2)}, u32[]{:S(2)}) collective-permute-start(f32[2,16,512]{2,1,0:T(8,128)S(1)} %pad_maximum_fusion.1), channel_id=1, source_target_pairs={{0,32},{16,48},{32,0},{48,16},{64,96},{80,112},{96,64},{112,80},{1... | collective-permute-start | bytes 196616 | tf_op jit(solution)/shard_map/ppermute | solution.py:121
  15.6 16.0 %collective-permute-start.2 = (f32[2,16,512]{2,1,0:T(8,128)S(1)}, f32[2,16,512]{2,1,0:T(8,128)S(1)}, u32[]{:S(2)}, u32[]{:S(2)}) collective-permute-start(f32[2,16,512]{2,1,0:T(8,128)S(1)} %pad_maximum_fusion.2), channel_id=1, source_target_pairs={{0,64},{16,80},{32,96},{48,112},{64,0},{80,16},{96,32},{112,48},{1... | collective-permute-start | bytes 196616 | tf_op jit(solution)/shard_map/ppermute | solution.py:121
  20.1 11.5 %copy-start.1 = (f32[16,512]{1,0:T(8,128)S(1)}, f32[16,512]{1,0:T(8,128)}, u32[]{:S(2)}) copy-start(f32[16,512]{1,0:T(8,128)} %rates_ref.7) | copy-start | bytes 98308
  31.6 8.3 %collective-permute-start.3 = (f32[2,16,512]{2,1,0:T(8,128)S(1)}, f32[2,16,512]{2,1,0:T(8,128)S(1)}, u32[]{:S(2)}, u32[]{:S(2)}) collective-permute-start(f32[2,16,512]{2,1,0:T(8,128)S(1)} %pad_maximum_fusion.3), channel_id=1, source_target_pairs={{0,192},{16,208},{32,224},{48,240},{64,128},{80,144},{96,160},{112... | collective-permute-start | bytes 196616 | tf_op jit(solution)/shard_map/ppermute | solution.py:121
  40.0 22.5 %collective-permute-start.4 = (f32[2,16,512]{2,1,0:T(8,128)S(1)}, f32[2,16,512]{2,1,0:T(8,128)S(1)}, u32[]{:S(2)}, u32[]{:S(2)}) collective-permute-start(f32[2,16,512]{2,1,0:T(8,128)S(1)} %pad_maximum_fusion.4), channel_id=1, source_target_pairs={{0,256},{16,272},{32,288},{48,304},{64,320},{80,336},{96,352},{112... | collective-permute-start | bytes 196616 | tf_op jit(solution)/shard_map/ppermute | solution.py:121
  51.0 11.5 %copy-start.2 = (f32[16,512]{1,0:T(8,128)S(1)}, f32[16,512]{1,0:T(8,128)}, u32[]{:S(2)}) copy-start(f32[16,512]{1,0:T(8,128)} %rates_ref.7) | copy-start | bytes 98308
  62.5 13.5 %copy-start.12 = (f32[16,512]{1,0:T(8,128)S(1)}, f32[16,512]{1,0:T(8,128)}, u32[]{:S(2)}) copy-start(f32[16,512]{1,0:T(8,128)} %get-tuple-element.30.scaled_ref) | copy-start | bytes 98308
  62.5 16.8 %copy-start.7 = (f32[256,512]{1,0:T(8,128)S(1)}, f32[256,512]{1,0:T(8,128)}, u32[]{:S(2)}) copy-start(f32[256,512]{1,0:T(8,128)} %shard_map.94) | copy-start | bytes 1572868
  62.5 13.4 %collective-permute-start.5 = (f32[2,16,512]{2,1,0:T(8,128)S(1)}, f32[2,16,512]{2,1,0:T(8,128)S(1)}, u32[]{:S(2)}, u32[]{:S(2)}) collective-permute-start(f32[2,16,512]{2,1,0:T(8,128)S(1)} %pad_maximum_fusion.5), channel_id=1, source_target_pairs={{0,768},{16,784},{32,800},{48,816},{64,832},{80,848},{96,864},{112... | collective-permute-start | bytes 196616 | tf_op jit(solution)/shard_map/ppermute | solution.py:121
  80.4 0.8 copy-start.3
  80.4 4.1 %copy-start.9 = (bf16[256,512]{1,0:T(8,128)(2,1)S(1)}, bf16[256,512]{1,0:T(8,128)(2,1)}, u32[]{:S(2)}) copy-start(bf16[256,512]{1,0:T(8,128)(2,1)} %param.6) | copy-start | bytes 786436
  81.2 3.3 %copy-start.6 = (f32[256,512]{1,0:T(8,128)S(1)}, f32[256,512]{1,0:T(8,128)}, u32[]{:S(2)}) copy-start(f32[256,512]{1,0:T(8,128)} %shard_map.93) | copy-start | bytes 1572868
  81.2 3.3 %copy-start.8 = (bf16[256,512]{1,0:T(8,128)(2,1)S(1)}, bf16[256,512]{1,0:T(8,128)(2,1)}, u32[]{:S(2)}) copy-start(bf16[256,512]{1,0:T(8,128)(2,1)} %param.7) | copy-start | bytes 786436

commit v7 on v6

--- a/solution.py
+++ b/solution.py
@@ -112,7 +112,7 @@
     while span < count:
         rounds.append(span)
         span *= 2
-    slots = {rounds[min(2, len(rounds) - 1)]: 0, rounds[min(4, len(rounds) - 1)]: 1}
+    slots = {span: k for k, span in enumerate(rounds[len(rounds) - len(cover) :])}
     cover = list(cover)
     fwd_total, bwd_total = fwd_state, bwd_state
     fwd_in = jnp.zeros_like(fwd_state)
@@ -149,15 +149,21 @@
     gated = lax.optimization_barrier((query_f * key_f).astype(jnp.bfloat16)).astype(jnp.float32)
     weighted = cot_f * value_f
     reversed_weighted = weighted[::-1]
-    fwd_pieces = local_pass(gated, scaled, rates)
-    bwd_pieces = local_pass(reversed_weighted, scaled, rates)
-    fwd_in, bwd_in, (fwd_pieces, bwd_pieces) = incoming_states(
+    half = rates.shape[0] // 2
+    cover = tuple(
+        local_pass(signal, scaled[modes], rates[modes])
+        for signal in (gated, reversed_weighted)
+        for modes in (slice(0, half), slice(half, None))
+    )
+    fwd_in, bwd_in, cover = incoming_states(
         end_state(gated, rates),
         end_state(reversed_weighted, rates),
         rates,
         length,
-        (fwd_pieces, bwd_pieces),
+        cover,
     )
+    fwd_pieces = cover[0] + cover[1]
+    bwd_pieces = cover[2] + cover[3]
     mixed = apply_incoming(fwd_pieces, fwd_in, scaled, rates)
     back = apply_incoming(bwd_pieces, bwd_in, scaled, rates)[::-1]
     output = (value_f * mixed).astype(jnp.bfloat16)

time: 88 us -> 86.9 us (0.988)
  waiting for transfers between devices: 8.71 us -> 3.27 us
  Pallas kernels: 28.3 us -> 32.3 us
  local copies, waits for them, and re-layouts: 2.03 us -> 4.89 us
  other arithmetic: 9.01 us -> 7.24 us
    ppermute x6, waiting for transfers between devices: 8.71 us -> 3.27 us  [incoming_states(): lax.ppermute(jnp.stack([fwd_total, bwd_total]), 'ctx', [(i, partner(i, sp...]
    pallas_call x2 -> x4, Pallas kernels: 23 us -> 26.9 us  [local_pass(): pl.pallas_call(local_kernel, out_shape=jax.ShapeDtypeStruct((length, widt...]
    unnamed x28 -> x30, local copies, waits for them, and re-layouts: 1.46 us -> 3.09 us
    slice x0 -> x2, local copies, waits for them, and re-layouts: none -> 1.23 us  [the longest x1 0.61 us: per_device(): rates[modes]]
    convert_element_type x1, other arithmetic: 2.24 us -> 1.19 us  [per_device(): grad_key = (back * query_f).astype(jnp.bfloat16)]
    add x1, other arithmetic: 1.1 us -> 0.08 us  [apply_incoming(): return pieces.reshape(count * BLOCK, width) + extra]
  transfers between devices with their start and end apart: 6 -> 6, of which waited for: 4 -> 2; matrix products, arithmetic and copies ran while one was open for 0% -> 2% of each run, Pallas kernels for 26% -> 31%
where the time goes in v7:
time: 86.9 us; the launch traced here: 86.3 us
  starting transfers between devices  37.4 us (43%)
  Pallas kernels  32.3 us (37%)
  other arithmetic  7.24 us (8%)
  local copies, waits for them, and re-layouts  4.89 us (6%)
  waiting for transfers between devices  3.27 us (4%)
  between operations  1.13 us (1%)
    ppermute x6, starting transfers between devices, incoming_states(): lax.ppermute(jnp.stack([fwd_total, bwd_total]), 'ctx', [(i, partner(i, sp...  37.4 us
    pallas_call x4, Pallas kernels, local_pass(): pl.pallas_call(local_kernel, out_shape=jax.ShapeDtypeStruct((length, widt...  26.9 us
    pallas_call x2, Pallas kernels, apply_incoming(): pl.pallas_call(carried_kernel, out_shape=jax.ShapeDtypeStruct((count * BL...  5.42 us
    ppermute x6, waiting for transfers between devices, incoming_states(): lax.ppermute(jnp.stack([fwd_total, bwd_total]), 'ctx', [(i, partner(i, sp...  3.27 us
    unnamed x30, local copies, waits for them, and re-layouts  3.09 us
    reduce_sum x2, other arithmetic, end_state(): return jnp.sum(outer * jnp.sum(inner[None] * rows, axis=1), axis=0)  2.14 us
  transfers between devices with their start and end apart: 6, of which 2 were waited for; matrix products, arithmetic and copies ran while one was open for 2% of the time, Pallas kernels for 31%

profile of v7, /device:TPU:6, one launch (start us, length us, event | category | flops | bytes accessed | tf_op | source)
XLA Modules:
  0.0 86.3 jit_solution(17136903893510418210)
XLA Ops:
  0.7 0.8 neg.5
  1.4 1.1 %fusion.2 = bf16[256,512]{1,0:T(8,128)(2,1)S(1)} fusion(bf16[256,512]{1,0:T(8,128)(2,1)} %param.7, bf16[256,512]{1,0:T(8,128)(2,1)} %param.6), kind=kLoop, calls=%fused_computation.10 | loop fusion | flops 524288 | bytes 786432 | tf_op jit(solution)/shard_map/convert_element_type | solution.py:149
  2.6 0.9 %copy-done.12 = bf16[256,512]{1,0:T(8,128)(2,1)S(1)} copy-done((bf16[256,512]{1,0:T(8,128)(2,1)S(1)}, bf16[256,512]{1,0:T(8,128)(2,1)}, u32[]{:S(2)}) %copy-start.12) | copy-done | bytes 262168
  3.6 0.3 rev.6.signal_ref
  3.9 0.1 multiply_exponential_fusion
  4.1 0.3 copy-done.1
  4.3 1.9 %multiply_reduce_fusion.1 = (f32[16,16,512]{2,1,0:T(8,128)S(1)}, f32[16,16,512]{2,1,0:T(8,128)S(1)}) fusion(f32[16,16,512]{2,1,0:T(8,128)S(1)} %bitcast.173, f32[16,16,512]{2,1,0:T(8,128)S(1)} %multiply_exponential_fusion, f32[16,16,512]{2,1,0:T(8,128)S(1)} %bitcast.172), kind=kLoop, calls=%fused_computation.1 | loop fusion | flops 8126464 | bytes 2621440 | tf_op jit(solution)/shard_map/reduce_sum | solution.py:84
  6.3 0.2 multiply_reduce_fusion.3
  6.5 1.9 %collective-permute-start = (f32[2,16,512]{2,1,0:T(8,128)S(1)}, f32[2,16,512]{2,1,0:T(8,128)S(1)}, u32[]{:S(2)}, u32[]{:S(2)}) collective-permute-start(f32[2,16,512]{2,1,0:T(8,128)S(1)} %pad_maximum_fusion), channel_id=1, source_target_pairs={{0,16},{16,0},{32,48},{48,32},{64,80},{80,64},{96,112},{112,96},{1... | collective-permute-start | bytes 196616 | tf_op jit(solution)/shard_map/ppermute | solution.py:121
  8.5 1.2 %collective-permute-done = f32[2,16,512]{2,1,0:T(8,128)S(1)} collective-permute-done((f32[2,16,512]{2,1,0:T(8,128)S(1)}, f32[2,16,512]{2,1,0:T(8,128)S(1)}, u32[]{:S(2)}, u32[]{:S(2)}) %collective-permute-start) | collective-permute-done | bytes 65568 | tf_op jit(solution)/shard_map/ppermute | solution.py:121
  9.7 3.5 %collective-permute-start.1 = (f32[2,16,512]{2,1,0:T(8,128)S(1)}, f32[2,16,512]{2,1,0:T(8,128)S(1)}, u32[]{:S(2)}, u32[]{:S(2)}) collective-permute-start(f32[2,16,512]{2,1,0:T(8,128)S(1)} %pad_maximum_fusion.1), channel_id=1, source_target_pairs={{0,32},{16,48},{32,0},{48,16},{64,96},{80,112},{96,64},{112,80},{1... | collective-permute-start | bytes 196616 | tf_op jit(solution)/shard_map/ppermute | solution.py:121
  13.2 0.6 fusion.33
  13.8 2.1 %collective-permute-done.1 = f32[2,16,512]{2,1,0:T(8,128)S(1)} collective-permute-done((f32[2,16,512]{2,1,0:T(8,128)S(1)}, f32[2,16,512]{2,1,0:T(8,128)S(1)}, u32[]{:S(2)}, u32[]{:S(2)}) %collective-permute-start.1) | collective-permute-done | bytes 65568 | tf_op jit(solution)/shard_map/ppermute | solution.py:121
  16.0 4.5 %collective-permute-start.2 = (f32[2,16,512]{2,1,0:T(8,128)S(1)}, f32[2,16,512]{2,1,0:T(8,128)S(1)}, u32[]{:S(2)}, u32[]{:S(2)}) collective-permute-start(f32[2,16,512]{2,1,0:T(8,128)S(1)} %pad_maximum_fusion.2), channel_id=1, source_target_pairs={{0,64},{16,80},{32,96},{48,112},{64,0},{80,16},{96,32},{112,48},{1... | collective-permute-start | bytes 196616 | tf_op jit(solution)/shard_map/ppermute | solution.py:121
  20.5 0.6 fusion.34
  21.1 6.7 %shard_map.93 = f32[256,512]{1,0:T(8,128)} custom-call(f32[256,512]{1,0:T(8,128)} %copy-done.1, f32[8,512]{1,0:T(8,128)} %get-tuple-element.41.scaled_ref, f32[8,512]{1,0:T(8,128)} %get-tuple-element.39.rates_ref), custom_call_target="tpu_custom_call" | custom-call | tf_op jit(solution)/shard_map/pallas_call | solution.py:45
  27.9 5.7 %collective-permute-start.3 = (f32[2,16,512]{2,1,0:T(8,128)S(1)}, f32[2,16,512]{2,1,0:T(8,128)S(1)}, u32[]{:S(2)}, u32[]{:S(2)}) collective-permute-start(f32[2,16,512]{2,1,0:T(8,128)S(1)} %pad_maximum_fusion.3), channel_id=1, source_target_pairs={{0,192},{16,208},{32,224},{48,240},{64,128},{80,144},{96,160},{112... | collective-permute-start | bytes 196616 | tf_op jit(solution)/shard_map/ppermute | solution.py:121
  33.6 6.7 %shard_map.94 = f32[256,512]{1,0:T(8,128)} custom-call(f32[256,512]{1,0:T(8,128)} %copy-done.1, f32[8,512]{1,0:T(8,128)} %get-tuple-element.40.scaled_ref, f32[8,512]{1,0:T(8,128)} %get-tuple-element.38.rates_ref), custom_call_target="tpu_custom_call" | custom-call | tf_op jit(solution)/shard_map/pallas_call | solution.py:45
  40.3 10.9 %collective-permute-start.4 = (f32[2,16,512]{2,1,0:T(8,128)S(1)}, f32[2,16,512]{2,1,0:T(8,128)S(1)}, u32[]{:S(2)}, u32[]{:S(2)}) collective-permute-start(f32[2,16,512]{2,1,0:T(8,128)S(1)} %pad_maximum_fusion.4), channel_id=1, source_target_pairs={{0,256},{16,272},{32,288},{48,304},{64,320},{80,336},{96,352},{112... | collective-permute-start | bytes 196616 | tf_op jit(solution)/shard_map/ppermute | solution.py:121
  51.3 6.7 %shard_map.95 = f32[256,512]{1,0:T(8,128)} custom-call(f32[256,512]{1,0:T(8,128)} %copy-done, f32[8,512]{1,0:T(8,128)} %get-tuple-element.41.scaled_ref, f32[8,512]{1,0:T(8,128)} %get-tuple-element.39.rates_ref), custom_call_target="tpu_custom_call" | custom-call | tf_op jit(solution)/shard_map/pallas_call | solution.py:45
  58.0 10.9 %collective-permute-start.5 = (f32[2,16,512]{2,1,0:T(8,128)S(1)}, f32[2,16,512]{2,1,0:T(8,128)S(1)}, u32[]{:S(2)}, u32[]{:S(2)}) collective-permute-start(f32[2,16,512]{2,1,0:T(8,128)S(1)} %pad_maximum_fusion.5), channel_id=1, source_target_pairs={{0,768},{16,784},{32,800},{48,816},{64,832},{80,848},{96,864},{112... | collective-permute-start | bytes 196616 | tf_op jit(solution)/shard_map/ppermute | solution.py:121
  69.1 6.8 %shard_map.96 = f32[256,512]{1,0:T(8,128)} custom-call(f32[256,512]{1,0:T(8,128)} %copy-done, f32[8,512]{1,0:T(8,128)} %get-tuple-element.40.scaled_ref, f32[8,512]{1,0:T(8,128)} %get-tuple-element.38.rates_ref), custom_call_target="tpu_custom_call" | custom-call | tf_op jit(solution)/shard_map/pallas_call | solution.py:45
  76.0 0.7 fusion.8.weights_ref
  76.6 2.7 %shard_map.97 = f32[256,512]{1,0:T(8,128)} custom-call(f32[16,512]{1,0:T(8,128)} %fusion.8.weights_ref, f32[16,512]{1,0:T(8,128)} %rates_ref.3), custom_call_target="tpu_custom_call" | custom-call | tf_op jit(solution)/shard_map/pallas_call | solution.py:71
  79.4 0.7 fusion.6.weights_ref
  80.0 2.7 %shard_map.98 = f32[256,512]{1,0:T(8,128)} custom-call(f32[16,512]{1,0:T(8,128)} %fusion.6.weights_ref, f32[16,512]{1,0:T(8,128)} %rates_ref.3), custom_call_target="tpu_custom_call" | custom-call | tf_op jit(solution)/shard_map/pallas_call | solution.py:71
  82.7 0.1 add.178
  82.8 0.9 %copy-done.9 = f32[256,512]{1,0:T(8,128)S(1)} copy-done((f32[256,512]{1,0:T(8,128)S(1)}, f32[256,512]{1,0:T(8,128)}, u32[]{:S(2)}) %copy-start.9) | copy-done | bytes 524312
  83.8 0.1 bitcast_add_fusion
  83.9 0.3 rev.7
  84.2 0.7 copy-done.8
  85.1 1.2 %fusion.1 = (bf16[256,512]{1,0:T(8,128)(2,1)}, bf16[256,512]{1,0:T(8,128)(2,1)}, bf16[256,512]{1,0:T(8,128)(2,1)}, bf16[256,512]{1,0:T(8,128)(2,1)}) fusion(f32[256,512]{1,0:T(8,128)S(1)} %rev.7, bf16[256,512]{1,0:T(8,128)(2,1)S(1)} %copy-done.11, bf16[256,512]{1,0:T(8,128)(2,1)S(1)} %copy-done.10, f32[256,512]{1,0:T(8,128)S(1)} %copy-done.8, ...), kind=kLoop, calls=%fused_computation.9 | loop fusion | flops 1703936 | bytes 3670016 | tf_op jit(solution)/shard_map/convert_element_type | solution.py:172
  (46 shorter events, 0.7 us)
Async XLA Ops:
  2.5 1.0 %copy-start.12 = (bf16[256,512]{1,0:T(8,128)(2,1)S(1)}, bf16[256,512]{1,0:T(8,128)(2,1)}, u32[]{:S(2)}) copy-start(bf16[256,512]{1,0:T(8,128)(2,1)} %param.11) | copy-start | bytes 786436
  2.5 1.0 %copy-start.13 = (bf16[256,512]{1,0:T(8,128)(2,1)S(1)}, bf16[256,512]{1,0:T(8,128)(2,1)}, u32[]{:S(2)}) copy-start(bf16[256,512]{1,0:T(8,128)(2,1)} %param.8) | copy-start | bytes 786436
  3.5 0.8 copy-start.1
  3.9 2.4 %copy-start = (f32[256,512]{1,0:T(8,128)}, f32[256,512]{1,0:T(8,128)S(1)}, u32[]{:S(2)}) copy-start(f32[256,512]{1,0:T(8,128)S(1)} %rev.6.signal_ref) | copy-start | bytes 1572868
  6.3 3.4 %copy-start.2 = (f32[16,512]{1,0:T(8,128)S(1)}, f32[16,512]{1,0:T(8,128)}, u32[]{:S(2)}) copy-start(f32[16,512]{1,0:T(8,128)} %rates_ref.3) | copy-start | bytes 98308
  6.5 9.4 %copy-start.14 = (f32[16,512]{1,0:T(8,128)S(1)}, f32[16,512]{1,0:T(8,128)}, u32[]{:S(2)}) copy-start(f32[16,512]{1,0:T(8,128)} %param.9) | copy-start | bytes 98308
  6.5 3.1 %collective-permute-start = (f32[2,16,512]{2,1,0:T(8,128)S(1)}, f32[2,16,512]{2,1,0:T(8,128)S(1)}, u32[]{:S(2)}, u32[]{:S(2)}) collective-permute-start(f32[2,16,512]{2,1,0:T(8,128)S(1)} %pad_maximum_fusion), channel_id=1, source_target_pairs={{0,16},{16,0},{32,48},{48,32},{64,80},{80,64},{96,112},{112,96},{1... | collective-permute-start | bytes 196616 | tf_op jit(solution)/shard_map/ppermute | solution.py:121
  9.7 6.2 %collective-permute-start.1 = (f32[2,16,512]{2,1,0:T(8,128)S(1)}, f32[2,16,512]{2,1,0:T(8,128)S(1)}, u32[]{:S(2)}, u32[]{:S(2)}) collective-permute-start(f32[2,16,512]{2,1,0:T(8,128)S(1)} %pad_maximum_fusion.1), channel_id=1, source_target_pairs={{0,32},{16,48},{32,0},{48,16},{64,96},{80,112},{96,64},{112,80},{1... | collective-permute-start | bytes 196616 | tf_op jit(solution)/shard_map/ppermute | solution.py:121
  16.0 11.8 %collective-permute-start.2 = (f32[2,16,512]{2,1,0:T(8,128)S(1)}, f32[2,16,512]{2,1,0:T(8,128)S(1)}, u32[]{:S(2)}, u32[]{:S(2)}) collective-permute-start(f32[2,16,512]{2,1,0:T(8,128)S(1)} %pad_maximum_fusion.2), channel_id=1, source_target_pairs={{0,64},{16,80},{32,96},{48,112},{64,0},{80,16},{96,32},{112,48},{1... | collective-permute-start | bytes 196616 | tf_op jit(solution)/shard_map/ppermute | solution.py:121
  27.9 12.4 %collective-permute-start.3 = (f32[2,16,512]{2,1,0:T(8,128)S(1)}, f32[2,16,512]{2,1,0:T(8,128)S(1)}, u32[]{:S(2)}, u32[]{:S(2)}) collective-permute-start(f32[2,16,512]{2,1,0:T(8,128)S(1)} %pad_maximum_fusion.3), channel_id=1, source_target_pairs={{0,192},{16,208},{32,224},{48,240},{64,128},{80,144},{96,160},{112... | collective-permute-start | bytes 196616 | tf_op jit(solution)/shard_map/ppermute | solution.py:121
  40.3 17.6 %collective-permute-start.4 = (f32[2,16,512]{2,1,0:T(8,128)S(1)}, f32[2,16,512]{2,1,0:T(8,128)S(1)}, u32[]{:S(2)}, u32[]{:S(2)}) collective-permute-start(f32[2,16,512]{2,1,0:T(8,128)S(1)} %pad_maximum_fusion.4), channel_id=1, source_target_pairs={{0,256},{16,272},{32,288},{48,304},{64,320},{80,336},{96,352},{112... | collective-permute-start | bytes 196616 | tf_op jit(solution)/shard_map/ppermute | solution.py:121
  58.0 17.9 %collective-permute-start.5 = (f32[2,16,512]{2,1,0:T(8,128)S(1)}, f32[2,16,512]{2,1,0:T(8,128)S(1)}, u32[]{:S(2)}, u32[]{:S(2)}) collective-permute-start(f32[2,16,512]{2,1,0:T(8,128)S(1)} %pad_maximum_fusion.5), channel_id=1, source_target_pairs={{0,768},{16,784},{32,800},{48,816},{64,832},{80,848},{96,864},{112... | collective-permute-start | bytes 196616 | tf_op jit(solution)/shard_map/ppermute | solution.py:121
  69.0 6.8 %copy-start.4 = (f32[256,512]{1,0:T(8,128)S(1)}, f32[256,512]{1,0:T(8,128)}, u32[]{:S(2)}) copy-start(f32[256,512]{1,0:T(8,128)} %shard_map.93) | copy-start | bytes 1572868
  69.1 6.8 %copy-start.5 = (f32[256,512]{1,0:T(8,128)S(1)}, f32[256,512]{1,0:T(8,128)}, u32[]{:S(2)}) copy-start(f32[256,512]{1,0:T(8,128)} %shard_map.94) | copy-start | bytes 1572868
  75.9 3.4 %copy-start.3 = (f32[16,512]{1,0:T(8,128)S(1)}, f32[16,512]{1,0:T(8,128)}, u32[]{:S(2)}) copy-start(f32[16,512]{1,0:T(8,128)} %rates_ref.3) | copy-start | bytes 98308
  76.6 6.1 %copy-start.7 = (f32[256,512]{1,0:T(8,128)S(1)}, f32[256,512]{1,0:T(8,128)}, u32[]{:S(2)}) copy-start(f32[256,512]{1,0:T(8,128)} %shard_map.96) | copy-start | bytes 1572868
  79.4 3.4 %copy-start.6 = (f32[256,512]{1,0:T(8,128)S(1)}, f32[256,512]{1,0:T(8,128)}, u32[]{:S(2)}) copy-start(f32[256,512]{1,0:T(8,128)} %shard_map.95) | copy-start | bytes 1572868
  82.7 1.0 %copy-start.9 = (f32[256,512]{1,0:T(8,128)S(1)}, f32[256,512]{1,0:T(8,128)}, u32[]{:S(2)}) copy-start(f32[256,512]{1,0:T(8,128)} %shard_map.98) | copy-start | bytes 1572868
  83.9 1.0 %copy-start.8 = (f32[256,512]{1,0:T(8,128)S(1)}, f32[256,512]{1,0:T(8,128)}, u32[]{:S(2)}) copy-start(f32[256,512]{1,0:T(8,128)} %shard_map.97) | copy-start | bytes 1572868
  83.9 1.1 %copy-start.10 = (bf16[256,512]{1,0:T(8,128)(2,1)S(1)}, bf16[256,512]{1,0:T(8,128)(2,1)}, u32[]{:S(2)}) copy-start(bf16[256,512]{1,0:T(8,128)(2,1)} %param.7) | copy-start | bytes 786436
  83.9 1.2 %copy-start.11 = (bf16[256,512]{1,0:T(8,128)(2,1)S(1)}, bf16[256,512]{1,0:T(8,128)(2,1)}, u32[]{:S(2)}) copy-start(bf16[256,512]{1,0:T(8,128)(2,1)} %param.6) | copy-start | bytes 786436

commit v8 on v7

--- a/solution.py
+++ b/solution.py
@@ -48,30 +48,32 @@
     return pieces.reshape(length // BLOCK, BLOCK, width)
 
 
-def carried_kernel(weights_ref, rates_ref, out_ref):
-    length, width = out_ref.shape
+def carried_kernel(fwd_ref, bwd_ref, scaled_ref, rates_ref, fwd_out, bwd_out):
+    length, width = fwd_out.shape
     order = rates_ref.shape[0]
     lags = lax.broadcasted_iota(jnp.int32, (BLOCK, width), 0).astype(jnp.float32) + 1.0
-    out_ref[...] = jnp.zeros(out_ref.shape, jnp.float32)
+    fwd_out[...] = jnp.zeros(fwd_out.shape, jnp.float32)
+    bwd_out[...] = jnp.zeros(bwd_out.shape, jnp.float32)
 
     def mode(m, carry):
         rate = rates_ref[pl.ds(m, 1), :]
-        weight = weights_ref[pl.ds(m, 1), :]
+        weight = scaled_ref[pl.ds(m, 1), :]
+        fwd_weight = weight * fwd_ref[pl.ds(m, 1), :]
+        bwd_weight = weight * bwd_ref[pl.ds(m, 1), :]
         after = jnp.exp(-rate * lags)
         for b in range(length // BLOCK):
             rows = pl.ds(b * BLOCK, BLOCK)
-            out_ref[rows, :] += after * (weight * jnp.exp(-rate * float(b * BLOCK)))
+            start = jnp.exp(-rate * float(b * BLOCK))
+            fwd_out[rows, :] += after * (fwd_weight * start)
+            bwd_out[rows, :] += after * (bwd_weight * start)
         return carry
 
     lax.fori_loop(0, order, mode, 0)
 
 
-def apply_incoming(pieces, incoming, scaled, rates):
-    count, _, width = pieces.shape
-    extra = pl.pallas_call(
-        carried_kernel, out_shape=jax.ShapeDtypeStruct((count * BLOCK, width), jnp.float32)
-    )(scaled * incoming, rates)
-    return pieces.reshape(count * BLOCK, width) + extra
+def carried(fwd_in, bwd_in, scaled, rates, length):
+    shape = jax.ShapeDtypeStruct((length, fwd_in.shape[1]), jnp.float32)
+    return pl.pallas_call(carried_kernel, out_shape=(shape, shape))(fwd_in, bwd_in, scaled, rates)
 
 
 def end_state(signal, rates):
@@ -164,8 +166,9 @@
     )
     fwd_pieces = cover[0] + cover[1]
     bwd_pieces = cover[2] + cover[3]
-    mixed = apply_incoming(fwd_pieces, fwd_in, scaled, rates)
-    back = apply_incoming(bwd_pieces, bwd_in, scaled, rates)[::-1]
+    fwd_extra, bwd_extra = carried(fwd_in, bwd_in, scaled, rates, length)
+    mixed = fwd_pieces.reshape(length, -1) + fwd_extra
+    back = (bwd_pieces.reshape(length, -1) + bwd_extra)[::-1]
     output = (value_f * mixed).astype(jnp.bfloat16)
     grad_value = (cot_f * mixed).astype(jnp.bfloat16)
     grad_query = (back * key_f).astype(jnp.bfloat16)

time: 86.9 us -> 87 us (level)
  other arithmetic: 7.24 us -> 9.06 us
  Pallas kernels: 32.3 us -> 30.5 us
    convert_element_type x0 -> x1, other arithmetic: none -> 2.2 us  [per_device(): grad_value = (cot_f * mixed).astype(jnp.bfloat16)]
    pallas_call x2 -> x1, Pallas kernels: 5.42 us -> 3.67 us  [carried(): pl.pallas_call(carried_kernel, out_shape=(shape, shape))]
    mul x2 -> x0, other arithmetic: 1.34 us -> none  [apply_incoming(): scaled * incoming]
    add x1 -> x2, other arithmetic: 0.08 us -> 1.33 us  [the longest x1 0.67 us: incoming_states(): bwd_in + jnp.where(upper, 0.0, jnp.exp(-rates * (length * (span - 1.0 - o...]
    unnamed x30 -> x26, local copies, waits for them, and re-layouts: 3.09 us -> 3.13 us
where the time goes in v8:
time: 87 us; the launch traced here: 86.3 us
  starting transfers between devices  37.4 us (43%)
  Pallas kernels  30.5 us (35%)
  other arithmetic  9.06 us (10%)
  local copies, waits for them, and re-layouts  4.91 us (6%)
  waiting for transfers between devices  3.27 us (4%)
  between operations  1.11 us (1%)
    ppermute x6, starting transfers between devices, incoming_states(): lax.ppermute(jnp.stack([fwd_total, bwd_total]), 'ctx', [(i, partner(i, sp...  37.4 us
    pallas_call x4, Pallas kernels, local_pass(): pl.pallas_call(local_kernel, out_shape=jax.ShapeDtypeStruct((length, widt...  26.9 us
    pallas_call x1, Pallas kernels, carried(): pl.pallas_call(carried_kernel, out_shape=(shape, shape))  3.67 us
    ppermute x6, waiting for transfers between devices, incoming_states(): lax.ppermute(jnp.stack([fwd_total, bwd_total]), 'ctx', [(i, partner(i, sp...  3.27 us
    unnamed x26, local copies, waits for them, and re-layouts  3.13 us
    convert_element_type x1, other arithmetic, per_device(): grad_value = (cot_f * mixed).astype(jnp.bfloat16)  2.2 us
    reduce_sum x2, other arithmetic, end_state(): return jnp.sum(outer * jnp.sum(inner[None] * rows, axis=1), axis=0)  2.14 us
  transfers between devices with their start and end apart: 6, of which 2 were waited for; matrix products, arithmetic and copies ran while one was open for 2% of the time, Pallas kernels for 31%

profile of v8, /device:TPU:6, one launch (start us, length us, event | category | flops | bytes accessed | tf_op | source)
XLA Modules:
  0.0 86.3 jit_solution(15132273734997768409)
XLA Ops:
  0.7 0.8 neg.5
  1.4 1.1 %fusion.2 = bf16[256,512]{1,0:T(8,128)(2,1)S(1)} fusion(bf16[256,512]{1,0:T(8,128)(2,1)} %param.7, bf16[256,512]{1,0:T(8,128)(2,1)} %param.6), kind=kLoop, calls=%fused_computation.10 | loop fusion | flops 524288 | bytes 786432 | tf_op jit(solution)/shard_map/convert_element_type | solution.py:151
  2.6 0.9 %copy-done.7 = bf16[256,512]{1,0:T(8,128)(2,1)S(1)} copy-done((bf16[256,512]{1,0:T(8,128)(2,1)S(1)}, bf16[256,512]{1,0:T(8,128)(2,1)}, u32[]{:S(2)}) %copy-start.7) | copy-done | bytes 262168
  3.6 0.3 rev.6.signal_ref
  3.9 0.1 multiply_exponential_fusion
  4.1 0.3 copy-done.1
  4.4 1.9 %multiply_reduce_fusion.1 = (f32[16,16,512]{2,1,0:T(8,128)S(1)}, f32[16,16,512]{2,1,0:T(8,128)S(1)}) fusion(f32[16,16,512]{2,1,0:T(8,128)S(1)} %bitcast.169, f32[16,16,512]{2,1,0:T(8,128)S(1)} %multiply_exponential_fusion, f32[16,16,512]{2,1,0:T(8,128)S(1)} %bitcast.168), kind=kLoop, calls=%fused_computation.1 | loop fusion | flops 8126464 | bytes 2621440 | tf_op jit(solution)/shard_map/reduce_sum | solution.py:86
  6.4 0.2 multiply_reduce_fusion.3
  6.6 1.9 %collective-permute-start = (f32[2,16,512]{2,1,0:T(8,128)S(1)}, f32[2,16,512]{2,1,0:T(8,128)S(1)}, u32[]{:S(2)}, u32[]{:S(2)}) collective-permute-start(f32[2,16,512]{2,1,0:T(8,128)S(1)} %pad_maximum_fusion), channel_id=1, source_target_pairs={{0,16},{16,0},{32,48},{48,32},{64,80},{80,64},{96,112},{112,96},{1... | collective-permute-start | bytes 196616 | tf_op jit(solution)/shard_map/ppermute | solution.py:123
  8.5 1.2 %collective-permute-done = f32[2,16,512]{2,1,0:T(8,128)S(1)} collective-permute-done((f32[2,16,512]{2,1,0:T(8,128)S(1)}, f32[2,16,512]{2,1,0:T(8,128)S(1)}, u32[]{:S(2)}, u32[]{:S(2)}) %collective-permute-start) | collective-permute-done | bytes 65568 | tf_op jit(solution)/shard_map/ppermute | solution.py:123
  9.8 3.5 %collective-permute-start.1 = (f32[2,16,512]{2,1,0:T(8,128)S(1)}, f32[2,16,512]{2,1,0:T(8,128)S(1)}, u32[]{:S(2)}, u32[]{:S(2)}) collective-permute-start(f32[2,16,512]{2,1,0:T(8,128)S(1)} %pad_maximum_fusion.1), channel_id=1, source_target_pairs={{0,32},{16,48},{32,0},{48,16},{64,96},{80,112},{96,64},{112,80},{1... | collective-permute-start | bytes 196616 | tf_op jit(solution)/shard_map/ppermute | solution.py:123
  13.3 0.6 fusion.31
  13.9 2.1 %collective-permute-done.1 = f32[2,16,512]{2,1,0:T(8,128)S(1)} collective-permute-done((f32[2,16,512]{2,1,0:T(8,128)S(1)}, f32[2,16,512]{2,1,0:T(8,128)S(1)}, u32[]{:S(2)}, u32[]{:S(2)}) %collective-permute-start.1) | collective-permute-done | bytes 65568 | tf_op jit(solution)/shard_map/ppermute | solution.py:123
  16.0 4.5 %collective-permute-start.2 = (f32[2,16,512]{2,1,0:T(8,128)S(1)}, f32[2,16,512]{2,1,0:T(8,128)S(1)}, u32[]{:S(2)}, u32[]{:S(2)}) collective-permute-start(f32[2,16,512]{2,1,0:T(8,128)S(1)} %pad_maximum_fusion.2), channel_id=1, source_target_pairs={{0,64},{16,80},{32,96},{48,112},{64,0},{80,16},{96,32},{112,48},{1... | collective-permute-start | bytes 196616 | tf_op jit(solution)/shard_map/ppermute | solution.py:123
  20.5 0.6 fusion.32
  21.1 6.7 %shard_map.93 = f32[256,512]{1,0:T(8,128)} custom-call(f32[256,512]{1,0:T(8,128)} %copy-done.1, f32[8,512]{1,0:T(8,128)} %get-tuple-element.45.scaled_ref, f32[8,512]{1,0:T(8,128)} %get-tuple-element.43.rates_ref), custom_call_target="tpu_custom_call" | custom-call | tf_op jit(solution)/shard_map/pallas_call | solution.py:45
  27.9 5.7 %collective-permute-start.3 = (f32[2,16,512]{2,1,0:T(8,128)S(1)}, f32[2,16,512]{2,1,0:T(8,128)S(1)}, u32[]{:S(2)}, u32[]{:S(2)}) collective-permute-start(f32[2,16,512]{2,1,0:T(8,128)S(1)} %pad_maximum_fusion.3), channel_id=1, source_target_pairs={{0,192},{16,208},{32,224},{48,240},{64,128},{80,144},{96,160},{112... | collective-permute-start | bytes 196616 | tf_op jit(solution)/shard_map/ppermute | solution.py:123
  33.6 6.7 %shard_map.94 = f32[256,512]{1,0:T(8,128)} custom-call(f32[256,512]{1,0:T(8,128)} %copy-done.1, f32[8,512]{1,0:T(8,128)} %get-tuple-element.44.scaled_ref, f32[8,512]{1,0:T(8,128)} %get-tuple-element.42.rates_ref), custom_call_target="tpu_custom_call" | custom-call | tf_op jit(solution)/shard_map/pallas_call | solution.py:45
  40.4 10.9 %collective-permute-start.4 = (f32[2,16,512]{2,1,0:T(8,128)S(1)}, f32[2,16,512]{2,1,0:T(8,128)S(1)}, u32[]{:S(2)}, u32[]{:S(2)}) collective-permute-start(f32[2,16,512]{2,1,0:T(8,128)S(1)} %pad_maximum_fusion.4), channel_id=1, source_target_pairs={{0,256},{16,272},{32,288},{48,304},{64,320},{80,336},{96,352},{112... | collective-permute-start | bytes 196616 | tf_op jit(solution)/shard_map/ppermute | solution.py:123
  51.3 6.7 %shard_map.95 = f32[256,512]{1,0:T(8,128)} custom-call(f32[256,512]{1,0:T(8,128)} %copy-done, f32[8,512]{1,0:T(8,128)} %get-tuple-element.45.scaled_ref, f32[8,512]{1,0:T(8,128)} %get-tuple-element.43.rates_ref), custom_call_target="tpu_custom_call" | custom-call | tf_op jit(solution)/shard_map/pallas_call | solution.py:45
  58.1 10.9 %collective-permute-start.5 = (f32[2,16,512]{2,1,0:T(8,128)S(1)}, f32[2,16,512]{2,1,0:T(8,128)S(1)}, u32[]{:S(2)}, u32[]{:S(2)}) collective-permute-start(f32[2,16,512]{2,1,0:T(8,128)S(1)} %pad_maximum_fusion.5), channel_id=1, source_target_pairs={{0,768},{16,784},{32,800},{48,816},{64,832},{80,848},{96,864},{112... | collective-permute-start | bytes 196616 | tf_op jit(solution)/shard_map/ppermute | solution.py:123
  69.1 6.8 %shard_map.96 = f32[256,512]{1,0:T(8,128)} custom-call(f32[256,512]{1,0:T(8,128)} %copy-done, f32[8,512]{1,0:T(8,128)} %get-tuple-element.44.scaled_ref, f32[8,512]{1,0:T(8,128)} %get-tuple-element.42.rates_ref), custom_call_target="tpu_custom_call" | custom-call | tf_op jit(solution)/shard_map/pallas_call | solution.py:45
  75.9 0.1 add.156
  76.0 0.9 %copy-done.5 = f32[256,512]{1,0:T(8,128)S(1)} copy-done((f32[256,512]{1,0:T(8,128)S(1)}, f32[256,512]{1,0:T(8,128)}, u32[]{:S(2)}) %copy-start.5) | copy-done | bytes 524312
  77.0 0.2 copy-done.6
  77.2 0.7 fusion.5.bwd_ref
  77.9 0.7 fusion.6.fwd_ref
  78.5 3.7 %shard_map.97 = (f32[256,512]{1,0:T(8,128)}, f32[256,512]{1,0:T(8,128)}) custom-call(f32[16,512]{1,0:T(8,128)} %fusion.6.fwd_ref, f32[16,512]{1,0:T(8,128)} %fusion.5.bwd_ref, f32[16,512]{1,0:T(8,128)} %copy-done.11, f32[16,512]{1,0:T(8,128)} %rates_ref.1), custom_call_target="tpu_custom_call" | custom-call | tf_op jit(solution)/shard_map/pallas_call | solution.py:76
  82.2 2.2 %fusion.4 = (bf16[256,512]{1,0:T(8,128)(2,1)}, bf16[256,512]{1,0:T(8,128)(2,1)}, f32[256,512]{1,0:T(8,128)S(1)}) fusion(bf16[256,512]{1,0:T(8,128)(2,1)S(1)} %copy-done.7, f32[256,512]{1,0:T(8,128)} %get-tuple-element.20, f32[4,64,512]{2,1,0:T(8,128)S(1)} %add.156, bf16[256,512]{1,0:T(8,128)(2,1)S(1)} %copy-done.8, f32[256,512]{1,0:T(8,128)} %get-tuple-element.23, ...), kind=kLoop, calls=%fused_computation.12 | loop fusion | flops 1048576 | bytes 3670016 | tf_op jit(solution)/shard_map/convert_element_type | solution.py:173
  84.4 0.3 rev.7
  84.7 0.7 copy-done.9
  85.4 0.9 %fusion.1 = (bf16[256,512]{1,0:T(8,128)(2,1)}, bf16[256,512]{1,0:T(8,128)(2,1)}) fusion(f32[256,512]{1,0:T(8,128)S(1)} %rev.7, bf16[256,512]{1,0:T(8,128)(2,1)S(1)} %copy-done.10, bf16[256,512]{1,0:T(8,128)(2,1)S(1)} %copy-done.9), kind=kLoop, calls=%fused_computation.9 | loop fusion | flops 786432 | bytes 1572864 | tf_op jit(solution)/shard_map/convert_element_type | solution.py:175
  (41 shorter events, 0.6 us)
Async XLA Ops:
  2.5 1.0 %copy-start.7 = (bf16[256,512]{1,0:T(8,128)(2,1)S(1)}, bf16[256,512]{1,0:T(8,128)(2,1)}, u32[]{:S(2)}) copy-start(bf16[256,512]{1,0:T(8,128)(2,1)} %param.11) | copy-start | bytes 786436
  2.5 1.0 %copy-start.8 = (bf16[256,512]{1,0:T(8,128)(2,1)S(1)}, bf16[256,512]{1,0:T(8,128)(2,1)}, u32[]{:S(2)}) copy-start(bf16[256,512]{1,0:T(8,128)(2,1)} %param.8) | copy-start | bytes 786436
  3.5 0.8 copy-start.1
  3.9 2.4 %copy-start = (f32[256,512]{1,0:T(8,128)}, f32[256,512]{1,0:T(8,128)S(1)}, u32[]{:S(2)}) copy-start(f32[256,512]{1,0:T(8,128)S(1)} %rev.6.signal_ref) | copy-start | bytes 1572868
  6.3 3.4 %copy-start.2 = (f32[16,512]{1,0:T(8,128)S(1)}, f32[16,512]{1,0:T(8,128)}, u32[]{:S(2)}) copy-start(f32[16,512]{1,0:T(8,128)} %rates_ref.1) | copy-start | bytes 98308
  6.6 9.4 %copy-start.12 = (f32[16,512]{1,0:T(8,128)S(1)}, f32[16,512]{1,0:T(8,128)}, u32[]{:S(2)}) copy-start(f32[16,512]{1,0:T(8,128)} %param.9) | copy-start | bytes 98308
  6.6 3.1 %collective-permute-start = (f32[2,16,512]{2,1,0:T(8,128)S(1)}, f32[2,16,512]{2,1,0:T(8,128)S(1)}, u32[]{:S(2)}, u32[]{:S(2)}) collective-permute-start(f32[2,16,512]{2,1,0:T(8,128)S(1)} %pad_maximum_fusion), channel_id=1, source_target_pairs={{0,16},{16,0},{32,48},{48,32},{64,80},{80,64},{96,112},{112,96},{1... | collective-permute-start | bytes 196616 | tf_op jit(solution)/shard_map/ppermute | solution.py:123
  9.8 6.2 %collective-permute-start.1 = (f32[2,16,512]{2,1,0:T(8,128)S(1)}, f32[2,16,512]{2,1,0:T(8,128)S(1)}, u32[]{:S(2)}, u32[]{:S(2)}) collective-permute-start(f32[2,16,512]{2,1,0:T(8,128)S(1)} %pad_maximum_fusion.1), channel_id=1, source_target_pairs={{0,32},{16,48},{32,0},{48,16},{64,96},{80,112},{96,64},{112,80},{1... | collective-permute-start | bytes 196616 | tf_op jit(solution)/shard_map/ppermute | solution.py:123
  16.0 11.8 %copy-start.11 = (f32[16,512]{1,0:T(8,128)}, f32[16,512]{1,0:T(8,128)S(1)}, u32[]{:S(2)}) copy-start(f32[16,512]{1,0:T(8,128)S(1)} %get-tuple-element.46.scaled_ref) | copy-start | bytes 98308
  16.0 11.8 %collective-permute-start.2 = (f32[2,16,512]{2,1,0:T(8,128)S(1)}, f32[2,16,512]{2,1,0:T(8,128)S(1)}, u32[]{:S(2)}, u32[]{:S(2)}) collective-permute-start(f32[2,16,512]{2,1,0:T(8,128)S(1)} %pad_maximum_fusion.2), channel_id=1, source_target_pairs={{0,64},{16,80},{32,96},{48,112},{64,0},{80,16},{96,32},{112,48},{1... | collective-permute-start | bytes 196616 | tf_op jit(solution)/shard_map/ppermute | solution.py:123
  27.9 12.5 %collective-permute-start.3 = (f32[2,16,512]{2,1,0:T(8,128)S(1)}, f32[2,16,512]{2,1,0:T(8,128)S(1)}, u32[]{:S(2)}, u32[]{:S(2)}) collective-permute-start(f32[2,16,512]{2,1,0:T(8,128)S(1)} %pad_maximum_fusion.3), channel_id=1, source_target_pairs={{0,192},{16,208},{32,224},{48,240},{64,128},{80,144},{96,160},{112... | collective-permute-start | bytes 196616 | tf_op jit(solution)/shard_map/ppermute | solution.py:123
  40.4 17.7 %collective-permute-start.4 = (f32[2,16,512]{2,1,0:T(8,128)S(1)}, f32[2,16,512]{2,1,0:T(8,128)S(1)}, u32[]{:S(2)}, u32[]{:S(2)}) collective-permute-start(f32[2,16,512]{2,1,0:T(8,128)S(1)} %pad_maximum_fusion.4), channel_id=1, source_target_pairs={{0,256},{16,272},{32,288},{48,304},{64,320},{80,336},{96,352},{112... | collective-permute-start | bytes 196616 | tf_op jit(solution)/shard_map/ppermute | solution.py:123
  58.1 17.9 %collective-permute-start.5 = (f32[2,16,512]{2,1,0:T(8,128)S(1)}, f32[2,16,512]{2,1,0:T(8,128)S(1)}, u32[]{:S(2)}, u32[]{:S(2)}) collective-permute-start(f32[2,16,512]{2,1,0:T(8,128)S(1)} %pad_maximum_fusion.5), channel_id=1, source_target_pairs={{0,768},{16,784},{32,800},{48,816},{64,832},{80,848},{96,864},{112... | collective-permute-start | bytes 196616 | tf_op jit(solution)/shard_map/ppermute | solution.py:123
  69.1 6.8 %copy-start.3 = (f32[256,512]{1,0:T(8,128)S(1)}, f32[256,512]{1,0:T(8,128)}, u32[]{:S(2)}) copy-start(f32[256,512]{1,0:T(8,128)} %shard_map.93) | copy-start | bytes 1572868
  69.1 6.8 %copy-start.4 = (f32[256,512]{1,0:T(8,128)S(1)}, f32[256,512]{1,0:T(8,128)}, u32[]{:S(2)}) copy-start(f32[256,512]{1,0:T(8,128)} %shard_map.94) | copy-start | bytes 1572868
  75.9 1.0 %copy-start.5 = (f32[256,512]{1,0:T(8,128)S(1)}, f32[256,512]{1,0:T(8,128)}, u32[]{:S(2)}) copy-start(f32[256,512]{1,0:T(8,128)} %shard_map.95) | copy-start | bytes 1572868
  75.9 1.2 %copy-start.6 = (f32[256,512]{1,0:T(8,128)S(1)}, f32[256,512]{1,0:T(8,128)}, u32[]{:S(2)}) copy-start(f32[256,512]{1,0:T(8,128)} %shard_map.96) | copy-start | bytes 1572868
  84.4 0.9 %copy-start.9 = (bf16[256,512]{1,0:T(8,128)(2,1)S(1)}, bf16[256,512]{1,0:T(8,128)(2,1)}, u32[]{:S(2)}) copy-start(bf16[256,512]{1,0:T(8,128)(2,1)} %param.7) | copy-start | bytes 786436
  84.4 1.0 %copy-start.10 = (bf16[256,512]{1,0:T(8,128)(2,1)S(1)}, bf16[256,512]{1,0:T(8,128)(2,1)}, u32[]{:S(2)}) copy-start(bf16[256,512]{1,0:T(8,128)(2,1)} %param.6) | copy-start | bytes 786436

commit v9 on v8

--- a/solution.py
+++ b/solution.py
@@ -14,7 +14,7 @@
     lower = (
         lax.broadcasted_iota(jnp.int32, (BLOCK, BLOCK), 0)
         >= lax.broadcasted_iota(jnp.int32, (BLOCK, BLOCK), 1)
-    ).astype(jnp.float32)
+    ).astype(jnp.bfloat16)
     out_ref[...] = jnp.zeros(out_ref.shape, jnp.float32)
 
     def mode(m, carry):
@@ -26,11 +26,11 @@
         state = jnp.zeros((1, width), jnp.float32)
         for b in range(length // BLOCK):
             rows = pl.ds(b * BLOCK, BLOCK)
-            summed = jnp.dot(
-                lower,
-                rising * signal_ref[rows, :],
-                precision=lax.Precision.HIGHEST,
-                preferred_element_type=jnp.float32,
+            lifted = rising * signal_ref[rows, :]
+            high = lifted.astype(jnp.bfloat16)
+            low = (lifted - high.astype(jnp.float32)).astype(jnp.bfloat16)
+            summed = jnp.dot(lower, high, preferred_element_type=jnp.float32) + jnp.dot(
+                lower, low, preferred_element_type=jnp.float32
             )
             states = falling * (summed + step_decay * state)
             out_ref[rows, :] += weight * states

time: 87 us -> 80.1 us (0.921)
  Pallas kernels: 30.5 us -> 21.6 us
  starting transfers between devices: 37.4 us -> 39.5 us
    pallas_call x4, Pallas kernels: 26.9 us -> 18 us  [local_pass(): pl.pallas_call(local_kernel, out_shape=jax.ShapeDtypeStruct((length, widt...]
    ppermute x6, starting transfers between devices: 37.4 us -> 39.5 us  [incoming_states(): lax.ppermute(jnp.stack([fwd_total, bwd_total]), 'ctx', [(i, partner(i, sp...]
  transfers between devices with their start and end apart: 6 -> 6, of which waited for: 2 -> 2; matrix products, arithmetic and copies ran while one was open for 2% -> 2% of each run, Pallas kernels for 31% -> 23%
where the time goes in v9:
time: 80.1 us; the launch traced here: 79.5 us
  starting transfers between devices  39.5 us (49%)
  Pallas kernels  21.6 us (27%)
  other arithmetic  9.06 us (11%)
  local copies, waits for them, and re-layouts  4.91 us (6%)
  waiting for transfers between devices  3.27 us (4%)
  between operations  1.11 us (1%)
    ppermute x6, starting transfers between devices, incoming_states(): lax.ppermute(jnp.stack([fwd_total, bwd_total]), 'ctx', [(i, partner(i, sp...  39.5 us
    pallas_call x4, Pallas kernels, local_pass(): pl.pallas_call(local_kernel, out_shape=jax.ShapeDtypeStruct((length, widt...  18 us
    pallas_call x1, Pallas kernels, carried(): pl.pallas_call(carried_kernel, out_shape=(shape, shape))  3.67 us
    ppermute x6, waiting for transfers between devices, incoming_states(): lax.ppermute(jnp.stack([fwd_total, bwd_total]), 'ctx', [(i, partner(i, sp...  3.27 us
    unnamed x26, local copies, waits for them, and re-layouts  3.13 us
    convert_element_type x1, other arithmetic, per_device(): grad_value = (cot_f * mixed).astype(jnp.bfloat16)  2.2 us
    reduce_sum x2, other arithmetic, end_state(): return jnp.sum(outer * jnp.sum(inner[None] * rows, axis=1), axis=0)  2.14 us
  transfers between devices with their start and end apart: 6, of which 2 were waited for; matrix products, arithmetic and copies ran while one was open for 2% of the time, Pallas kernels for 23%

profile of v9, /device:TPU:6, one launch (start us, length us, event | category | flops | bytes accessed | tf_op | source)
XLA Modules:
  0.0 79.5 jit_solution(11560956819219407290)
XLA Ops:
  0.7 0.8 neg.5
  1.4 1.1 %fusion.2 = bf16[256,512]{1,0:T(8,128)(2,1)S(1)} fusion(bf16[256,512]{1,0:T(8,128)(2,1)} %param.7, bf16[256,512]{1,0:T(8,128)(2,1)} %param.6), kind=kLoop, calls=%fused_computation.10 | loop fusion | flops 524288 | bytes 786432 | tf_op jit(solution)/shard_map/convert_element_type | solution.py:151
  2.6 0.9 %copy-done.7 = bf16[256,512]{1,0:T(8,128)(2,1)S(1)} copy-done((bf16[256,512]{1,0:T(8,128)(2,1)S(1)}, bf16[256,512]{1,0:T(8,128)(2,1)}, u32[]{:S(2)}) %copy-start.7) | copy-done | bytes 262168
  3.6 0.3 rev.6.signal_ref
  3.9 0.1 multiply_exponential_fusion
  4.1 0.3 copy-done.1
  4.4 1.9 %multiply_reduce_fusion.1 = (f32[16,16,512]{2,1,0:T(8,128)S(1)}, f32[16,16,512]{2,1,0:T(8,128)S(1)}) fusion(f32[16,16,512]{2,1,0:T(8,128)S(1)} %bitcast.169, f32[16,16,512]{2,1,0:T(8,128)S(1)} %multiply_exponential_fusion, f32[16,16,512]{2,1,0:T(8,128)S(1)} %bitcast.168), kind=kLoop, calls=%fused_computation.1 | loop fusion | flops 8126464 | bytes 2621440 | tf_op jit(solution)/shard_map/reduce_sum | solution.py:86
  6.4 0.2 multiply_reduce_fusion.3
  6.6 1.9 %collective-permute-start = (f32[2,16,512]{2,1,0:T(8,128)S(1)}, f32[2,16,512]{2,1,0:T(8,128)S(1)}, u32[]{:S(2)}, u32[]{:S(2)}) collective-permute-start(f32[2,16,512]{2,1,0:T(8,128)S(1)} %pad_maximum_fusion), channel_id=1, source_target_pairs={{0,16},{16,0},{32,48},{48,32},{64,80},{80,64},{96,112},{112,96},{1... | collective-permute-start | bytes 196616 | tf_op jit(solution)/shard_map/ppermute | solution.py:123
  8.5 1.2 %collective-permute-done = f32[2,16,512]{2,1,0:T(8,128)S(1)} collective-permute-done((f32[2,16,512]{2,1,0:T(8,128)S(1)}, f32[2,16,512]{2,1,0:T(8,128)S(1)}, u32[]{:S(2)}, u32[]{:S(2)}) %collective-permute-start) | collective-permute-done | bytes 65568 | tf_op jit(solution)/shard_map/ppermute | solution.py:123
  9.8 3.5 %collective-permute-start.1 = (f32[2,16,512]{2,1,0:T(8,128)S(1)}, f32[2,16,512]{2,1,0:T(8,128)S(1)}, u32[]{:S(2)}, u32[]{:S(2)}) collective-permute-start(f32[2,16,512]{2,1,0:T(8,128)S(1)} %pad_maximum_fusion.1), channel_id=1, source_target_pairs={{0,32},{16,48},{32,0},{48,16},{64,96},{80,112},{96,64},{112,80},{1... | collective-permute-start | bytes 196616 | tf_op jit(solution)/shard_map/ppermute | solution.py:123
  13.3 0.6 fusion.31
  13.9 2.1 %collective-permute-done.1 = f32[2,16,512]{2,1,0:T(8,128)S(1)} collective-permute-done((f32[2,16,512]{2,1,0:T(8,128)S(1)}, f32[2,16,512]{2,1,0:T(8,128)S(1)}, u32[]{:S(2)}, u32[]{:S(2)}) %collective-permute-start.1) | collective-permute-done | bytes 65568 | tf_op jit(solution)/shard_map/ppermute | solution.py:123
  16.0 4.5 %collective-permute-start.2 = (f32[2,16,512]{2,1,0:T(8,128)S(1)}, f32[2,16,512]{2,1,0:T(8,128)S(1)}, u32[]{:S(2)}, u32[]{:S(2)}) collective-permute-start(f32[2,16,512]{2,1,0:T(8,128)S(1)} %pad_maximum_fusion.2), channel_id=1, source_target_pairs={{0,64},{16,80},{32,96},{48,112},{64,0},{80,16},{96,32},{112,48},{1... | collective-permute-start | bytes 196616 | tf_op jit(solution)/shard_map/ppermute | solution.py:123
  20.5 0.6 fusion.32
  21.1 4.5 %shard_map.93 = f32[256,512]{1,0:T(8,128)} custom-call(f32[256,512]{1,0:T(8,128)} %copy-done.1, f32[8,512]{1,0:T(8,128)} %get-tuple-element.45.scaled_ref, f32[8,512]{1,0:T(8,128)} %get-tuple-element.43.rates_ref), custom_call_target="tpu_custom_call" | custom-call | tf_op jit(solution)/shard_map/pallas_call | solution.py:45
  25.6 5.7 %collective-permute-start.3 = (f32[2,16,512]{2,1,0:T(8,128)S(1)}, f32[2,16,512]{2,1,0:T(8,128)S(1)}, u32[]{:S(2)}, u32[]{:S(2)}) collective-permute-start(f32[2,16,512]{2,1,0:T(8,128)S(1)} %pad_maximum_fusion.3), channel_id=1, source_target_pairs={{0,192},{16,208},{32,224},{48,240},{64,128},{80,144},{96,160},{112... | collective-permute-start | bytes 196616 | tf_op jit(solution)/shard_map/ppermute | solution.py:123
  31.4 4.5 %shard_map.94 = f32[256,512]{1,0:T(8,128)} custom-call(f32[256,512]{1,0:T(8,128)} %copy-done.1, f32[8,512]{1,0:T(8,128)} %get-tuple-element.44.scaled_ref, f32[8,512]{1,0:T(8,128)} %get-tuple-element.42.rates_ref), custom_call_target="tpu_custom_call" | custom-call | tf_op jit(solution)/shard_map/pallas_call | solution.py:45
  35.9 10.9 %collective-permute-start.4 = (f32[2,16,512]{2,1,0:T(8,128)S(1)}, f32[2,16,512]{2,1,0:T(8,128)S(1)}, u32[]{:S(2)}, u32[]{:S(2)}) collective-permute-start(f32[2,16,512]{2,1,0:T(8,128)S(1)} %pad_maximum_fusion.4), channel_id=1, source_target_pairs={{0,256},{16,272},{32,288},{48,304},{64,320},{80,336},{96,352},{112... | collective-permute-start | bytes 196616 | tf_op jit(solution)/shard_map/ppermute | solution.py:123
  46.9 4.5 %shard_map.95 = f32[256,512]{1,0:T(8,128)} custom-call(f32[256,512]{1,0:T(8,128)} %copy-done, f32[8,512]{1,0:T(8,128)} %get-tuple-element.45.scaled_ref, f32[8,512]{1,0:T(8,128)} %get-tuple-element.43.rates_ref), custom_call_target="tpu_custom_call" | custom-call | tf_op jit(solution)/shard_map/pallas_call | solution.py:45
  51.4 13.0 %collective-permute-start.5 = (f32[2,16,512]{2,1,0:T(8,128)S(1)}, f32[2,16,512]{2,1,0:T(8,128)S(1)}, u32[]{:S(2)}, u32[]{:S(2)}) collective-permute-start(f32[2,16,512]{2,1,0:T(8,128)S(1)} %pad_maximum_fusion.5), channel_id=1, source_target_pairs={{0,768},{16,784},{32,800},{48,816},{64,832},{80,848},{96,864},{112... | collective-permute-start | bytes 196616 | tf_op jit(solution)/shard_map/ppermute | solution.py:123
  64.5 4.5 %shard_map.96 = f32[256,512]{1,0:T(8,128)} custom-call(f32[256,512]{1,0:T(8,128)} %copy-done, f32[8,512]{1,0:T(8,128)} %get-tuple-element.44.scaled_ref, f32[8,512]{1,0:T(8,128)} %get-tuple-element.42.rates_ref), custom_call_target="tpu_custom_call" | custom-call | tf_op jit(solution)/shard_map/pallas_call | solution.py:45
  69.1 0.1 add.156
  69.2 0.9 %copy-done.5 = f32[256,512]{1,0:T(8,128)S(1)} copy-done((f32[256,512]{1,0:T(8,128)S(1)}, f32[256,512]{1,0:T(8,128)}, u32[]{:S(2)}) %copy-start.5) | copy-done | bytes 524312
  70.1 0.2 copy-done.6
  70.3 0.7 fusion.5.bwd_ref
  71.0 0.7 fusion.6.fwd_ref
  71.7 3.7 %shard_map.97 = (f32[256,512]{1,0:T(8,128)}, f32[256,512]{1,0:T(8,128)}) custom-call(f32[16,512]{1,0:T(8,128)} %fusion.6.fwd_ref, f32[16,512]{1,0:T(8,128)} %fusion.5.bwd_ref, f32[16,512]{1,0:T(8,128)} %copy-done.11, f32[16,512]{1,0:T(8,128)} %rates_ref.1), custom_call_target="tpu_custom_call" | custom-call | tf_op jit(solution)/shard_map/pallas_call | solution.py:76
  75.3 2.2 %fusion.4 = (bf16[256,512]{1,0:T(8,128)(2,1)}, bf16[256,512]{1,0:T(8,128)(2,1)}, f32[256,512]{1,0:T(8,128)S(1)}) fusion(bf16[256,512]{1,0:T(8,128)(2,1)S(1)} %copy-done.7, f32[256,512]{1,0:T(8,128)} %get-tuple-element.20, f32[4,64,512]{2,1,0:T(8,128)S(1)} %add.156, bf16[256,512]{1,0:T(8,128)(2,1)S(1)} %copy-done.8, f32[256,512]{1,0:T(8,128)} %get-tuple-element.23, ...), kind=kLoop, calls=%fused_computation.12 | loop fusion | flops 1048576 | bytes 3670016 | tf_op jit(solution)/shard_map/convert_element_type | solution.py:173
  77.5 0.3 rev.7
  77.8 0.7 copy-done.9
  78.6 0.9 %fusion.1 = (bf16[256,512]{1,0:T(8,128)(2,1)}, bf16[256,512]{1,0:T(8,128)(2,1)}) fusion(f32[256,512]{1,0:T(8,128)S(1)} %rev.7, bf16[256,512]{1,0:T(8,128)(2,1)S(1)} %copy-done.10, bf16[256,512]{1,0:T(8,128)(2,1)S(1)} %copy-done.9), kind=kLoop, calls=%fused_computation.9 | loop fusion | flops 786432 | bytes 1572864 | tf_op jit(solution)/shard_map/convert_element_type | solution.py:175
  (41 shorter events, 0.6 us)
Async XLA Ops:
  2.5 1.0 %copy-start.7 = (bf16[256,512]{1,0:T(8,128)(2,1)S(1)}, bf16[256,512]{1,0:T(8,128)(2,1)}, u32[]{:S(2)}) copy-start(bf16[256,512]{1,0:T(8,128)(2,1)} %param.11) | copy-start | bytes 786436
  2.5 1.0 %copy-start.8 = (bf16[256,512]{1,0:T(8,128)(2,1)S(1)}, bf16[256,512]{1,0:T(8,128)(2,1)}, u32[]{:S(2)}) copy-start(bf16[256,512]{1,0:T(8,128)(2,1)} %param.8) | copy-start | bytes 786436
  3.5 0.8 %copy-start.1 = (f32[256,512]{1,0:T(8,128)}, f32[256,512]{1,0:T(8,128)S(1)}, u32[]{:S(2)}) copy-start(f32[256,512]{1,0:T(8,128)S(1)} %convert_element_type.66.signal_ref) | copy-start | bytes 1572868
  3.9 2.4 %copy-start = (f32[256,512]{1,0:T(8,128)}, f32[256,512]{1,0:T(8,128)S(1)}, u32[]{:S(2)}) copy-start(f32[256,512]{1,0:T(8,128)S(1)} %rev.6.signal_ref) | copy-start | bytes 1572868
  6.3 3.4 %copy-start.2 = (f32[16,512]{1,0:T(8,128)S(1)}, f32[16,512]{1,0:T(8,128)}, u32[]{:S(2)}) copy-start(f32[16,512]{1,0:T(8,128)} %rates_ref.1) | copy-start | bytes 98308
  6.6 9.4 %copy-start.12 = (f32[16,512]{1,0:T(8,128)S(1)}, f32[16,512]{1,0:T(8,128)}, u32[]{:S(2)}) copy-start(f32[16,512]{1,0:T(8,128)} %param.9) | copy-start | bytes 98308
  6.6 3.1 %collective-permute-start = (f32[2,16,512]{2,1,0:T(8,128)S(1)}, f32[2,16,512]{2,1,0:T(8,128)S(1)}, u32[]{:S(2)}, u32[]{:S(2)}) collective-permute-start(f32[2,16,512]{2,1,0:T(8,128)S(1)} %pad_maximum_fusion), channel_id=1, source_target_pairs={{0,16},{16,0},{32,48},{48,32},{64,80},{80,64},{96,112},{112,96},{1... | collective-permute-start | bytes 196616 | tf_op jit(solution)/shard_map/ppermute | solution.py:123
  9.8 6.2 %collective-permute-start.1 = (f32[2,16,512]{2,1,0:T(8,128)S(1)}, f32[2,16,512]{2,1,0:T(8,128)S(1)}, u32[]{:S(2)}, u32[]{:S(2)}) collective-permute-start(f32[2,16,512]{2,1,0:T(8,128)S(1)} %pad_maximum_fusion.1), channel_id=1, source_target_pairs={{0,32},{16,48},{32,0},{48,16},{64,96},{80,112},{96,64},{112,80},{1... | collective-permute-start | bytes 196616 | tf_op jit(solution)/shard_map/ppermute | solution.py:123
  16.0 9.6 %copy-start.11 = (f32[16,512]{1,0:T(8,128)}, f32[16,512]{1,0:T(8,128)S(1)}, u32[]{:S(2)}) copy-start(f32[16,512]{1,0:T(8,128)S(1)} %get-tuple-element.46.scaled_ref) | copy-start | bytes 98308
  16.0 9.6 %collective-permute-start.2 = (f32[2,16,512]{2,1,0:T(8,128)S(1)}, f32[2,16,512]{2,1,0:T(8,128)S(1)}, u32[]{:S(2)}, u32[]{:S(2)}) collective-permute-start(f32[2,16,512]{2,1,0:T(8,128)S(1)} %pad_maximum_fusion.2), channel_id=1, source_target_pairs={{0,64},{16,80},{32,96},{48,112},{64,0},{80,16},{96,32},{112,48},{1... | collective-permute-start | bytes 196616 | tf_op jit(solution)/shard_map/ppermute | solution.py:123
  25.6 10.2 %collective-permute-start.3 = (f32[2,16,512]{2,1,0:T(8,128)S(1)}, f32[2,16,512]{2,1,0:T(8,128)S(1)}, u32[]{:S(2)}, u32[]{:S(2)}) collective-permute-start(f32[2,16,512]{2,1,0:T(8,128)S(1)} %pad_maximum_fusion.3), channel_id=1, source_target_pairs={{0,192},{16,208},{32,224},{48,240},{64,128},{80,144},{96,160},{112... | collective-permute-start | bytes 196616 | tf_op jit(solution)/shard_map/ppermute | solution.py:123
  35.9 15.4 %collective-permute-start.4 = (f32[2,16,512]{2,1,0:T(8,128)S(1)}, f32[2,16,512]{2,1,0:T(8,128)S(1)}, u32[]{:S(2)}, u32[]{:S(2)}) collective-permute-start(f32[2,16,512]{2,1,0:T(8,128)S(1)} %pad_maximum_fusion.4), channel_id=1, source_target_pairs={{0,256},{16,272},{32,288},{48,304},{64,320},{80,336},{96,352},{112... | collective-permute-start | bytes 196616 | tf_op jit(solution)/shard_map/ppermute | solution.py:123
  51.4 17.7 %collective-permute-start.5 = (f32[2,16,512]{2,1,0:T(8,128)S(1)}, f32[2,16,512]{2,1,0:T(8,128)S(1)}, u32[]{:S(2)}, u32[]{:S(2)}) collective-permute-start(f32[2,16,512]{2,1,0:T(8,128)S(1)} %pad_maximum_fusion.5), channel_id=1, source_target_pairs={{0,768},{16,784},{32,800},{48,816},{64,832},{80,848},{96,864},{112... | collective-permute-start | bytes 196616 | tf_op jit(solution)/shard_map/ppermute | solution.py:123
  64.5 4.6 %copy-start.3 = (f32[256,512]{1,0:T(8,128)S(1)}, f32[256,512]{1,0:T(8,128)}, u32[]{:S(2)}) copy-start(f32[256,512]{1,0:T(8,128)} %shard_map.93) | copy-start | bytes 1572868
  64.5 4.6 %copy-start.4 = (f32[256,512]{1,0:T(8,128)S(1)}, f32[256,512]{1,0:T(8,128)}, u32[]{:S(2)}) copy-start(f32[256,512]{1,0:T(8,128)} %shard_map.94) | copy-start | bytes 1572868
  69.1 1.0 %copy-start.5 = (f32[256,512]{1,0:T(8,128)S(1)}, f32[256,512]{1,0:T(8,128)}, u32[]{:S(2)}) copy-start(f32[256,512]{1,0:T(8,128)} %shard_map.95) | copy-start | bytes 1572868
  69.1 1.2 %copy-start.6 = (f32[256,512]{1,0:T(8,128)S(1)}, f32[256,512]{1,0:T(8,128)}, u32[]{:S(2)}) copy-start(f32[256,512]{1,0:T(8,128)} %shard_map.96) | copy-start | bytes 1572868
  77.5 0.9 %copy-start.9 = (bf16[256,512]{1,0:T(8,128)(2,1)S(1)}, bf16[256,512]{1,0:T(8,128)(2,1)}, u32[]{:S(2)}) copy-start(bf16[256,512]{1,0:T(8,128)(2,1)} %param.7) | copy-start | bytes 786436
  77.5 1.0 %copy-start.10 = (bf16[256,512]{1,0:T(8,128)(2,1)S(1)}, bf16[256,512]{1,0:T(8,128)(2,1)}, u32[]{:S(2)}) copy-start(bf16[256,512]{1,0:T(8,128)(2,1)} %param.6) | copy-start | bytes 786436

commit v10 on v9

--- a/solution.py
+++ b/solution.py
@@ -48,7 +48,7 @@
     return pieces.reshape(length // BLOCK, BLOCK, width)
 
 
-def carried_kernel(fwd_ref, bwd_ref, scaled_ref, rates_ref, fwd_out, bwd_out):
+def carried_kernel(fwd_ref, bwd_ref, got_ref, into_ref, scaled_ref, rates_ref, fwd_out, bwd_out):
     length, width = fwd_out.shape
     order = rates_ref.shape[0]
     lags = lax.broadcasted_iota(jnp.int32, (BLOCK, width), 0).astype(jnp.float32) + 1.0
@@ -58,8 +58,10 @@
     def mode(m, carry):
         rate = rates_ref[pl.ds(m, 1), :]
         weight = scaled_ref[pl.ds(m, 1), :]
-        fwd_weight = weight * fwd_ref[pl.ds(m, 1), :]
-        bwd_weight = weight * bwd_ref[pl.ds(m, 1), :]
+        fwd_in = fwd_ref[pl.ds(m, 1), :] + into_ref[0, pl.ds(m, 1), :] * got_ref[0, pl.ds(m, 1), :]
+        bwd_in = bwd_ref[pl.ds(m, 1), :] + into_ref[1, pl.ds(m, 1), :] * got_ref[1, pl.ds(m, 1), :]
+        fwd_weight = weight * fwd_in
+        bwd_weight = weight * bwd_in
         after = jnp.exp(-rate * lags)
         for b in range(length // BLOCK):
             rows = pl.ds(b * BLOCK, BLOCK)
@@ -71,9 +73,11 @@
     lax.fori_loop(0, order, mode, 0)
 
 
-def carried(fwd_in, bwd_in, scaled, rates, length):
+def carried(fwd_in, bwd_in, last, scaled, rates, length):
     shape = jax.ShapeDtypeStruct((length, fwd_in.shape[1]), jnp.float32)
-    return pl.pallas_call(carried_kernel, out_shape=(shape, shape))(fwd_in, bwd_in, scaled, rates)
+    return pl.pallas_call(carried_kernel, out_shape=(shape, shape))(
+        fwd_in, bwd_in, last[0], last[1], scaled, rates
+    )
 
 
 def end_state(signal, rates):
@@ -130,15 +134,18 @@
         fwd_got, bwd_got = got[0], got[1]
         upper = (place // span) % 2 == 1
         offset = (place % span).astype(jnp.float32)
-        fwd_in = fwd_in + jnp.where(upper, jnp.exp(-rates * (length * offset)), 0.0) * fwd_got
-        bwd_in = bwd_in + jnp.where(
-            upper, 0.0, jnp.exp(-rates * (length * (span - 1.0 - offset)))
-        ) * bwd_got
+        fwd_weight = jnp.where(upper, jnp.exp(-rates * (length * offset)), 0.0)
+        bwd_weight = jnp.where(upper, 0.0, jnp.exp(-rates * (length * (span - 1.0 - offset))))
+        if 2 * span >= count:
+            last = (got, jnp.stack([fwd_weight, bwd_weight]))
+            break
+        fwd_in = fwd_in + fwd_weight * fwd_got
+        bwd_in = bwd_in + bwd_weight * bwd_got
         if 2 * span < count:
             whole = jnp.exp(-rates * (length * span))
             fwd_total = jnp.where(upper, whole * fwd_got + fwd_total, whole * fwd_total + fwd_got)
             bwd_total = jnp.where(upper, bwd_got + whole * bwd_total, bwd_total + whole * bwd_got)
-    return fwd_in, bwd_in, tuple(cover)
+    return fwd_in, bwd_in, last, tuple(cover)
 
 
 def per_device(query, key_proj, value, residues, rates, cotangent):
@@ -157,7 +164,7 @@
         for signal in (gated, reversed_weighted)
         for modes in (slice(0, half), slice(half, None))
     )
-    fwd_in, bwd_in, cover = incoming_states(
+    fwd_in, bwd_in, last, cover = incoming_states(
         end_state(gated, rates),
         end_state(reversed_weighted, rates),
         rates,
@@ -166,7 +173,7 @@
     )
     fwd_pieces = cover[0] + cover[1]
     bwd_pieces = cover[2] + cover[3]
-    fwd_extra, bwd_extra = carried(fwd_in, bwd_in, scaled, rates, length)
+    fwd_extra, bwd_extra = carried(fwd_in, bwd_in, last, scaled, rates, length)
     mixed = fwd_pieces.reshape(length, -1) + fwd_extra
     back = (bwd_pieces.reshape(length, -1) + bwd_extra)[::-1]
     output = (value_f * mixed).astype(jnp.bfloat16)

time: 80.1 us -> 85.6 us (1.069)
  waiting for transfers between devices: 3.27 us -> 5.5 us
  starting transfers between devices: 39.5 us -> 41.6 us
  other arithmetic: 9.06 us -> 10.8 us
    ppermute x6, waiting for transfers between devices: 3.27 us -> 5.5 us  [incoming_states(): lax.ppermute(jnp.stack([fwd_total, bwd_total]), 'ctx', [(i, partner(i, sp...]
    ppermute x6, starting transfers between devices: 39.5 us -> 41.6 us  [incoming_states(): lax.ppermute(jnp.stack([fwd_total, bwd_total]), 'ctx', [(i, partner(i, sp...]
    add x1, other arithmetic: 0.08 us -> 1.18 us  [per_device(): fwd_pieces = cover[0] + cover[1]]
  transfers between devices with their start and end apart: 6 -> 6, of which waited for: 2 -> 4; matrix products, arithmetic and copies ran while one was open for 2% -> 4% of each run, Pallas kernels for 23% -> 21%
where the time goes in v10:
time: 85.6 us; the launch traced here: 84.9 us
  starting transfers between devices  41.6 us (49%)
  Pallas kernels  21.7 us (25%)
  other arithmetic  10.8 us (13%)
  waiting for transfers between devices  5.5 us (6%)
  local copies, waits for them, and re-layouts  4.33 us (5%)
  between operations  1.01 us (1%)
    ppermute x6, starting transfers between devices, incoming_states(): lax.ppermute(jnp.stack([fwd_total, bwd_total]), 'ctx', [(i, partner(i, sp...  41.6 us
    pallas_call x4, Pallas kernels, local_pass(): pl.pallas_call(local_kernel, out_shape=jax.ShapeDtypeStruct((length, widt...  17.9 us
    ppermute x6, waiting for transfers between devices, incoming_states(): lax.ppermute(jnp.stack([fwd_total, bwd_total]), 'ctx', [(i, partner(i, sp...  5.5 us
    pallas_call x1, Pallas kernels, carried(): pl.pallas_call(carried_kernel, out_shape=(shape, shape))  3.78 us
    unnamed x26, local copies, waits for them, and re-layouts  2.55 us
    convert_element_type x1, other arithmetic, per_device(): grad_value = (cot_f * mixed).astype(jnp.bfloat16)  2.2 us
    reduce_sum x2, other arithmetic, end_state(): return jnp.sum(outer * jnp.sum(inner[None] * rows, axis=1), axis=0)  2.14 us
  transfers between devices with their start and end apart: 6, of which 4 were waited for; matrix products, arithmetic and copies ran while one was open for 4% of the time, Pallas kernels for 21%

profile of v10, /device:TPU:6, one launch (start us, length us, event | category | flops | bytes accessed | tf_op | source)
XLA Modules:
  0.0 84.9 jit_solution(11175919053455320180)
XLA Ops:
  0.7 0.8 neg.5
  1.4 1.1 %fusion.2 = bf16[256,512]{1,0:T(8,128)(2,1)S(1)} fusion(bf16[256,512]{1,0:T(8,128)(2,1)} %param.7, bf16[256,512]{1,0:T(8,128)(2,1)} %param.6), kind=kLoop, calls=%fused_computation.10 | loop fusion | flops 524288 | bytes 786432 | tf_op jit(solution)/shard_map/convert_element_type | solution.py:158
  2.6 0.9 %copy-done.6 = bf16[256,512]{1,0:T(8,128)(2,1)S(1)} copy-done((bf16[256,512]{1,0:T(8,128)(2,1)S(1)}, bf16[256,512]{1,0:T(8,128)(2,1)}, u32[]{:S(2)}) %copy-start.6) | copy-done | bytes 262168
  3.6 0.3 rev.6.signal_ref
  4.1 0.3 copy-done
  4.3 1.9 %multiply_reduce_fusion.1 = (f32[16,16,512]{2,1,0:T(8,128)S(1)}, f32[16,16,512]{2,1,0:T(8,128)S(1)}) fusion(f32[16,16,512]{2,1,0:T(8,128)S(1)} %bitcast.160, f32[16,16,512]{2,1,0:T(8,128)S(1)} %multiply_exponential_fusion, f32[16,16,512]{2,1,0:T(8,128)S(1)} %bitcast.161), kind=kLoop, calls=%fused_computation.1 | loop fusion | flops 8126464 | bytes 2621440 | tf_op jit(solution)/shard_map/reduce_sum | solution.py:90
  6.5 1.9 %collective-permute-start = (f32[2,16,512]{2,1,0:T(8,128)S(1)}, f32[2,16,512]{2,1,0:T(8,128)S(1)}, u32[]{:S(2)}, u32[]{:S(2)}) collective-permute-start(f32[2,16,512]{2,1,0:T(8,128)S(1)} %pad_maximum_fusion), channel_id=1, source_target_pairs={{0,16},{16,0},{32,48},{48,32},{64,80},{80,64},{96,112},{112,96},{1... | collective-permute-start | bytes 196616 | tf_op jit(solution)/shard_map/ppermute | solution.py:127
  8.5 1.2 %collective-permute-done = f32[2,16,512]{2,1,0:T(8,128)S(1)} collective-permute-done((f32[2,16,512]{2,1,0:T(8,128)S(1)}, f32[2,16,512]{2,1,0:T(8,128)S(1)}, u32[]{:S(2)}, u32[]{:S(2)}) %collective-permute-start) | collective-permute-done | bytes 65568 | tf_op jit(solution)/shard_map/ppermute | solution.py:127
  9.7 3.5 %collective-permute-start.1 = (f32[2,16,512]{2,1,0:T(8,128)S(1)}, f32[2,16,512]{2,1,0:T(8,128)S(1)}, u32[]{:S(2)}, u32[]{:S(2)}) collective-permute-start(f32[2,16,512]{2,1,0:T(8,128)S(1)} %pad_maximum_fusion.1), channel_id=1, source_target_pairs={{0,32},{16,48},{32,0},{48,16},{64,96},{80,112},{96,64},{112,80},{1... | collective-permute-start | bytes 196616 | tf_op jit(solution)/shard_map/ppermute | solution.py:127
  13.2 0.6 fusion.29
  13.8 2.1 %collective-permute-done.1 = f32[2,16,512]{2,1,0:T(8,128)S(1)} collective-permute-done((f32[2,16,512]{2,1,0:T(8,128)S(1)}, f32[2,16,512]{2,1,0:T(8,128)S(1)}, u32[]{:S(2)}, u32[]{:S(2)}) %collective-permute-start.1) | collective-permute-done | bytes 65568 | tf_op jit(solution)/shard_map/ppermute | solution.py:127
  16.0 4.5 %collective-permute-start.2 = (f32[2,16,512]{2,1,0:T(8,128)S(1)}, f32[2,16,512]{2,1,0:T(8,128)S(1)}, u32[]{:S(2)}, u32[]{:S(2)}) collective-permute-start(f32[2,16,512]{2,1,0:T(8,128)S(1)} %pad_maximum_fusion.2), channel_id=1, source_target_pairs={{0,64},{16,80},{32,96},{48,112},{64,0},{80,16},{96,32},{112,48},{1... | collective-permute-start | bytes 196616 | tf_op jit(solution)/shard_map/ppermute | solution.py:127
  20.5 0.6 fusion.30
  21.1 4.5 %shard_map.93 = f32[256,512]{1,0:T(8,128)} custom-call(f32[256,512]{1,0:T(8,128)} %copy-done, f32[8,512]{1,0:T(8,128)} %get-tuple-element.48.scaled_ref, f32[8,512]{1,0:T(8,128)} %get-tuple-element.46.rates_ref), custom_call_target="tpu_custom_call" | custom-call | tf_op jit(solution)/shard_map/pallas_call | solution.py:45
  25.6 5.7 %collective-permute-start.3 = (f32[2,16,512]{2,1,0:T(8,128)S(1)}, f32[2,16,512]{2,1,0:T(8,128)S(1)}, u32[]{:S(2)}, u32[]{:S(2)}) collective-permute-start(f32[2,16,512]{2,1,0:T(8,128)S(1)} %pad_maximum_fusion.3), channel_id=1, source_target_pairs={{0,192},{16,208},{32,224},{48,240},{64,128},{80,144},{96,160},{112... | collective-permute-start | bytes 196616 | tf_op jit(solution)/shard_map/ppermute | solution.py:127
  31.5 4.5 %shard_map.95 = f32[256,512]{1,0:T(8,128)} custom-call(f32[256,512]{1,0:T(8,128)} %copy-done.1, f32[8,512]{1,0:T(8,128)} %get-tuple-element.48.scaled_ref, f32[8,512]{1,0:T(8,128)} %get-tuple-element.46.rates_ref), custom_call_target="tpu_custom_call" | custom-call | tf_op jit(solution)/shard_map/pallas_call | solution.py:45
  35.9 4.5 %shard_map.96 = f32[256,512]{1,0:T(8,128)} custom-call(f32[256,512]{1,0:T(8,128)} %copy-done.1, f32[8,512]{1,0:T(8,128)} %get-tuple-element.47.scaled_ref, f32[8,512]{1,0:T(8,128)} %get-tuple-element.45.rates_ref), custom_call_target="tpu_custom_call" | custom-call | tf_op jit(solution)/shard_map/pallas_call | solution.py:45
  40.4 4.5 %shard_map.94 = f32[256,512]{1,0:T(8,128)} custom-call(f32[256,512]{1,0:T(8,128)} %copy-done, f32[8,512]{1,0:T(8,128)} %get-tuple-element.47.scaled_ref, f32[8,512]{1,0:T(8,128)} %get-tuple-element.45.rates_ref), custom_call_target="tpu_custom_call" | custom-call | tf_op jit(solution)/shard_map/pallas_call | solution.py:45
  44.9 11.0 %collective-permute-start.4 = (f32[2,16,512]{2,1,0:T(8,128)S(1)}, f32[2,16,512]{2,1,0:T(8,128)S(1)}, u32[]{:S(2)}, u32[]{:S(2)}) collective-permute-start(f32[2,16,512]{2,1,0:T(8,128)S(1)} %pad_maximum_fusion.4), channel_id=1, source_target_pairs={{0,256},{16,272},{32,288},{48,304},{64,320},{80,336},{96,352},{112... | collective-permute-start | bytes 196616 | tf_op jit(solution)/shard_map/ppermute | solution.py:127
  56.0 0.6 pad_maximum_fusion.6.into_ref
  56.6 1.2 %add.150 = f32[4,64,512]{2,1,0:T(8,128)S(1)} add(f32[4,64,512]{2,1,0:T(8,128)S(1)} %bitcast.162, f32[4,64,512]{2,1,0:T(8,128)} %bitcast.165) | non-fusion elementwise | flops 131072 | bytes 1572864 | tf_op jit(solution)/shard_map/add | solution.py:174
  57.8 0.7 collective-permute-done.4
  58.5 0.7 fusion.12
  59.1 15.0 %collective-permute-start.5 = (f32[2,16,512]{2,1,0:T(8,128)S(1)}, f32[2,16,512]{2,1,0:T(8,128)S(1)}, u32[]{:S(2)}, u32[]{:S(2)}) collective-permute-start(f32[2,16,512]{2,1,0:T(8,128)S(1)} %pad_maximum_fusion.5), channel_id=1, source_target_pairs={{0,768},{16,784},{32,800},{48,816},{64,832},{80,848},{96,864},{112... | collective-permute-start | bytes 196616 | tf_op jit(solution)/shard_map/ppermute | solution.py:127
  74.1 0.7 fusion.9.fwd_ref
  74.8 1.6 %collective-permute-done.5.got_ref = f32[2,16,512]{2,1,0:T(8,128)S(1)} collective-permute-done((f32[2,16,512]{2,1,0:T(8,128)S(1)}, f32[2,16,512]{2,1,0:T(8,128)S(1)}, u32[]{:S(2)}, u32[]{:S(2)}) %collective-permute-start.5) | collective-permute-done | bytes 65568 | tf_op jit(solution)/shard_map/ppermute | solution.py:127
  76.5 0.5 copy-done.11
  77.0 3.8 %shard_map.97 = (f32[256,512]{1,0:T(8,128)}, f32[256,512]{1,0:T(8,128)}) custom-call(f32[16,512]{1,0:T(8,128)} %fusion.9.fwd_ref, f32[16,512]{1,0:T(8,128)} %get-tuple-element.38.bwd_ref, f32[2,16,512]{2,1,0:T(8,128)} %copy-done.11, f32[2,16,512]{2,1,0:T(8,128)} %pad_maximum_fusion.6.into_ref, f32[16,512]{1,0:T(8,128)} %copy-done.10, f32[16,512]{1,0:T(8,128)} %rates_ref.1), custom_call_target="tpu_custom_call" | custom-call | tf_op jit(solution)/shard_map/pallas_call | solution.py:78
  80.8 2.2 %fusion.4 = (bf16[256,512]{1,0:T(8,128)(2,1)}, bf16[256,512]{1,0:T(8,128)(2,1)}, f32[256,512]{1,0:T(8,128)S(1)}) fusion(bf16[256,512]{1,0:T(8,128)(2,1)S(1)} %copy-done.6, f32[256,512]{1,0:T(8,128)} %get-tuple-element.20, f32[4,64,512]{2,1,0:T(8,128)S(1)} %add.150, bf16[256,512]{1,0:T(8,128)(2,1)S(1)} %copy-done.7, f32[256,512]{1,0:T(8,128)} %get-tuple-element.23, ...), kind=kLoop, calls=%fused_computation.12 | loop fusion | flops 1048576 | bytes 3670016 | tf_op jit(solution)/shard_map/convert_element_type | solution.py:180
  83.0 0.3 rev.7
  83.3 0.7 copy-done.8
  84.0 0.9 %fusion.1 = (bf16[256,512]{1,0:T(8,128)(2,1)}, bf16[256,512]{1,0:T(8,128)(2,1)}) fusion(f32[256,512]{1,0:T(8,128)S(1)} %rev.7, bf16[256,512]{1,0:T(8,128)(2,1)S(1)} %copy-done.9, bf16[256,512]{1,0:T(8,128)(2,1)S(1)} %copy-done.8), kind=kLoop, calls=%fused_computation.9 | loop fusion | flops 786432 | bytes 1572864 | tf_op jit(solution)/shard_map/convert_element_type | solution.py:182
  (41 shorter events, 0.9 us)
Async XLA Ops:
  2.5 1.0 %copy-start.6 = (bf16[256,512]{1,0:T(8,128)(2,1)S(1)}, bf16[256,512]{1,0:T(8,128)(2,1)}, u32[]{:S(2)}) copy-start(bf16[256,512]{1,0:T(8,128)(2,1)} %param.11) | copy-start | bytes 786436
  2.5 1.0 %copy-start.7 = (bf16[256,512]{1,0:T(8,128)(2,1)S(1)}, bf16[256,512]{1,0:T(8,128)(2,1)}, u32[]{:S(2)}) copy-start(bf16[256,512]{1,0:T(8,128)(2,1)} %param.8) | copy-start | bytes 786436
  3.5 0.8 copy-start
  3.9 2.4 %copy-start.1 = (f32[256,512]{1,0:T(8,128)}, f32[256,512]{1,0:T(8,128)S(1)}, u32[]{:S(2)}) copy-start(f32[256,512]{1,0:T(8,128)S(1)} %rev.6.signal_ref) | copy-start | bytes 1572868
  6.3 3.4 %copy-start.2 = (f32[16,512]{1,0:T(8,128)S(1)}, f32[16,512]{1,0:T(8,128)}, u32[]{:S(2)}) copy-start(f32[16,512]{1,0:T(8,128)} %rates_ref.1) | copy-start | bytes 98308
  6.5 9.4 %copy-start.12 = (f32[16,512]{1,0:T(8,128)S(1)}, f32[16,512]{1,0:T(8,128)}, u32[]{:S(2)}) copy-start(f32[16,512]{1,0:T(8,128)} %param.9) | copy-start | bytes 98308
  6.5 3.1 %collective-permute-start = (f32[2,16,512]{2,1,0:T(8,128)S(1)}, f32[2,16,512]{2,1,0:T(8,128)S(1)}, u32[]{:S(2)}, u32[]{:S(2)}) collective-permute-start(f32[2,16,512]{2,1,0:T(8,128)S(1)} %pad_maximum_fusion), channel_id=1, source_target_pairs={{0,16},{16,0},{32,48},{48,32},{64,80},{80,64},{96,112},{112,96},{1... | collective-permute-start | bytes 196616 | tf_op jit(solution)/shard_map/ppermute | solution.py:127
  9.7 6.2 %collective-permute-start.1 = (f32[2,16,512]{2,1,0:T(8,128)S(1)}, f32[2,16,512]{2,1,0:T(8,128)S(1)}, u32[]{:S(2)}, u32[]{:S(2)}) collective-permute-start(f32[2,16,512]{2,1,0:T(8,128)S(1)} %pad_maximum_fusion.1), channel_id=1, source_target_pairs={{0,32},{16,48},{32,0},{48,16},{64,96},{80,112},{96,64},{112,80},{1... | collective-permute-start | bytes 196616 | tf_op jit(solution)/shard_map/ppermute | solution.py:127
  16.0 9.6 %copy-start.10 = (f32[16,512]{1,0:T(8,128)}, f32[16,512]{1,0:T(8,128)S(1)}, u32[]{:S(2)}) copy-start(f32[16,512]{1,0:T(8,128)S(1)} %get-tuple-element.49.scaled_ref) | copy-start | bytes 98308
  16.0 9.6 %collective-permute-start.2 = (f32[2,16,512]{2,1,0:T(8,128)S(1)}, f32[2,16,512]{2,1,0:T(8,128)S(1)}, u32[]{:S(2)}, u32[]{:S(2)}) collective-permute-start(f32[2,16,512]{2,1,0:T(8,128)S(1)} %pad_maximum_fusion.2), channel_id=1, source_target_pairs={{0,64},{16,80},{32,96},{48,112},{64,0},{80,16},{96,32},{112,48},{1... | collective-permute-start | bytes 196616 | tf_op jit(solution)/shard_map/ppermute | solution.py:127
  25.6 19.2 %collective-permute-start.3 = (f32[2,16,512]{2,1,0:T(8,128)S(1)}, f32[2,16,512]{2,1,0:T(8,128)S(1)}, u32[]{:S(2)}, u32[]{:S(2)}) collective-permute-start(f32[2,16,512]{2,1,0:T(8,128)S(1)} %pad_maximum_fusion.3), channel_id=1, source_target_pairs={{0,192},{16,208},{32,224},{48,240},{64,128},{80,144},{96,160},{112... | collective-permute-start | bytes 196616 | tf_op jit(solution)/shard_map/ppermute | solution.py:127
  44.9 11.8 %copy-start.3 = (f32[256,512]{1,0:T(8,128)S(1)}, f32[256,512]{1,0:T(8,128)}, u32[]{:S(2)}) copy-start(f32[256,512]{1,0:T(8,128)} %shard_map.93) | copy-start | bytes 1572868
  44.9 13.6 %collective-permute-start.4 = (f32[2,16,512]{2,1,0:T(8,128)S(1)}, f32[2,16,512]{2,1,0:T(8,128)S(1)}, u32[]{:S(2)}, u32[]{:S(2)}) collective-permute-start(f32[2,16,512]{2,1,0:T(8,128)S(1)} %pad_maximum_fusion.4), channel_id=1, source_target_pairs={{0,256},{16,272},{32,288},{48,304},{64,320},{80,336},{96,352},{112... | collective-permute-start | bytes 196616 | tf_op jit(solution)/shard_map/ppermute | solution.py:127
  56.6 19.8 %copy-start.5 = (f32[256,512]{1,0:T(8,128)S(1)}, f32[256,512]{1,0:T(8,128)}, u32[]{:S(2)}) copy-start(f32[256,512]{1,0:T(8,128)} %shard_map.96) | copy-start | bytes 1572868
  57.8 18.6 %copy-start.4 = (f32[256,512]{1,0:T(8,128)S(1)}, f32[256,512]{1,0:T(8,128)}, u32[]{:S(2)}) copy-start(f32[256,512]{1,0:T(8,128)} %shard_map.95) | copy-start | bytes 1572868
  59.1 17.2 %collective-permute-start.5 = (f32[2,16,512]{2,1,0:T(8,128)S(1)}, f32[2,16,512]{2,1,0:T(8,128)S(1)}, u32[]{:S(2)}, u32[]{:S(2)}) collective-permute-start(f32[2,16,512]{2,1,0:T(8,128)S(1)} %pad_maximum_fusion.5), channel_id=1, source_target_pairs={{0,768},{16,784},{32,800},{48,816},{64,832},{80,848},{96,864},{112... | collective-permute-start | bytes 196616 | tf_op jit(solution)/shard_map/ppermute | solution.py:127
  76.4 0.6 copy-start.11
  83.0 0.9 %copy-start.8 = (bf16[256,512]{1,0:T(8,128)(2,1)S(1)}, bf16[256,512]{1,0:T(8,128)(2,1)}, u32[]{:S(2)}) copy-start(bf16[256,512]{1,0:T(8,128)(2,1)} %param.7) | copy-start | bytes 786436
  83.0 1.0 %copy-start.9 = (bf16[256,512]{1,0:T(8,128)(2,1)S(1)}, bf16[256,512]{1,0:T(8,128)(2,1)}, u32[]{:S(2)}) copy-start(bf16[256,512]{1,0:T(8,128)(2,1)} %param.6) | copy-start | bytes 786436

commit v11 on v9

--- a/solution.py
+++ b/solution.py
@@ -7,15 +7,16 @@
 BLOCK = 64
 
 
-def local_kernel(signal_ref, scaled_ref, rates_ref, out_ref):
-    length, width = signal_ref.shape
+def local_kernel(fwd_ref, bwd_ref, scaled_ref, rates_ref, fwd_out, bwd_out):
+    length, width = fwd_ref.shape
     order = rates_ref.shape[0]
     lags = lax.broadcasted_iota(jnp.int32, (BLOCK, width), 0).astype(jnp.float32)
     lower = (
         lax.broadcasted_iota(jnp.int32, (BLOCK, BLOCK), 0)
         >= lax.broadcasted_iota(jnp.int32, (BLOCK, BLOCK), 1)
     ).astype(jnp.bfloat16)
-    out_ref[...] = jnp.zeros(out_ref.shape, jnp.float32)
+    fwd_out[...] = jnp.zeros(fwd_out.shape, jnp.float32)
+    bwd_out[...] = jnp.zeros(bwd_out.shape, jnp.float32)
 
     def mode(m, carry):
         rate = rates_ref[pl.ds(m, 1), :]
@@ -23,29 +24,31 @@
         rising = jnp.exp(rate * lags)
         falling = jnp.exp(-rate * lags)
         step_decay = jnp.exp(-rate)
-        state = jnp.zeros((1, width), jnp.float32)
-        for b in range(length // BLOCK):
-            rows = pl.ds(b * BLOCK, BLOCK)
-            lifted = rising * signal_ref[rows, :]
-            high = lifted.astype(jnp.bfloat16)
-            low = (lifted - high.astype(jnp.float32)).astype(jnp.bfloat16)
-            summed = jnp.dot(lower, high, preferred_element_type=jnp.float32) + jnp.dot(
-                lower, low, preferred_element_type=jnp.float32
-            )
-            states = falling * (summed + step_decay * state)
-            out_ref[rows, :] += weight * states
-            state = states[BLOCK - 1 : BLOCK, :]
+        for signal_ref, out_ref in ((fwd_ref, fwd_out), (bwd_ref, bwd_out)):
+            state = jnp.zeros((1, width), jnp.float32)
+            for b in range(length // BLOCK):
+                rows = pl.ds(b * BLOCK, BLOCK)
+                lifted = rising * signal_ref[rows, :]
+                high = lifted.astype(jnp.bfloat16)
+                low = (lifted - high.astype(jnp.float32)).astype(jnp.bfloat16)
+                summed = jnp.dot(lower, high, preferred_element_type=jnp.float32) + jnp.dot(
+                    lower, low, preferred_element_type=jnp.float32
+                )
+                states = falling * (summed + step_decay * state)
+                out_ref[rows, :] += weight * states
+                state = states[BLOCK - 1 : BLOCK, :]
         return carry
 
     lax.fori_loop(0, order, mode, 0)
 
 
-def local_pass(signal, scaled, rates):
-    length, width = signal.shape
-    pieces = pl.pallas_call(
-        local_kernel, out_shape=jax.ShapeDtypeStruct((length, width), jnp.float32)
-    )(signal, scaled, rates)
-    return pieces.reshape(length // BLOCK, BLOCK, width)
+def local_pass(fwd_signal, bwd_signal, scaled, rates):
+    length, width = fwd_signal.shape
+    shape = jax.ShapeDtypeStruct((length, width), jnp.float32)
+    fwd_pieces, bwd_pieces = pl.pallas_call(local_kernel, out_shape=(shape, shape))(
+        fwd_signal, bwd_signal, scaled, rates
+    )
+    return fwd_pieces, bwd_pieces
 
 
 def carried_kernel(fwd_ref, bwd_ref, scaled_ref, rates_ref, fwd_out, bwd_out):
@@ -153,8 +156,7 @@
     reversed_weighted = weighted[::-1]
     half = rates.shape[0] // 2
     cover = tuple(
-        local_pass(signal, scaled[modes], rates[modes])
-        for signal in (gated, reversed_weighted)
+        local_pass(gated, reversed_weighted, scaled[modes], rates[modes])
         for modes in (slice(0, half), slice(half, None))
     )
     fwd_in, bwd_in, cover = incoming_states(
@@ -164,11 +166,11 @@
         length,
         cover,
     )
-    fwd_pieces = cover[0] + cover[1]
-    bwd_pieces = cover[2] + cover[3]
+    fwd_pieces = cover[0][0] + cover[1][0]
+    bwd_pieces = cover[0][1] + cover[1][1]
     fwd_extra, bwd_extra = carried(fwd_in, bwd_in, scaled, rates, length)
-    mixed = fwd_pieces.reshape(length, -1) + fwd_extra
-    back = (bwd_pieces.reshape(length, -1) + bwd_extra)[::-1]
+    mixed = fwd_pieces + fwd_extra
+    back = (bwd_pieces + bwd_extra)[::-1]
     output = (value_f * mixed).astype(jnp.bfloat16)
     grad_value = (cot_f * mixed).astype(jnp.bfloat16)
     grad_query = (back * key_f).astype(jnp.bfloat16)

time: 80.1 us -> 77 us (0.961)
  Pallas kernels: 21.6 us -> 15.4 us
  waiting for transfers between devices: 3.27 us -> 8.25 us
  starting transfers between devices: 39.5 us -> 38.1 us
  local copies, waits for them, and re-layouts: 4.91 us -> 3.81 us
    pallas_call x4 -> x2, Pallas kernels: 18 us -> 11.7 us  [local_pass(): pl.pallas_call(local_kernel, out_shape=(shape, shape))]
    ppermute x6, waiting for transfers between devices: 3.27 us -> 8.25 us  [incoming_states(): lax.ppermute(jnp.stack([fwd_total, bwd_total]), 'ctx', [(i, partner(i, sp...]
    ppermute x6, starting transfers between devices: 39.5 us -> 38.1 us  [incoming_states(): lax.ppermute(jnp.stack([fwd_total, bwd_total]), 'ctx', [(i, partner(i, sp...]
    unnamed x26 -> x22, local copies, waits for them, and re-layouts: 3.13 us -> 2.03 us
  transfers between devices with their start and end apart: 6 -> 6, of which waited for: 2 -> 4; matrix products, arithmetic and copies ran while one was open for 2% -> 2% of each run, Pallas kernels for 23% -> 15%
where the time goes in v11:
time: 77 us; the launch traced here: 76 us
  starting transfers between devices  38.1 us (49%)
  Pallas kernels  15.4 us (20%)
  other arithmetic  9.42 us (12%)
  waiting for transfers between devices  8.25 us (11%)
  local copies, waits for them, and re-layouts  3.81 us (5%)
  between operations  1.07 us (1%)
    ppermute x6, starting transfers between devices, incoming_states(): lax.ppermute(jnp.stack([fwd_total, bwd_total]), 'ctx', [(i, partner(i, sp...  38.1 us
    pallas_call x2, Pallas kernels, local_pass(): pl.pallas_call(local_kernel, out_shape=(shape, shape))  11.7 us
    ppermute x6, waiting for transfers between devices, incoming_states(): lax.ppermute(jnp.stack([fwd_total, bwd_total]), 'ctx', [(i, partner(i, sp...  8.25 us
    pallas_call x1, Pallas kernels, carried(): pl.pallas_call(carried_kernel, out_shape=(shape, shape))  3.68 us
    convert_element_type x1, other arithmetic, per_device(): grad_value = (cot_f * mixed).astype(jnp.bfloat16)  2.73 us
    reduce_sum x2, other arithmetic, end_state(): return jnp.sum(outer * jnp.sum(inner[None] * rows, axis=1), axis=0)  2.14 us
    unnamed x22, local copies, waits for them, and re-layouts  2.03 us
  transfers between devices with their start and end apart: 6, of which 4 were waited for; matrix products, arithmetic and copies ran while one was open for 2% of the time, Pallas kernels for 15%

profile of v11, /device:TPU:6, one launch (start us, length us, event | category | flops | bytes accessed | tf_op | source)
XLA Modules:
  0.0 76.0 jit_solution(4421049184671462549)
XLA Ops:
  0.7 0.8 %neg.5 = f32[16,512]{1,0:T(8,128)S(1)} negate(f32[16,512]{1,0:T(8,128)} %rates_ref.1) | non-fusion elementwise | flops 8192 | bytes 65536 | tf_op jit(solution)/shard_map/neg | solution.py:141
  1.4 1.1 %fusion.2 = bf16[256,512]{1,0:T(8,128)(2,1)S(1)} fusion(bf16[256,512]{1,0:T(8,128)(2,1)} %param.7, bf16[256,512]{1,0:T(8,128)(2,1)} %param.6), kind=kLoop, calls=%fused_computation.10 | loop fusion | flops 524288 | bytes 786432 | tf_op jit(solution)/shard_map/convert_element_type | solution.py:154
  2.6 0.9 %copy-done.3 = bf16[256,512]{1,0:T(8,128)(2,1)S(1)} copy-done((bf16[256,512]{1,0:T(8,128)(2,1)S(1)}, bf16[256,512]{1,0:T(8,128)(2,1)}, u32[]{:S(2)}) %copy-start.3) | copy-done | bytes 262168
  3.5 0.1 copy-done.4
  3.6 0.1 convert_multiply_fusion.1
  3.6 0.3 rev.6.bwd_ref
  3.9 0.1 multiply_exponential_fusion
  4.1 0.3 copy-done
  4.4 1.9 %multiply_reduce_fusion.1 = (f32[16,16,512]{2,1,0:T(8,128)S(1)}, f32[16,16,512]{2,1,0:T(8,128)S(1)}) fusion(f32[16,16,512]{2,1,0:T(8,128)S(1)} %bitcast.124, f32[16,16,512]{2,1,0:T(8,128)S(1)} %multiply_exponential_fusion, f32[16,16,512]{2,1,0:T(8,128)S(1)} %bitcast.125), kind=kLoop, calls=%fused_computation.1 | loop fusion | flops 8126464 | bytes 2621440 | tf_op jit(solution)/shard_map/reduce_sum | solution.py:89
  6.3 0.2 multiply_reduce_fusion.3
  6.6 1.9 %collective-permute-start = (f32[2,16,512]{2,1,0:T(8,128)S(1)}, f32[2,16,512]{2,1,0:T(8,128)S(1)}, u32[]{:S(2)}, u32[]{:S(2)}) collective-permute-start(f32[2,16,512]{2,1,0:T(8,128)S(1)} %pad_maximum_fusion), channel_id=1, source_target_pairs={{0,16},{16,0},{32,48},{48,32},{64,80},{80,64},{96,112},{112,96},{1... | collective-permute-start | bytes 196616 | tf_op jit(solution)/shard_map/ppermute | solution.py:126
  8.5 1.2 %collective-permute-done = f32[2,16,512]{2,1,0:T(8,128)S(1)} collective-permute-done((f32[2,16,512]{2,1,0:T(8,128)S(1)}, f32[2,16,512]{2,1,0:T(8,128)S(1)}, u32[]{:S(2)}, u32[]{:S(2)}) %collective-permute-start) | collective-permute-done | bytes 65568 | tf_op jit(solution)/shard_map/ppermute | solution.py:126
  9.8 3.5 %collective-permute-start.1 = (f32[2,16,512]{2,1,0:T(8,128)S(1)}, f32[2,16,512]{2,1,0:T(8,128)S(1)}, u32[]{:S(2)}, u32[]{:S(2)}) collective-permute-start(f32[2,16,512]{2,1,0:T(8,128)S(1)} %pad_maximum_fusion.1), channel_id=1, source_target_pairs={{0,32},{16,48},{32,0},{48,16},{64,96},{80,112},{96,64},{112,80},{1... | collective-permute-start | bytes 196616 | tf_op jit(solution)/shard_map/ppermute | solution.py:126
  13.3 2.6 %collective-permute-done.1 = f32[2,16,512]{2,1,0:T(8,128)S(1)} collective-permute-done((f32[2,16,512]{2,1,0:T(8,128)S(1)}, f32[2,16,512]{2,1,0:T(8,128)S(1)}, u32[]{:S(2)}, u32[]{:S(2)}) %collective-permute-start.1) | collective-permute-done | bytes 65568 | tf_op jit(solution)/shard_map/ppermute | solution.py:126
  16.0 4.5 %collective-permute-start.2 = (f32[2,16,512]{2,1,0:T(8,128)S(1)}, f32[2,16,512]{2,1,0:T(8,128)S(1)}, u32[]{:S(2)}, u32[]{:S(2)}) collective-permute-start(f32[2,16,512]{2,1,0:T(8,128)S(1)} %pad_maximum_fusion.2), channel_id=1, source_target_pairs={{0,64},{16,80},{32,96},{48,112},{64,0},{80,16},{96,32},{112,48},{1... | collective-permute-start | bytes 196616 | tf_op jit(solution)/shard_map/ppermute | solution.py:126
  20.5 2.5 %collective-permute-done.2 = f32[2,16,512]{2,1,0:T(8,128)S(1)} collective-permute-done((f32[2,16,512]{2,1,0:T(8,128)S(1)}, f32[2,16,512]{2,1,0:T(8,128)S(1)}, u32[]{:S(2)}, u32[]{:S(2)}) %collective-permute-start.2) | collective-permute-done | bytes 65568 | tf_op jit(solution)/shard_map/ppermute | solution.py:126
  23.1 6.2 %collective-permute-start.3 = (f32[2,16,512]{2,1,0:T(8,128)S(1)}, f32[2,16,512]{2,1,0:T(8,128)S(1)}, u32[]{:S(2)}, u32[]{:S(2)}) collective-permute-start(f32[2,16,512]{2,1,0:T(8,128)S(1)} %pad_maximum_fusion.3), channel_id=1, source_target_pairs={{0,192},{16,208},{32,224},{48,240},{64,128},{80,144},{96,160},{112... | collective-permute-start | bytes 196616 | tf_op jit(solution)/shard_map/ppermute | solution.py:126
  29.2 0.6 fusion.19
  29.9 1.9 %collective-permute-done.3 = f32[2,16,512]{2,1,0:T(8,128)S(1)} collective-permute-done((f32[2,16,512]{2,1,0:T(8,128)S(1)}, f32[2,16,512]{2,1,0:T(8,128)S(1)}, u32[]{:S(2)}, u32[]{:S(2)}) %collective-permute-start.3) | collective-permute-done | bytes 65568 | tf_op jit(solution)/shard_map/ppermute | solution.py:126
  31.8 10.9 %collective-permute-start.4 = (f32[2,16,512]{2,1,0:T(8,128)S(1)}, f32[2,16,512]{2,1,0:T(8,128)S(1)}, u32[]{:S(2)}, u32[]{:S(2)}) collective-permute-start(f32[2,16,512]{2,1,0:T(8,128)S(1)} %pad_maximum_fusion.4), channel_id=1, source_target_pairs={{0,256},{16,272},{32,288},{48,304},{64,320},{80,336},{96,352},{112... | collective-permute-start | bytes 196616 | tf_op jit(solution)/shard_map/ppermute | solution.py:126
  42.8 0.6 fusion.20
  43.4 5.8 %shard_map.93 = (f32[256,512]{1,0:T(8,128)}, f32[256,512]{1,0:T(8,128)}) custom-call(f32[256,512]{1,0:T(8,128)} %copy-done, f32[256,512]{1,0:T(8,128)} %copy-done.1, f32[8,512]{1,0:T(8,128)} %get-tuple-element.49.scaled_ref, f32[8,512]{1,0:T(8,128)} %get-tuple-element.47.rates_ref), custom_call_target="tpu_custom_call" | custom-call | tf_op jit(solution)/shard_map/pallas_call | solution.py:48
  49.3 11.1 %collective-permute-start.5 = (f32[2,16,512]{2,1,0:T(8,128)S(1)}, f32[2,16,512]{2,1,0:T(8,128)S(1)}, u32[]{:S(2)}, u32[]{:S(2)}) collective-permute-start(f32[2,16,512]{2,1,0:T(8,128)S(1)} %pad_maximum_fusion.5), channel_id=1, source_target_pairs={{0,768},{16,784},{32,800},{48,816},{64,832},{80,848},{96,864},{112... | collective-permute-start | bytes 196616 | tf_op jit(solution)/shard_map/ppermute | solution.py:126
  60.5 5.9 %shard_map.94 = (f32[256,512]{1,0:T(8,128)}, f32[256,512]{1,0:T(8,128)}) custom-call(f32[256,512]{1,0:T(8,128)} %copy-done, f32[256,512]{1,0:T(8,128)} %copy-done.1, f32[8,512]{1,0:T(8,128)} %get-tuple-element.48.scaled_ref, f32[8,512]{1,0:T(8,128)} %get-tuple-element.46.rates_ref), custom_call_target="tpu_custom_call" | custom-call | tf_op jit(solution)/shard_map/pallas_call | solution.py:48
  66.4 0.7 fusion.5.bwd_ref
  67.0 0.7 fusion.6.fwd_ref
  67.7 3.7 %shard_map.95 = (f32[256,512]{1,0:T(8,128)}, f32[256,512]{1,0:T(8,128)}) custom-call(f32[16,512]{1,0:T(8,128)} %fusion.6.fwd_ref, f32[16,512]{1,0:T(8,128)} %fusion.5.bwd_ref, f32[16,512]{1,0:T(8,128)} %copy-done.9, f32[16,512]{1,0:T(8,128)} %rates_ref.1), custom_call_target="tpu_custom_call" | custom-call | tf_op jit(solution)/shard_map/pallas_call | solution.py:79
  71.4 2.7 %fusion.4 = (bf16[256,512]{1,0:T(8,128)(2,1)}, bf16[256,512]{1,0:T(8,128)(2,1)}, f32[256,512]{1,0:T(8,128)S(1)}) fusion(bf16[256,512]{1,0:T(8,128)(2,1)S(1)} %copy-done.3, f32[256,512]{1,0:T(8,128)} %get-tuple-element.24, f32[256,512]{1,0:T(8,128)S(1)} %copy-done.7, f32[256,512]{1,0:T(8,128)} %get-tuple-element.22, bf16[256,512]{1,0:T(8,128)(2,1)S(1)} %copy-done.4, ...), kind=kLoop, calls=%fused_computation.12 | loop fusion | flops 1310720 | bytes 4718592 | tf_op jit(solution)/shard_map/convert_element_type | solution.py:175
  74.1 0.3 rev.7
  74.4 0.7 copy-done.5
  75.1 0.1 copy-done.6
  75.1 0.9 %fusion.1 = (bf16[256,512]{1,0:T(8,128)(2,1)}, bf16[256,512]{1,0:T(8,128)(2,1)}) fusion(f32[256,512]{1,0:T(8,128)S(1)} %rev.7, bf16[256,512]{1,0:T(8,128)(2,1)S(1)} %copy-done.6, bf16[256,512]{1,0:T(8,128)(2,1)S(1)} %copy-done.5), kind=kLoop, calls=%fused_computation.9 | loop fusion | flops 786432 | bytes 1572864 | tf_op jit(solution)/shard_map/convert_element_type | solution.py:177
  (33 shorter events, 0.3 us)
Async XLA Ops:
  2.5 1.0 %copy-start.3 = (bf16[256,512]{1,0:T(8,128)(2,1)S(1)}, bf16[256,512]{1,0:T(8,128)(2,1)}, u32[]{:S(2)}) copy-start(bf16[256,512]{1,0:T(8,128)(2,1)} %param.11) | copy-start | bytes 786436
  2.5 1.0 %copy-start.4 = (bf16[256,512]{1,0:T(8,128)(2,1)S(1)}, bf16[256,512]{1,0:T(8,128)(2,1)}, u32[]{:S(2)}) copy-start(bf16[256,512]{1,0:T(8,128)(2,1)} %param.8) | copy-start | bytes 786436
  3.5 0.8 %copy-start = (f32[256,512]{1,0:T(8,128)}, f32[256,512]{1,0:T(8,128)S(1)}, u32[]{:S(2)}) copy-start(f32[256,512]{1,0:T(8,128)S(1)} %convert_element_type.66.fwd_ref) | copy-start | bytes 1572868
  3.9 2.4 %copy-start.1 = (f32[256,512]{1,0:T(8,128)}, f32[256,512]{1,0:T(8,128)S(1)}, u32[]{:S(2)}) copy-start(f32[256,512]{1,0:T(8,128)S(1)} %rev.6.bwd_ref) | copy-start | bytes 1572868
  6.3 3.4 %copy-start.2 = (f32[16,512]{1,0:T(8,128)S(1)}, f32[16,512]{1,0:T(8,128)}, u32[]{:S(2)}) copy-start(f32[16,512]{1,0:T(8,128)} %rates_ref.1) | copy-start | bytes 98308
  6.6 3.1 %collective-permute-start = (f32[2,16,512]{2,1,0:T(8,128)S(1)}, f32[2,16,512]{2,1,0:T(8,128)S(1)}, u32[]{:S(2)}, u32[]{:S(2)}) collective-permute-start(f32[2,16,512]{2,1,0:T(8,128)S(1)} %pad_maximum_fusion), channel_id=1, source_target_pairs={{0,16},{16,0},{32,48},{48,32},{64,80},{80,64},{96,112},{112,96},{1... | collective-permute-start | bytes 196616 | tf_op jit(solution)/shard_map/ppermute | solution.py:126
  9.7 22.0 %copy-start.10 = (f32[16,512]{1,0:T(8,128)S(1)}, f32[16,512]{1,0:T(8,128)}, u32[]{:S(2)}) copy-start(f32[16,512]{1,0:T(8,128)} %param.9) | copy-start | bytes 98308
  9.8 6.2 %collective-permute-start.1 = (f32[2,16,512]{2,1,0:T(8,128)S(1)}, f32[2,16,512]{2,1,0:T(8,128)S(1)}, u32[]{:S(2)}, u32[]{:S(2)}) collective-permute-start(f32[2,16,512]{2,1,0:T(8,128)S(1)} %pad_maximum_fusion.1), channel_id=1, source_target_pairs={{0,32},{16,48},{32,0},{48,16},{64,96},{80,112},{96,64},{112,80},{1... | collective-permute-start | bytes 196616 | tf_op jit(solution)/shard_map/ppermute | solution.py:126
  16.0 7.1 %collective-permute-start.2 = (f32[2,16,512]{2,1,0:T(8,128)S(1)}, f32[2,16,512]{2,1,0:T(8,128)S(1)}, u32[]{:S(2)}, u32[]{:S(2)}) collective-permute-start(f32[2,16,512]{2,1,0:T(8,128)S(1)} %pad_maximum_fusion.2), channel_id=1, source_target_pairs={{0,64},{16,80},{32,96},{48,112},{64,0},{80,16},{96,32},{112,48},{1... | collective-permute-start | bytes 196616 | tf_op jit(solution)/shard_map/ppermute | solution.py:126
  23.1 8.7 %collective-permute-start.3 = (f32[2,16,512]{2,1,0:T(8,128)S(1)}, f32[2,16,512]{2,1,0:T(8,128)S(1)}, u32[]{:S(2)}, u32[]{:S(2)}) collective-permute-start(f32[2,16,512]{2,1,0:T(8,128)S(1)} %pad_maximum_fusion.3), channel_id=1, source_target_pairs={{0,192},{16,208},{32,224},{48,240},{64,128},{80,144},{96,160},{112... | collective-permute-start | bytes 196616 | tf_op jit(solution)/shard_map/ppermute | solution.py:126
  31.8 17.4 %copy-start.9 = (f32[16,512]{1,0:T(8,128)}, f32[16,512]{1,0:T(8,128)S(1)}, u32[]{:S(2)}) copy-start(f32[16,512]{1,0:T(8,128)S(1)} %get-tuple-element.50.scaled_ref) | copy-start | bytes 98308
  31.8 17.4 %collective-permute-start.4 = (f32[2,16,512]{2,1,0:T(8,128)S(1)}, f32[2,16,512]{2,1,0:T(8,128)S(1)}, u32[]{:S(2)}, u32[]{:S(2)}) collective-permute-start(f32[2,16,512]{2,1,0:T(8,128)S(1)} %pad_maximum_fusion.4), channel_id=1, source_target_pairs={{0,256},{16,272},{32,288},{48,304},{64,320},{80,336},{96,352},{112... | collective-permute-start | bytes 196616 | tf_op jit(solution)/shard_map/ppermute | solution.py:126
  49.3 17.1 %collective-permute-start.5 = (f32[2,16,512]{2,1,0:T(8,128)S(1)}, f32[2,16,512]{2,1,0:T(8,128)S(1)}, u32[]{:S(2)}, u32[]{:S(2)}) collective-permute-start(f32[2,16,512]{2,1,0:T(8,128)S(1)} %pad_maximum_fusion.5), channel_id=1, source_target_pairs={{0,768},{16,784},{32,800},{48,816},{64,832},{80,848},{96,864},{112... | collective-permute-start | bytes 196616 | tf_op jit(solution)/shard_map/ppermute | solution.py:126
  60.5 10.9 %copy-start.8 = (f32[256,512]{1,0:T(8,128)S(1)}, f32[256,512]{1,0:T(8,128)}, u32[]{:S(2)}) copy-start(f32[256,512]{1,0:T(8,128)} %get-tuple-element.25) | copy-start | bytes 1572868
  66.4 5.0 %copy-start.7 = (f32[256,512]{1,0:T(8,128)S(1)}, f32[256,512]{1,0:T(8,128)}, u32[]{:S(2)}) copy-start(f32[256,512]{1,0:T(8,128)} %get-tuple-element.18) | copy-start | bytes 1572868
  74.1 0.9 %copy-start.5 = (bf16[256,512]{1,0:T(8,128)(2,1)S(1)}, bf16[256,512]{1,0:T(8,128)(2,1)}, u32[]{:S(2)}) copy-start(bf16[256,512]{1,0:T(8,128)(2,1)} %param.7) | copy-start | bytes 786436
  74.1 1.0 %copy-start.6 = (bf16[256,512]{1,0:T(8,128)(2,1)S(1)}, bf16[256,512]{1,0:T(8,128)(2,1)}, u32[]{:S(2)}) copy-start(bf16[256,512]{1,0:T(8,128)(2,1)} %param.6) | copy-start | bytes 786436

commit v12 on v11

--- a/solution.py
+++ b/solution.py
@@ -2,6 +2,7 @@
 import jax.numpy as jnp
 from jax import lax
 from jax.experimental import pallas as pl
+from jax.experimental.pallas import tpu as pltpu
 from jax.sharding import PartitionSpec as P
 
 BLOCK = 64
@@ -51,7 +52,10 @@
     return fwd_pieces, bwd_pieces
 
 
-def carried_kernel(fwd_ref, bwd_ref, scaled_ref, rates_ref, fwd_out, bwd_out):
+def carried_kernel(
+    fwd_ref, bwd_ref, scaled_ref, rates_ref, pieces_ref, value_ref, cot_ref,
+    out_ref, grad_ref, bwd_out, fwd_out,
+):
     length, width = fwd_out.shape
     order = rates_ref.shape[0]
     lags = lax.broadcasted_iota(jnp.int32, (BLOCK, width), 0).astype(jnp.float32) + 1.0
@@ -72,11 +76,20 @@
         return carry
 
     lax.fori_loop(0, order, mode, 0)
-
-
-def carried(fwd_in, bwd_in, scaled, rates, length):
-    shape = jax.ShapeDtypeStruct((length, fwd_in.shape[1]), jnp.float32)
-    return pl.pallas_call(carried_kernel, out_shape=(shape, shape))(fwd_in, bwd_in, scaled, rates)
+    mixed = pieces_ref[...] + fwd_out[...]
+    out_ref[...] = (value_ref[...].astype(jnp.float32) * mixed).astype(jnp.bfloat16)
+    grad_ref[...] = (cot_ref[...].astype(jnp.float32) * mixed).astype(jnp.bfloat16)
+
+
+def carried(fwd_in, bwd_in, scaled, rates, pieces, value, cot):
+    length, width = pieces.shape
+    half = jax.ShapeDtypeStruct((length, width), jnp.bfloat16)
+    full = jax.ShapeDtypeStruct((length, width), jnp.float32)
+    return pl.pallas_call(
+        carried_kernel,
+        out_shape=(half, half, full),
+        scratch_shapes=[pltpu.VMEM((length, width), jnp.float32)],
+    )(fwd_in, bwd_in, scaled, rates, pieces, value, cot)
 
 
 def end_state(signal, rates):
@@ -168,11 +181,10 @@
     )
     fwd_pieces = cover[0][0] + cover[1][0]
     bwd_pieces = cover[0][1] + cover[1][1]
-    fwd_extra, bwd_extra = carried(fwd_in, bwd_in, scaled, rates, length)
-    mixed = fwd_pieces + fwd_extra
+    output, grad_value, bwd_extra = carried(
+        fwd_in, bwd_in, scaled, rates, fwd_pieces, value, cotangent
+    )
     back = (bwd_pieces + bwd_extra)[::-1]
-    output = (value_f * mixed).astype(jnp.bfloat16)
-    grad_value = (cot_f * mixed).astype(jnp.bfloat16)
     grad_query = (back * key_f).astype(jnp.bfloat16)
     grad_key = (back * query_f).astype(jnp.bfloat16)
     return (output, grad_query, grad_key, grad_value)

time: 77 us -> 76.7 us (level)
    add x0 -> x2, other arithmetic: none -> 3.13 us  [the longest x1 1.94 us: per_device(): fwd_pieces = cover[0][0] + cover[1][0]]
    convert_element_type x1 -> x0, other arithmetic: 2.73 us -> none  [per_device(): grad_value = (cot_f * mixed).astype(jnp.bfloat16)]
    mul x1, other arithmetic: 0.07 us -> 1.1 us  [per_device(): weighted = cot_f * value_f]
    convert_element_type x1, other arithmetic: 1.09 us -> 0.07 us  [per_device(): (query_f * key_f).astype(jnp.bfloat16)]
    unnamed x22 -> x20, local copies, waits for them, and re-layouts: 2.03 us -> 1.49 us
where the time goes in v12:
time: 76.7 us; the launch traced here: 75.8 us
  starting transfers between devices  38.1 us (50%)
  Pallas kernels  16 us (21%)
  other arithmetic  9.07 us (12%)
  waiting for transfers between devices  8.25 us (11%)
  local copies, waits for them, and re-layouts  3.29 us (4%)
  between operations  1.08 us (1%)
    ppermute x6, starting transfers between devices, incoming_states(): lax.ppermute(jnp.stack([fwd_total, bwd_total]), 'ctx', [(i, partner(i, sp...  38.1 us
    pallas_call x2, Pallas kernels, local_pass(): pl.pallas_call(local_kernel, out_shape=(shape, shape))  11.7 us
    ppermute x6, waiting for transfers between devices, incoming_states(): lax.ppermute(jnp.stack([fwd_total, bwd_total]), 'ctx', [(i, partner(i, sp...  8.25 us
    pallas_call x1, Pallas kernels, carried(): pl.pallas_call(carried_kernel, out_shape=(half, half, full), scratch_shap...  4.27 us
    reduce_sum x2, other arithmetic, end_state(): return jnp.sum(outer * jnp.sum(inner[None] * rows, axis=1), axis=0)  2.14 us
    add x1, other arithmetic, per_device(): fwd_pieces = cover[0][0] + cover[1][0]  1.94 us
  transfers between devices with their start and end apart: 6, of which 4 were waited for; matrix products, arithmetic and copies ran while one was open for 2% of the time, Pallas kernels for 15%

profile of v12, /device:TPU:6, one launch (start us, length us, event | category | flops | bytes accessed | tf_op | source)
XLA Modules:
  0.0 75.8 jit_solution(15552452507312001531)
XLA Ops:
  0.7 1.1 %convert_multiply_fusion.3 = f32[256,512]{1,0:T(8,128)S(1)} fusion(bf16[256,512]{1,0:T(8,128)(2,1)} %value_ref.1, bf16[256,512]{1,0:T(8,128)(2,1)} %cot_ref.1), kind=kLoop, calls=%fused_computation.10 | loop fusion | flops 393216 | bytes 1048576 | tf_op jit(solution)/shard_map/mul | solution.py:168
  1.8 0.0 copy-start.3
  1.8 0.3 rev.6.bwd_ref
  2.1 0.6 copy-done.3
  2.7 0.1 copy-done.4
  2.8 0.1 fusion.1
  2.9 0.1 convert_element_type.59.fwd_ref
  2.9 0.7 copy-done.2
  3.7 0.1 multiply_exponential_fusion
  3.8 2.0 %multiply_reduce_fusion.1 = (f32[16,16,512]{2,1,0:T(8,128)S(1)}, f32[16,16,512]{2,1,0:T(8,128)S(1)}) fusion(f32[16,16,512]{2,1,0:T(8,128)S(1)} %bitcast.125, f32[16,16,512]{2,1,0:T(8,128)S(1)} %multiply_exponential_fusion, f32[16,16,512]{2,1,0:T(8,128)S(1)} %bitcast.124), kind=kLoop, calls=%fused_computation.1 | loop fusion | flops 8126464 | bytes 2621440 | tf_op jit(solution)/shard_map/reduce_sum | solution.py:102
  5.8 0.2 multiply_reduce_fusion.3
  6.0 1.9 %collective-permute-start = (f32[2,16,512]{2,1,0:T(8,128)S(1)}, f32[2,16,512]{2,1,0:T(8,128)S(1)}, u32[]{:S(2)}, u32[]{:S(2)}) collective-permute-start(f32[2,16,512]{2,1,0:T(8,128)S(1)} %pad_maximum_fusion), channel_id=1, source_target_pairs={{0,16},{16,0},{32,48},{48,32},{64,80},{80,64},{96,112},{112,96},{1... | collective-permute-start | bytes 196616 | tf_op jit(solution)/shard_map/ppermute | solution.py:139
  8.0 1.2 %collective-permute-done = f32[2,16,512]{2,1,0:T(8,128)S(1)} collective-permute-done((f32[2,16,512]{2,1,0:T(8,128)S(1)}, f32[2,16,512]{2,1,0:T(8,128)S(1)}, u32[]{:S(2)}, u32[]{:S(2)}) %collective-permute-start) | collective-permute-done | bytes 65568 | tf_op jit(solution)/shard_map/ppermute | solution.py:139
  9.3 3.5 %collective-permute-start.1 = (f32[2,16,512]{2,1,0:T(8,128)S(1)}, f32[2,16,512]{2,1,0:T(8,128)S(1)}, u32[]{:S(2)}, u32[]{:S(2)}) collective-permute-start(f32[2,16,512]{2,1,0:T(8,128)S(1)} %pad_maximum_fusion.1), channel_id=1, source_target_pairs={{0,32},{16,48},{32,0},{48,16},{64,96},{80,112},{96,64},{112,80},{1... | collective-permute-start | bytes 196616 | tf_op jit(solution)/shard_map/ppermute | solution.py:139
  12.8 2.6 %collective-permute-done.1 = f32[2,16,512]{2,1,0:T(8,128)S(1)} collective-permute-done((f32[2,16,512]{2,1,0:T(8,128)S(1)}, f32[2,16,512]{2,1,0:T(8,128)S(1)}, u32[]{:S(2)}, u32[]{:S(2)}) %collective-permute-start.1) | collective-permute-done | bytes 65568 | tf_op jit(solution)/shard_map/ppermute | solution.py:139
  15.5 4.5 %collective-permute-start.2 = (f32[2,16,512]{2,1,0:T(8,128)S(1)}, f32[2,16,512]{2,1,0:T(8,128)S(1)}, u32[]{:S(2)}, u32[]{:S(2)}) collective-permute-start(f32[2,16,512]{2,1,0:T(8,128)S(1)} %pad_maximum_fusion.2), channel_id=1, source_target_pairs={{0,64},{16,80},{32,96},{48,112},{64,0},{80,16},{96,32},{112,48},{1... | collective-permute-start | bytes 196616 | tf_op jit(solution)/shard_map/ppermute | solution.py:139
  20.0 2.5 %collective-permute-done.2 = f32[2,16,512]{2,1,0:T(8,128)S(1)} collective-permute-done((f32[2,16,512]{2,1,0:T(8,128)S(1)}, f32[2,16,512]{2,1,0:T(8,128)S(1)}, u32[]{:S(2)}, u32[]{:S(2)}) %collective-permute-start.2) | collective-permute-done | bytes 65568 | tf_op jit(solution)/shard_map/ppermute | solution.py:139
  22.6 6.2 %collective-permute-start.3 = (f32[2,16,512]{2,1,0:T(8,128)S(1)}, f32[2,16,512]{2,1,0:T(8,128)S(1)}, u32[]{:S(2)}, u32[]{:S(2)}) collective-permute-start(f32[2,16,512]{2,1,0:T(8,128)S(1)} %pad_maximum_fusion.3), channel_id=1, source_target_pairs={{0,192},{16,208},{32,224},{48,240},{64,128},{80,144},{96,160},{112... | collective-permute-start | bytes 196616 | tf_op jit(solution)/shard_map/ppermute | solution.py:139
  28.7 0.6 fusion.17
  29.4 1.9 %collective-permute-done.3 = f32[2,16,512]{2,1,0:T(8,128)S(1)} collective-permute-done((f32[2,16,512]{2,1,0:T(8,128)S(1)}, f32[2,16,512]{2,1,0:T(8,128)S(1)}, u32[]{:S(2)}, u32[]{:S(2)}) %collective-permute-start.3) | collective-permute-done | bytes 65568 | tf_op jit(solution)/shard_map/ppermute | solution.py:139
  31.3 10.9 %collective-permute-start.4 = (f32[2,16,512]{2,1,0:T(8,128)S(1)}, f32[2,16,512]{2,1,0:T(8,128)S(1)}, u32[]{:S(2)}, u32[]{:S(2)}) collective-permute-start(f32[2,16,512]{2,1,0:T(8,128)S(1)} %pad_maximum_fusion.4), channel_id=1, source_target_pairs={{0,256},{16,272},{32,288},{48,304},{64,320},{80,336},{96,352},{112... | collective-permute-start | bytes 196616 | tf_op jit(solution)/shard_map/ppermute | solution.py:139
  42.2 0.6 fusion.18
  42.8 5.8 %shard_map.93 = (f32[256,512]{1,0:T(8,128)}, f32[256,512]{1,0:T(8,128)}) custom-call(f32[256,512]{1,0:T(8,128)} %copy-done.1, f32[256,512]{1,0:T(8,128)} %copy-done, f32[8,512]{1,0:T(8,128)} %get-tuple-element.49.scaled_ref, f32[8,512]{1,0:T(8,128)} %get-tuple-element.47.rates_ref), custom_call_target="tpu_custom_call" | custom-call | tf_op jit(solution)/shard_map/pallas_call | solution.py:49
  48.7 11.1 %collective-permute-start.5 = (f32[2,16,512]{2,1,0:T(8,128)S(1)}, f32[2,16,512]{2,1,0:T(8,128)S(1)}, u32[]{:S(2)}, u32[]{:S(2)}) collective-permute-start(f32[2,16,512]{2,1,0:T(8,128)S(1)} %pad_maximum_fusion.5), channel_id=1, source_target_pairs={{0,768},{16,784},{32,800},{48,816},{64,832},{80,848},{96,864},{112... | collective-permute-start | bytes 196616 | tf_op jit(solution)/shard_map/ppermute | solution.py:139
  59.9 5.9 %shard_map.94 = (f32[256,512]{1,0:T(8,128)}, f32[256,512]{1,0:T(8,128)}) custom-call(f32[256,512]{1,0:T(8,128)} %copy-done.1, f32[256,512]{1,0:T(8,128)} %copy-done, f32[8,512]{1,0:T(8,128)} %get-tuple-element.48.scaled_ref, f32[8,512]{1,0:T(8,128)} %get-tuple-element.46.rates_ref), custom_call_target="tpu_custom_call" | custom-call | tf_op jit(solution)/shard_map/pallas_call | solution.py:49
  65.9 1.9 %add.178.pieces_ref = f32[256,512]{1,0:T(8,128)} add(f32[256,512]{1,0:T(8,128)S(1)} %copy-done.5, f32[256,512]{1,0:T(8,128)} %get-tuple-element.24) | non-fusion elementwise | flops 131072 | bytes 1572864 | tf_op jit(solution)/shard_map/add | solution.py:182
  67.8 0.7 fusion.3.bwd_ref
  68.5 0.7 fusion.4.fwd_ref
  69.1 4.3 %shard_map.95 = (bf16[256,512]{1,0:T(8,128)(2,1)}, bf16[256,512]{1,0:T(8,128)(2,1)}, f32[256,512]{1,0:T(8,128)}) custom-call(f32[16,512]{1,0:T(8,128)} %fusion.4.fwd_ref, f32[16,512]{1,0:T(8,128)} %fusion.3.bwd_ref, f32[16,512]{1,0:T(8,128)} %copy-done.8, f32[16,512]{1,0:T(8,128)} %rates_ref.1, f32[256,512]{1,0:T(8,128)} %add.178.pieces_ref, ...), custom_call_target="tpu_custom_call" | custom-call | tf_op jit(solution)/shard_map/pallas_call | solution.py:88
  73.4 1.2 %add_add_fusion = f32[256,512]{1,0:T(8,128)S(1)} fusion(f32[256,512]{1,0:T(8,128)} %get-tuple-element.28, f32[256,512]{1,0:T(8,128)S(1)} %copy-done.6, f32[256,512]{1,0:T(8,128)S(1)} %copy-done.7), kind=kLoop, calls=%fused_computation.8 | loop fusion | flops 262144 | bytes 2097152 | tf_op jit(solution)/shard_map/add | solution.py:187
  74.6 0.3 rev.7
  74.9 0.9 %fusion = (bf16[256,512]{1,0:T(8,128)(2,1)}, bf16[256,512]{1,0:T(8,128)(2,1)}) fusion(f32[256,512]{1,0:T(8,128)S(1)} %rev.7, bf16[256,512]{1,0:T(8,128)(2,1)S(1)} %copy-done.4, bf16[256,512]{1,0:T(8,128)(2,1)S(1)} %copy-done.3), kind=kLoop, calls=%fused_computation.5 | loop fusion | flops 786432 | bytes 1572864 | tf_op jit(solution)/shard_map/convert_element_type | solution.py:189
  (32 shorter events, 0.3 us)
Async XLA Ops:
  1.8 1.0 %copy-start.3 = (bf16[256,512]{1,0:T(8,128)(2,1)S(1)}, bf16[256,512]{1,0:T(8,128)(2,1)}, u32[]{:S(2)}) copy-start(bf16[256,512]{1,0:T(8,128)(2,1)} %param.7) | copy-start | bytes 786436
  1.8 1.0 %copy-start.4 = (bf16[256,512]{1,0:T(8,128)(2,1)S(1)}, bf16[256,512]{1,0:T(8,128)(2,1)}, u32[]{:S(2)}) copy-start(bf16[256,512]{1,0:T(8,128)(2,1)} %param.6) | copy-start | bytes 786436
  2.8 1.0 %copy-start = (f32[256,512]{1,0:T(8,128)}, f32[256,512]{1,0:T(8,128)S(1)}, u32[]{:S(2)}) copy-start(f32[256,512]{1,0:T(8,128)S(1)} %rev.6.bwd_ref) | copy-start | bytes 1572868
  2.9 0.8 %copy-start.2 = (f32[16,512]{1,0:T(8,128)S(1)}, f32[16,512]{1,0:T(8,128)}, u32[]{:S(2)}) copy-start(f32[16,512]{1,0:T(8,128)} %rates_ref.1) | copy-start | bytes 98308
  3.7 2.1 %copy-start.1 = (f32[256,512]{1,0:T(8,128)}, f32[256,512]{1,0:T(8,128)S(1)}, u32[]{:S(2)}) copy-start(f32[256,512]{1,0:T(8,128)S(1)} %convert_element_type.59.fwd_ref) | copy-start | bytes 1572868
  5.8 3.4 %copy-start.9 = (f32[16,512]{1,0:T(8,128)S(1)}, f32[16,512]{1,0:T(8,128)}, u32[]{:S(2)}) copy-start(f32[16,512]{1,0:T(8,128)} %param.9) | copy-start | bytes 98308
  6.0 3.1 %collective-permute-start = (f32[2,16,512]{2,1,0:T(8,128)S(1)}, f32[2,16,512]{2,1,0:T(8,128)S(1)}, u32[]{:S(2)}, u32[]{:S(2)}) collective-permute-start(f32[2,16,512]{2,1,0:T(8,128)S(1)} %pad_maximum_fusion), channel_id=1, source_target_pairs={{0,16},{16,0},{32,48},{48,32},{64,80},{80,64},{96,112},{112,96},{1... | collective-permute-start | bytes 196616 | tf_op jit(solution)/shard_map/ppermute | solution.py:139
  9.2 33.0 %copy-start.8 = (f32[16,512]{1,0:T(8,128)}, f32[16,512]{1,0:T(8,128)S(1)}, u32[]{:S(2)}) copy-start(f32[16,512]{1,0:T(8,128)S(1)} %get-tuple-element.50.scaled_ref) | copy-start | bytes 98308
  9.3 6.2 %collective-permute-start.1 = (f32[2,16,512]{2,1,0:T(8,128)S(1)}, f32[2,16,512]{2,1,0:T(8,128)S(1)}, u32[]{:S(2)}, u32[]{:S(2)}) collective-permute-start(f32[2,16,512]{2,1,0:T(8,128)S(1)} %pad_maximum_fusion.1), channel_id=1, source_target_pairs={{0,32},{16,48},{32,0},{48,16},{64,96},{80,112},{96,64},{112,80},{1... | collective-permute-start | bytes 196616 | tf_op jit(solution)/shard_map/ppermute | solution.py:139
  15.5 7.1 %collective-permute-start.2 = (f32[2,16,512]{2,1,0:T(8,128)S(1)}, f32[2,16,512]{2,1,0:T(8,128)S(1)}, u32[]{:S(2)}, u32[]{:S(2)}) collective-permute-start(f32[2,16,512]{2,1,0:T(8,128)S(1)} %pad_maximum_fusion.2), channel_id=1, source_target_pairs={{0,64},{16,80},{32,96},{48,112},{64,0},{80,16},{96,32},{112,48},{1... | collective-permute-start | bytes 196616 | tf_op jit(solution)/shard_map/ppermute | solution.py:139
  22.6 8.7 %collective-permute-start.3 = (f32[2,16,512]{2,1,0:T(8,128)S(1)}, f32[2,16,512]{2,1,0:T(8,128)S(1)}, u32[]{:S(2)}, u32[]{:S(2)}) collective-permute-start(f32[2,16,512]{2,1,0:T(8,128)S(1)} %pad_maximum_fusion.3), channel_id=1, source_target_pairs={{0,192},{16,208},{32,224},{48,240},{64,128},{80,144},{96,160},{112... | collective-permute-start | bytes 196616 | tf_op jit(solution)/shard_map/ppermute | solution.py:139
  31.3 17.4 %collective-permute-start.4 = (f32[2,16,512]{2,1,0:T(8,128)S(1)}, f32[2,16,512]{2,1,0:T(8,128)S(1)}, u32[]{:S(2)}, u32[]{:S(2)}) collective-permute-start(f32[2,16,512]{2,1,0:T(8,128)S(1)} %pad_maximum_fusion.4), channel_id=1, source_target_pairs={{0,256},{16,272},{32,288},{48,304},{64,320},{80,336},{96,352},{112... | collective-permute-start | bytes 196616 | tf_op jit(solution)/shard_map/ppermute | solution.py:139
  48.7 17.1 %collective-permute-start.5 = (f32[2,16,512]{2,1,0:T(8,128)S(1)}, f32[2,16,512]{2,1,0:T(8,128)S(1)}, u32[]{:S(2)}, u32[]{:S(2)}) collective-permute-start(f32[2,16,512]{2,1,0:T(8,128)S(1)} %pad_maximum_fusion.5), channel_id=1, source_target_pairs={{0,768},{16,784},{32,800},{48,816},{64,832},{80,848},{96,864},{112... | collective-permute-start | bytes 196616 | tf_op jit(solution)/shard_map/ppermute | solution.py:139
  59.9 5.9 %copy-start.5 = (f32[256,512]{1,0:T(8,128)S(1)}, f32[256,512]{1,0:T(8,128)}, u32[]{:S(2)}) copy-start(f32[256,512]{1,0:T(8,128)} %get-tuple-element.23) | copy-start | bytes 1572868
  69.1 4.3 %copy-start.6 = (f32[256,512]{1,0:T(8,128)S(1)}, f32[256,512]{1,0:T(8,128)}, u32[]{:S(2)}) copy-start(f32[256,512]{1,0:T(8,128)} %get-tuple-element.26) | copy-start | bytes 1572868
  69.1 4.3 %copy-start.7 = (f32[256,512]{1,0:T(8,128)S(1)}, f32[256,512]{1,0:T(8,128)}, u32[]{:S(2)}) copy-start(f32[256,512]{1,0:T(8,128)} %get-tuple-element.27) | copy-start | bytes 1572868

commit v13 on v11

--- a/solution.py
+++ b/solution.py
@@ -117,7 +117,7 @@
     while span < count:
         rounds.append(span)
         span *= 2
-    slots = {span: k for k, span in enumerate(rounds[len(rounds) - len(cover) :])}
+    slots = {span: k for k, span in enumerate(rounds[len(rounds) - 2 * len(cover) + 1 :: 2])}
     cover = list(cover)
     fwd_total, bwd_total = fwd_state, bwd_state
     fwd_in = jnp.zeros_like(fwd_state)

time: 77 us -> 80.9 us (1.051)
  starting transfers between devices: 38.1 us -> 41.6 us
    ppermute x6, starting transfers between devices: 38.1 us -> 41.6 us  [incoming_states(): lax.ppermute(jnp.stack([fwd_total, bwd_total]), 'ctx', [(i, partner(i, sp...]
where the time goes in v13:
time: 80.9 us; the launch traced here: 80 us
  starting transfers between devices  41.6 us (51%)
  Pallas kernels  15.4 us (19%)
  other arithmetic  9.42 us (12%)
  waiting for transfers between devices  8.69 us (11%)
  local copies, waits for them, and re-layouts  3.81 us (5%)
  between operations  1.07 us (1%)
    ppermute x6, starting transfers between devices, incoming_states(): lax.ppermute(jnp.stack([fwd_total, bwd_total]), 'ctx', [(i, partner(i, sp...  41.6 us
    pallas_call x2, Pallas kernels, local_pass(): pl.pallas_call(local_kernel, out_shape=(shape, shape))  11.7 us
    ppermute x6, waiting for transfers between devices, incoming_states(): lax.ppermute(jnp.stack([fwd_total, bwd_total]), 'ctx', [(i, partner(i, sp...  8.69 us
    pallas_call x1, Pallas kernels, carried(): pl.pallas_call(carried_kernel, out_shape=(shape, shape))  3.68 us
    convert_element_type x1, other arithmetic, per_device(): grad_value = (cot_f * mixed).astype(jnp.bfloat16)  2.73 us
    reduce_sum x2, other arithmetic, end_state(): return jnp.sum(outer * jnp.sum(inner[None] * rows, axis=1), axis=0)  2.14 us
    unnamed x22, local copies, waits for them, and re-layouts  2.03 us
  transfers between devices with their start and end apart: 6, of which 4 were waited for; matrix products, arithmetic and copies ran while one was open for 2% of the time, Pallas kernels for 15%

profile of v13, /device:TPU:6, one launch (start us, length us, event | category | flops | bytes accessed | tf_op | source)
XLA Modules:
  0.0 80.0 jit_solution(1988475562816493204)
XLA Ops:
  0.7 0.8 neg.5
  1.4 1.1 %fusion.2 = bf16[256,512]{1,0:T(8,128)(2,1)S(1)} fusion(bf16[256,512]{1,0:T(8,128)(2,1)} %param.7, bf16[256,512]{1,0:T(8,128)(2,1)} %param.6), kind=kLoop, calls=%fused_computation.10 | loop fusion | flops 524288 | bytes 786432 | tf_op jit(solution)/shard_map/convert_element_type | solution.py:154
  2.6 0.9 %copy-done.3 = bf16[256,512]{1,0:T(8,128)(2,1)S(1)} copy-done((bf16[256,512]{1,0:T(8,128)(2,1)S(1)}, bf16[256,512]{1,0:T(8,128)(2,1)}, u32[]{:S(2)}) %copy-start.3) | copy-done | bytes 262168
  3.5 0.1 copy-done.4
  3.6 0.1 convert_multiply_fusion.1
  3.6 0.3 rev.6.bwd_ref
  3.9 0.1 multiply_exponential_fusion
  4.1 0.3 copy-done
  4.4 1.9 %multiply_reduce_fusion.1 = (f32[16,16,512]{2,1,0:T(8,128)S(1)}, f32[16,16,512]{2,1,0:T(8,128)S(1)}) fusion(f32[16,16,512]{2,1,0:T(8,128)S(1)} %bitcast.124, f32[16,16,512]{2,1,0:T(8,128)S(1)} %multiply_exponential_fusion, f32[16,16,512]{2,1,0:T(8,128)S(1)} %bitcast.125), kind=kLoop, calls=%fused_computation.1 | loop fusion | flops 8126464 | bytes 2621440 | tf_op jit(solution)/shard_map/reduce_sum | solution.py:89
  6.3 0.2 multiply_reduce_fusion.3
  6.6 1.9 %collective-permute-start = (f32[2,16,512]{2,1,0:T(8,128)S(1)}, f32[2,16,512]{2,1,0:T(8,128)S(1)}, u32[]{:S(2)}, u32[]{:S(2)}) collective-permute-start(f32[2,16,512]{2,1,0:T(8,128)S(1)} %pad_maximum_fusion), channel_id=1, source_target_pairs={{0,16},{16,0},{32,48},{48,32},{64,80},{80,64},{96,112},{112,96},{1... | collective-permute-start | bytes 196616 | tf_op jit(solution)/shard_map/ppermute | solution.py:126
  8.5 1.2 %collective-permute-done = f32[2,16,512]{2,1,0:T(8,128)S(1)} collective-permute-done((f32[2,16,512]{2,1,0:T(8,128)S(1)}, f32[2,16,512]{2,1,0:T(8,128)S(1)}, u32[]{:S(2)}, u32[]{:S(2)}) %collective-permute-start) | collective-permute-done | bytes 65568 | tf_op jit(solution)/shard_map/ppermute | solution.py:126
  9.8 3.5 %collective-permute-start.1 = (f32[2,16,512]{2,1,0:T(8,128)S(1)}, f32[2,16,512]{2,1,0:T(8,128)S(1)}, u32[]{:S(2)}, u32[]{:S(2)}) collective-permute-start(f32[2,16,512]{2,1,0:T(8,128)S(1)} %pad_maximum_fusion.1), channel_id=1, source_target_pairs={{0,32},{16,48},{32,0},{48,16},{64,96},{80,112},{96,64},{112,80},{1... | collective-permute-start | bytes 196616 | tf_op jit(solution)/shard_map/ppermute | solution.py:126
  13.3 2.6 %collective-permute-done.1 = f32[2,16,512]{2,1,0:T(8,128)S(1)} collective-permute-done((f32[2,16,512]{2,1,0:T(8,128)S(1)}, f32[2,16,512]{2,1,0:T(8,128)S(1)}, u32[]{:S(2)}, u32[]{:S(2)}) %collective-permute-start.1) | collective-permute-done | bytes 65568 | tf_op jit(solution)/shard_map/ppermute | solution.py:126
  16.0 4.5 %collective-permute-start.2 = (f32[2,16,512]{2,1,0:T(8,128)S(1)}, f32[2,16,512]{2,1,0:T(8,128)S(1)}, u32[]{:S(2)}, u32[]{:S(2)}) collective-permute-start(f32[2,16,512]{2,1,0:T(8,128)S(1)} %pad_maximum_fusion.2), channel_id=1, source_target_pairs={{0,64},{16,80},{32,96},{48,112},{64,0},{80,16},{96,32},{112,48},{1... | collective-permute-start | bytes 196616 | tf_op jit(solution)/shard_map/ppermute | solution.py:126
  20.5 0.6 fusion.19
  21.1 1.9 %collective-permute-done.2 = f32[2,16,512]{2,1,0:T(8,128)S(1)} collective-permute-done((f32[2,16,512]{2,1,0:T(8,128)S(1)}, f32[2,16,512]{2,1,0:T(8,128)S(1)}, u32[]{:S(2)}, u32[]{:S(2)}) %collective-permute-start.2) | collective-permute-done | bytes 65568 | tf_op jit(solution)/shard_map/ppermute | solution.py:126
  23.1 6.2 %collective-permute-start.3 = (f32[2,16,512]{2,1,0:T(8,128)S(1)}, f32[2,16,512]{2,1,0:T(8,128)S(1)}, u32[]{:S(2)}, u32[]{:S(2)}) collective-permute-start(f32[2,16,512]{2,1,0:T(8,128)S(1)} %pad_maximum_fusion.3), channel_id=1, source_target_pairs={{0,192},{16,208},{32,224},{48,240},{64,128},{80,144},{96,160},{112... | collective-permute-start | bytes 196616 | tf_op jit(solution)/shard_map/ppermute | solution.py:126
  29.3 0.6 fusion.20
  29.9 5.8 %shard_map.93 = (f32[256,512]{1,0:T(8,128)}, f32[256,512]{1,0:T(8,128)}) custom-call(f32[256,512]{1,0:T(8,128)} %copy-done, f32[256,512]{1,0:T(8,128)} %copy-done.1, f32[8,512]{1,0:T(8,128)} %get-tuple-element.49.scaled_ref, f32[8,512]{1,0:T(8,128)} %get-tuple-element.47.rates_ref), custom_call_target="tpu_custom_call" | custom-call | tf_op jit(solution)/shard_map/pallas_call | solution.py:48
  35.8 10.9 %collective-permute-start.4 = (f32[2,16,512]{2,1,0:T(8,128)S(1)}, f32[2,16,512]{2,1,0:T(8,128)S(1)}, u32[]{:S(2)}, u32[]{:S(2)}) collective-permute-start(f32[2,16,512]{2,1,0:T(8,128)S(1)} %pad_maximum_fusion.4), channel_id=1, source_target_pairs={{0,256},{16,272},{32,288},{48,304},{64,320},{80,336},{96,352},{112... | collective-permute-start | bytes 196616 | tf_op jit(solution)/shard_map/ppermute | solution.py:126
  46.8 2.9 %collective-permute-done.4 = f32[2,16,512]{2,1,0:T(8,128)S(1)} collective-permute-done((f32[2,16,512]{2,1,0:T(8,128)S(1)}, f32[2,16,512]{2,1,0:T(8,128)S(1)}, u32[]{:S(2)}, u32[]{:S(2)}) %collective-permute-start.4) | collective-permute-done | bytes 65568 | tf_op jit(solution)/shard_map/ppermute | solution.py:126
  49.7 14.6 %collective-permute-start.5 = (f32[2,16,512]{2,1,0:T(8,128)S(1)}, f32[2,16,512]{2,1,0:T(8,128)S(1)}, u32[]{:S(2)}, u32[]{:S(2)}) collective-permute-start(f32[2,16,512]{2,1,0:T(8,128)S(1)} %pad_maximum_fusion.5), channel_id=1, source_target_pairs={{0,768},{16,784},{32,800},{48,816},{64,832},{80,848},{96,864},{112... | collective-permute-start | bytes 196616 | tf_op jit(solution)/shard_map/ppermute | solution.py:126
  64.5 5.9 %shard_map.94 = (f32[256,512]{1,0:T(8,128)}, f32[256,512]{1,0:T(8,128)}) custom-call(f32[256,512]{1,0:T(8,128)} %copy-done, f32[256,512]{1,0:T(8,128)} %copy-done.1, f32[8,512]{1,0:T(8,128)} %get-tuple-element.48.scaled_ref, f32[8,512]{1,0:T(8,128)} %get-tuple-element.46.rates_ref), custom_call_target="tpu_custom_call" | custom-call | tf_op jit(solution)/shard_map/pallas_call | solution.py:48
  70.3 0.7 fusion.5.bwd_ref
  71.0 0.7 fusion.6.fwd_ref
  71.7 3.7 %shard_map.95 = (f32[256,512]{1,0:T(8,128)}, f32[256,512]{1,0:T(8,128)}) custom-call(f32[16,512]{1,0:T(8,128)} %fusion.6.fwd_ref, f32[16,512]{1,0:T(8,128)} %fusion.5.bwd_ref, f32[16,512]{1,0:T(8,128)} %copy-done.9, f32[16,512]{1,0:T(8,128)} %rates_ref.1), custom_call_target="tpu_custom_call" | custom-call | tf_op jit(solution)/shard_map/pallas_call | solution.py:79
  75.4 2.7 %fusion.4 = (bf16[256,512]{1,0:T(8,128)(2,1)}, bf16[256,512]{1,0:T(8,128)(2,1)}, f32[256,512]{1,0:T(8,128)S(1)}) fusion(bf16[256,512]{1,0:T(8,128)(2,1)S(1)} %copy-done.3, f32[256,512]{1,0:T(8,128)} %get-tuple-element.24, f32[256,512]{1,0:T(8,128)S(1)} %copy-done.7, f32[256,512]{1,0:T(8,128)} %get-tuple-element.22, bf16[256,512]{1,0:T(8,128)(2,1)S(1)} %copy-done.4, ...), kind=kLoop, calls=%fused_computation.12 | loop fusion | flops 1310720 | bytes 4718592 | tf_op jit(solution)/shard_map/convert_element_type | solution.py:175
  78.1 0.3 rev.7
  78.4 0.7 copy-done.5
  79.0 0.1 copy-done.6
  79.1 0.9 %fusion.1 = (bf16[256,512]{1,0:T(8,128)(2,1)}, bf16[256,512]{1,0:T(8,128)(2,1)}) fusion(f32[256,512]{1,0:T(8,128)S(1)} %rev.7, bf16[256,512]{1,0:T(8,128)(2,1)S(1)} %copy-done.6, bf16[256,512]{1,0:T(8,128)(2,1)S(1)} %copy-done.5), kind=kLoop, calls=%fused_computation.9 | loop fusion | flops 786432 | bytes 1572864 | tf_op jit(solution)/shard_map/convert_element_type | solution.py:177
  (33 shorter events, 0.3 us)
Async XLA Ops:
  2.5 1.0 %copy-start.3 = (bf16[256,512]{1,0:T(8,128)(2,1)S(1)}, bf16[256,512]{1,0:T(8,128)(2,1)}, u32[]{:S(2)}) copy-start(bf16[256,512]{1,0:T(8,128)(2,1)} %param.11) | copy-start | bytes 786436
  2.5 1.0 %copy-start.4 = (bf16[256,512]{1,0:T(8,128)(2,1)S(1)}, bf16[256,512]{1,0:T(8,128)(2,1)}, u32[]{:S(2)}) copy-start(bf16[256,512]{1,0:T(8,128)(2,1)} %param.8) | copy-start | bytes 786436
  3.5 0.8 %copy-start = (f32[256,512]{1,0:T(8,128)}, f32[256,512]{1,0:T(8,128)S(1)}, u32[]{:S(2)}) copy-start(f32[256,512]{1,0:T(8,128)S(1)} %convert_element_type.66.fwd_ref) | copy-start | bytes 1572868
  3.9 2.4 %copy-start.1 = (f32[256,512]{1,0:T(8,128)}, f32[256,512]{1,0:T(8,128)S(1)}, u32[]{:S(2)}) copy-start(f32[256,512]{1,0:T(8,128)S(1)} %rev.6.bwd_ref) | copy-start | bytes 1572868
  6.3 3.4 %copy-start.2 = (f32[16,512]{1,0:T(8,128)S(1)}, f32[16,512]{1,0:T(8,128)}, u32[]{:S(2)}) copy-start(f32[16,512]{1,0:T(8,128)} %rates_ref.1) | copy-start | bytes 98308
  6.6 16.5 %copy-start.10 = (f32[16,512]{1,0:T(8,128)S(1)}, f32[16,512]{1,0:T(8,128)}, u32[]{:S(2)}) copy-start(f32[16,512]{1,0:T(8,128)} %param.9) | copy-start | bytes 98308
  6.6 3.1 %collective-permute-start = (f32[2,16,512]{2,1,0:T(8,128)S(1)}, f32[2,16,512]{2,1,0:T(8,128)S(1)}, u32[]{:S(2)}, u32[]{:S(2)}) collective-permute-start(f32[2,16,512]{2,1,0:T(8,128)S(1)} %pad_maximum_fusion), channel_id=1, source_target_pairs={{0,16},{16,0},{32,48},{48,32},{64,80},{80,64},{96,112},{112,96},{1... | collective-permute-start | bytes 196616 | tf_op jit(solution)/shard_map/ppermute | solution.py:126
  9.8 6.2 %collective-permute-start.1 = (f32[2,16,512]{2,1,0:T(8,128)S(1)}, f32[2,16,512]{2,1,0:T(8,128)S(1)}, u32[]{:S(2)}, u32[]{:S(2)}) collective-permute-start(f32[2,16,512]{2,1,0:T(8,128)S(1)} %pad_maximum_fusion.1), channel_id=1, source_target_pairs={{0,32},{16,48},{32,0},{48,16},{64,96},{80,112},{96,64},{112,80},{1... | collective-permute-start | bytes 196616 | tf_op jit(solution)/shard_map/ppermute | solution.py:126
  16.0 7.1 %collective-permute-start.2 = (f32[2,16,512]{2,1,0:T(8,128)S(1)}, f32[2,16,512]{2,1,0:T(8,128)S(1)}, u32[]{:S(2)}, u32[]{:S(2)}) collective-permute-start(f32[2,16,512]{2,1,0:T(8,128)S(1)} %pad_maximum_fusion.2), channel_id=1, source_target_pairs={{0,64},{16,80},{32,96},{48,112},{64,0},{80,16},{96,32},{112,48},{1... | collective-permute-start | bytes 196616 | tf_op jit(solution)/shard_map/ppermute | solution.py:126
  23.1 12.7 %copy-start.9 = (f32[16,512]{1,0:T(8,128)}, f32[16,512]{1,0:T(8,128)S(1)}, u32[]{:S(2)}) copy-start(f32[16,512]{1,0:T(8,128)S(1)} %get-tuple-element.50.scaled_ref) | copy-start | bytes 98308
  23.1 12.6 %collective-permute-start.3 = (f32[2,16,512]{2,1,0:T(8,128)S(1)}, f32[2,16,512]{2,1,0:T(8,128)S(1)}, u32[]{:S(2)}, u32[]{:S(2)}) collective-permute-start(f32[2,16,512]{2,1,0:T(8,128)S(1)} %pad_maximum_fusion.3), channel_id=1, source_target_pairs={{0,192},{16,208},{32,224},{48,240},{64,128},{80,144},{96,160},{112... | collective-permute-start | bytes 196616 | tf_op jit(solution)/shard_map/ppermute | solution.py:126
  35.8 13.9 %collective-permute-start.4 = (f32[2,16,512]{2,1,0:T(8,128)S(1)}, f32[2,16,512]{2,1,0:T(8,128)S(1)}, u32[]{:S(2)}, u32[]{:S(2)}) collective-permute-start(f32[2,16,512]{2,1,0:T(8,128)S(1)} %pad_maximum_fusion.4), channel_id=1, source_target_pairs={{0,256},{16,272},{32,288},{48,304},{64,320},{80,336},{96,352},{112... | collective-permute-start | bytes 196616 | tf_op jit(solution)/shard_map/ppermute | solution.py:126
  49.7 20.6 %collective-permute-start.5 = (f32[2,16,512]{2,1,0:T(8,128)S(1)}, f32[2,16,512]{2,1,0:T(8,128)S(1)}, u32[]{:S(2)}, u32[]{:S(2)}) collective-permute-start(f32[2,16,512]{2,1,0:T(8,128)S(1)} %pad_maximum_fusion.5), channel_id=1, source_target_pairs={{0,768},{16,784},{32,800},{48,816},{64,832},{80,848},{96,864},{112... | collective-permute-start | bytes 196616 | tf_op jit(solution)/shard_map/ppermute | solution.py:126
  64.4 10.9 %copy-start.8 = (f32[256,512]{1,0:T(8,128)S(1)}, f32[256,512]{1,0:T(8,128)}, u32[]{:S(2)}) copy-start(f32[256,512]{1,0:T(8,128)} %get-tuple-element.25) | copy-start | bytes 1572868
  70.3 5.0 %copy-start.7 = (f32[256,512]{1,0:T(8,128)S(1)}, f32[256,512]{1,0:T(8,128)}, u32[]{:S(2)}) copy-start(f32[256,512]{1,0:T(8,128)} %get-tuple-element.18) | copy-start | bytes 1572868
  78.1 0.9 %copy-start.5 = (bf16[256,512]{1,0:T(8,128)(2,1)S(1)}, bf16[256,512]{1,0:T(8,128)(2,1)}, u32[]{:S(2)}) copy-start(bf16[256,512]{1,0:T(8,128)(2,1)} %param.7) | copy-start | bytes 786436
  78.1 1.0 %copy-start.6 = (bf16[256,512]{1,0:T(8,128)(2,1)S(1)}, bf16[256,512]{1,0:T(8,128)(2,1)}, u32[]{:S(2)}) copy-start(bf16[256,512]{1,0:T(8,128)(2,1)} %param.6) | copy-start | bytes 786436
